TPU v7x, 128 devices: a whole 4x4x4 slice. The times are simulated.
128 devices in a mesh: mode: 8 (over y, z_lo), depth: 16 (over x, z_hi, core).
Axes of the slice: x: 4, y: 4, z: 4 (z_hi: 2, z_lo: 2; z = z_hi * 2 + z_lo), core: 2. Of those that a mesh axis runs over, the one named last changes fastest.
Arguments:
- fields: float32 [40, 512, 16, 128], P('mode', 'depth'), may hold values from -6 to 6
- mean_field: float32 [512, 16, 128], P('depth'), may hold values from 0.5 to 2
- kl_modes: float32 [7, 512, 16, 128], P(None, 'depth'), may hold values from -3 to 3
- decay: float32 [512, 16, 128], P('depth'), may hold values from 0.4 to 1, as said below
- coupling: float32 [40, 40, 8], replicated, may hold values from -0.09375 to 0.09375
- pattern: int32 [40, 40, 8], replicated, may hold values 0 or 1
- mode_order: int32 [40], replicated, may hold values from 0 to 39, each once
Outputs:
- preconditioned: float32 [40, 512, 16, 128], P('mode', 'depth')
Inputs may be any that keep to these rules, and one draw needn't show every extreme that they name: decay lies strictly between 0 and 1 in every cell. mode_order names each of the 40 modes once.
All inputs are finite; a program needn't handle non-finite values.
Results may differ from a plain program's by a relative error of at most 0.0003.
Values sent between devices are 32-bit elements; how exact they have to be, the bound alone decides.
No kernel may reach another device: no remote copies, remote signals or barrier semaphores. Data moves between devices by JAX's collectives and lax.ppermute only.
A program may use at most 128 MiB of HBM per device.

v0:
```python
import jax
import jax.numpy as jnp
from jax import lax
from jax.sharding import PartitionSpec as P


def shifted(value, axis, steps):
    count = lax.axis_size(axis)
    first, last = (max(0, -steps), min(count, count - steps))
    return lax.ppermute(value, axis, [(source, source + steps) for source in range(first, last)])


def with_halo(cells, sides, width):
    for axis, dim in sides:
        count = lax.axis_size(axis)
        ends = count - 1
        head = lax.slice_in_dim(cells, 0, width, axis=dim)
        tail = lax.slice_in_dim(cells, cells.shape[dim] - width, cells.shape[dim], axis=dim)
        cells = jnp.concatenate(
            [
                lax.ppermute(tail, axis, [(i, (i + 1) % count) for i in range(ends)]),
                cells,
                lax.ppermute(head, axis, [((i + 1) % count, i) for i in range(ends)]),
            ],
            axis=dim,
        )
    return cells


def laplace(padded):
    lateral = jnp.pad(padded, ((0, 0), (0, 0), (1, 1), (1, 1)))
    centre = lateral[:, 1:-1, 1:-1, 1:-1]
    beside = lateral[:, 2:, 1:-1, 1:-1] + lateral[:, :-2, 1:-1, 1:-1]
    beside = beside + lateral[:, 1:-1, 2:, 1:-1] + lateral[:, 1:-1, :-2, 1:-1]
    beside = beside + lateral[:, 1:-1, 1:-1, 2:] + lateral[:, 1:-1, 1:-1, :-2]
    return 6.0 * centre - beside


def affine(earlier, later):
    return (later[0] * earlier[0], later[0] * earlier[1] + later[1])


def prefix_pair(ratio_field, source):
    return lax.associative_scan(affine, (ratio_field, source), axis=1)


def relay_down(ratio_last, source_last):
    chain_length = lax.axis_size("depth")

    def relay_turn(turn_index, carried):
        state_in = shifted(carried[1], "depth", 1)
        return (state_in, ratio_last * state_in + source_last)

    zeros_state = jnp.zeros_like(source_last)
    final_pair = lax.fori_loop(0, chain_length, relay_turn, (zeros_state, zeros_state))
    return final_pair[0]


def relay_up(ratio_last, source_last):
    chain_length = lax.axis_size("depth")

    def relay_turn(turn_index, carried):
        state_in = shifted(carried[1], "depth", -1)
        return (state_in, ratio_last * state_in + source_last)

    zeros_state = jnp.zeros_like(source_last)
    final_pair = lax.fori_loop(0, chain_length, relay_turn, (zeros_state, zeros_state))
    return final_pair[0]


def local(fields, mean_field, kl_modes, decay, coupling, pattern, mode_order):
    local_modes = fields.shape[0]
    cell_count = fields.shape[1] * fields.shape[2] * fields.shape[3]
    mode_total = mode_order.shape[0]
    my_first = lax.axis_index("mode") * local_modes
    order_onehot = (mode_order[:, None] == jnp.arange(mode_total, dtype=jnp.int32)[None, :]).astype(
        jnp.float32
    )
    masked = coupling * pattern.astype(jnp.float32)
    coupling_table = jnp.einsum(
        "ra,sb,abk->rsk", order_onehot, order_onehot, masked, precision=lax.Precision.HIGHEST
    )
    padded = with_halo(fields, (("depth", 1),), 1)
    flattened = laplace(padded).reshape(local_modes, cell_count)
    coefficients = jnp.concatenate([mean_field[None], kl_modes], axis=0).reshape(-1, cell_count)
    term_total = coefficients.shape[0]
    own_rows = jnp.transpose(
        lax.dynamic_slice_in_dim(coupling_table, my_first, local_modes, 0), (2, 0, 1)
    )
    field_piece = lax.all_gather(flattened, "mode", axis=0, tiled=True)
    accumulated = jnp.dot(
        own_rows.reshape(-1, field_piece.shape[0]),
        field_piece,
        precision=lax.Precision.HIGHEST,
        preferred_element_type=jnp.float32,
    )
    accumulated = accumulated.reshape(term_total, local_modes, cell_count)
    mixed_field = jnp.sum(coefficients[:, None, :] * accumulated, axis=0)
    mixed_field = mixed_field.reshape(fields.shape)
    gain_field = jnp.sqrt(1.0 - decay * decay)[None]
    ratio_field = decay[None]
    ratio_prefix, source_prefix = prefix_pair(ratio_field, gain_field * mixed_field)
    ratio_last = ratio_prefix[:, -1]
    source_last = source_prefix[:, -1]
    state_low = relay_down(ratio_last, source_last)
    smooth = source_prefix + ratio_prefix * state_low[:, None]
    back_ratio, back_source = prefix_pair(
        jnp.flip(ratio_field, axis=1), jnp.flip(gain_field * smooth, axis=1)
    )
    back_ratio_last = back_ratio[:, -1]
    back_source_last = back_source[:, -1]
    state_high = relay_up(back_ratio_last, back_source_last)
    return jnp.flip(back_source + back_ratio * state_high[:, None], axis=1)


def solution(mesh):
    in_specs = (
        P("mode", "depth", None, None),
        P("depth", None, None),
        P(None, "depth", None, None),
        P("depth", None, None),
        P(),
        P(),
        P(),
    )
    out_specs = P("mode", "depth", None, None)
    return jax.shard_map(local, mesh=mesh, in_specs=in_specs, out_specs=out_specs, check_vma=False)
```

profile of v0, /device:TPU:1, one launch (start us, length us, event | category | flops | bytes accessed | tf_op | source)
XLA Modules:
  0.0 690.0 jit_solution(12643377743317681385)
XLA Ops:
  42.4 310.6 %all-gather.3.cloned.1.call-done = f32[8,5,65536]{2,1,0:T(8,128)} async-done(((f32[1,5,65536]{2,1,0:T(8,128)}), f32[8,5,65536]{2,1,0:T(8,128)}) %all-gather.3.cloned.1.call-update) | async-done | bytes 10485776 | tf_op jit(solution)/shard_map/all_gather | solution.py:90
  353.0 11.7 %reshape.32 = f32[40,65536,1]{1,0,2:T(8,128)} reshape(f32[8,5,65536]{2,1,0:T(8,128)} %all-gather.3.cloned.1.call-done) | data formatting | bytes 20971520
  364.7 14.4 %fusion.3 = f32[5,65536]{1,0:T(8,128)S(1)} fusion(f32[40,65536,1]{1,0,2:T(8,128)} %reshape.32, f32[8,65536]{1,0:T(8,128)S(1)} %maximum_bitcast_fusion, f32[8,5,40]{2,1,0:T(8,128)S(1)} %constant_dynamic-slice_fusion), kind=kOutput, calls=%fused_computation.14 | convolution fusion | flops 1263206400 | bytes 13900032 | tf_op jit(solution)/shard_map/dot_general | solution.py:91
  387.2 135.9 %while.26 = (s32[]{:T(128)}, f32[5,16,128]{2,1,0:T(8,128)}, f32[5,16,128]{2,1,0:T(8,128)}, f32[1,16,128]{2,1,0:T(8,128)S(1)}, f32[5,16,128]{2,1,0:T(8,128)S(1)}, /*index=5*/s32[]{:T(128)}, s32[]{:T(128)}) while((s32[]{:T(128)}, f32[5,16,128]{2,1,0:T(8,128)}, f32[5,16,128]{2,1,0:T(8,128)}, f32[1,16,128]{2,1,0:T(8,128)S(1)}, ...), condition=%wide.region_2.3_spmd.clone, body=%wide.region_1.2_spmd.clone.sunk | while | flops 30723 | bytes 540827 | solution.py:55
  460.7 5.8 collective-permute-start
  469.1 6.6 collective-permute-start
  478.2 6.6 collective-permute-start
  487.3 6.6 collective-permute-start
  496.5 6.6 collective-permute-start
  505.6 6.6 collective-permute-start
  514.8 6.6 collective-permute-start
  532.4 146.3 %while.27 = (s32[]{:T(128)}, f32[5,16,128]{2,1,0:T(8,128)}, f32[5,16,128]{2,1,0:T(8,128)}, f32[1,16,128]{2,1,0:T(8,128)S(1)}, f32[5,16,128]{2,1,0:T(8,128)S(1)}, /*index=5*/s32[]{:T(128)}, s32[]{:T(128)}) while((s32[]{:T(128)}, f32[5,16,128]{2,1,0:T(8,128)}, f32[5,16,128]{2,1,0:T(8,128)}, f32[1,16,128]{2,1,0:T(8,128)S(1)}, ...), condition=%wide.region_4.5_spmd.clone, body=%wide.region_3.4_spmd.clone.sunk | while | flops 30723 | bytes 540827 | solution.py:67
  534.3 6.4 collective-permute-done.1
  553.0 6.4 collective-permute-done.1
  562.7 5.8 collective-permute-done.1
  571.8 5.8 collective-permute-done.1
  580.9 5.8 collective-permute-done.1
  590.1 5.8 collective-permute-done.1
  599.2 5.8 collective-permute-done.1
  608.3 5.8 collective-permute-done.1
  626.6 5.8 collective-permute-done.1
  635.7 5.8 collective-permute-done.1
  644.8 5.8 collective-permute-done.1
  672.2 5.8 collective-permute-done.1
  (380 shorter events, 222.2 us)
Async XLA Ops:
  6.5 346.5 %all-gather.3.cloned.1.call-start = ((), (), s32[]{:S(2)}) async-start(), calls=%async_computation | async-start | bytes 18874368 | tf_op jit(solution)/shard_map/all_gather | solution.py:90
  7.3 9.0 %collective-permute-start.2 = (f32[5,1,16,128]{3,2,1,0:T(8,128)S(1)}, f32[5,1,16,128]{3,2,1,0:T(8,128)S(1)}, u32[]{:S(2)}, u32[]{:S(2)}) collective-permute-start(f32[5,1,16,128]{3,2,1,0:T(8,128)S(1)} %get-tuple-element.116), channel_id=1, source_target_pairs={{1,0},{2,1},{3,2},{4,3},{5,4},{6,5},{7,6},{8,7},{9,8},{10,9},{11,1... | collective-permute-start | bytes 122888 | tf_op jit(solution)/shard_map/ppermute | solution.py:23
  469.1 7.7 %collective-permute-start = (f32[5,16,128]{2,1,0:T(8,128)S(1)}, f32[5,16,128]{2,1,0:T(8,128)S(1)}, u32[]{:S(2)}, u32[]{:S(2)}) collective-permute-start(f32[5,16,128]{2,1,0:T(8,128)S(1)} %broadcast_select_fusion.4), channel_id=1, source_target_pairs={{0,1},{1,2},{2,3},{3,4},{4,5},{5,6},{6,7},{7,8},{8,9},{9,10},{10,1... | collective-permute-start | bytes 122888 | tf_op jit(solution)/shard_map/while/body/eval_jaxpr/ppermute | solution.py:10
  478.2 7.7 %collective-permute-start = (f32[5,16,128]{2,1,0:T(8,128)S(1)}, f32[5,16,128]{2,1,0:T(8,128)S(1)}, u32[]{:S(2)}, u32[]{:S(2)}) collective-permute-start(f32[5,16,128]{2,1,0:T(8,128)S(1)} %broadcast_select_fusion.4), channel_id=1, source_target_pairs={{0,1},{1,2},{2,3},{3,4},{4,5},{5,6},{6,7},{7,8},{8,9},{9,10},{10,1... | collective-permute-start | bytes 122888 | tf_op jit(solution)/shard_map/while/body/eval_jaxpr/ppermute | solution.py:10
  487.3 7.7 %collective-permute-start = (f32[5,16,128]{2,1,0:T(8,128)S(1)}, f32[5,16,128]{2,1,0:T(8,128)S(1)}, u32[]{:S(2)}, u32[]{:S(2)}) collective-permute-start(f32[5,16,128]{2,1,0:T(8,128)S(1)} %broadcast_select_fusion.4), channel_id=1, source_target_pairs={{0,1},{1,2},{2,3},{3,4},{4,5},{5,6},{6,7},{7,8},{8,9},{9,10},{10,1... | collective-permute-start | bytes 122888 | tf_op jit(solution)/shard_map/while/body/eval_jaxpr/ppermute | solution.py:10
  496.5 7.7 %collective-permute-start = (f32[5,16,128]{2,1,0:T(8,128)S(1)}, f32[5,16,128]{2,1,0:T(8,128)S(1)}, u32[]{:S(2)}, u32[]{:S(2)}) collective-permute-start(f32[5,16,128]{2,1,0:T(8,128)S(1)} %broadcast_select_fusion.4), channel_id=1, source_target_pairs={{0,1},{1,2},{2,3},{3,4},{4,5},{5,6},{6,7},{7,8},{8,9},{9,10},{10,1... | collective-permute-start | bytes 122888 | tf_op jit(solution)/shard_map/while/body/eval_jaxpr/ppermute | solution.py:10
  505.6 7.7 %collective-permute-start = (f32[5,16,128]{2,1,0:T(8,128)S(1)}, f32[5,16,128]{2,1,0:T(8,128)S(1)}, u32[]{:S(2)}, u32[]{:S(2)}) collective-permute-start(f32[5,16,128]{2,1,0:T(8,128)S(1)} %broadcast_select_fusion.4), channel_id=1, source_target_pairs={{0,1},{1,2},{2,3},{3,4},{4,5},{5,6},{6,7},{7,8},{8,9},{9,10},{10,1... | collective-permute-start | bytes 122888 | tf_op jit(solution)/shard_map/while/body/eval_jaxpr/ppermute | solution.py:10
  514.8 7.7 %collective-permute-start = (f32[5,16,128]{2,1,0:T(8,128)S(1)}, f32[5,16,128]{2,1,0:T(8,128)S(1)}, u32[]{:S(2)}, u32[]{:S(2)}) collective-permute-start(f32[5,16,128]{2,1,0:T(8,128)S(1)} %broadcast_select_fusion.4), channel_id=1, source_target_pairs={{0,1},{1,2},{2,3},{3,4},{4,5},{5,6},{6,7},{7,8},{8,9},{9,10},{10,1... | collective-permute-start | bytes 122888 | tf_op jit(solution)/shard_map/while/body/eval_jaxpr/ppermute | solution.py:10
  532.4 8.3 %collective-permute-start.1 = (f32[5,16,128]{2,1,0:T(8,128)S(1)}, f32[5,16,128]{2,1,0:T(8,128)S(1)}, u32[]{:S(2)}, u32[]{:S(2)}) collective-permute-start(f32[5,16,128]{2,1,0:T(8,128)S(1)} %broadcast_select_fusion.5), channel_id=1, source_target_pairs={{1,0},{2,1},{3,2},{4,3},{5,4},{6,5},{7,6},{8,7},{9,8},{10,9},{11,1... | collective-permute-start | bytes 122888 | tf_op jit(solution)/shard_map/while/body/eval_jaxpr/ppermute | solution.py:10
  542.1 7.6 %collective-permute-start.1 = (f32[5,16,128]{2,1,0:T(8,128)S(1)}, f32[5,16,128]{2,1,0:T(8,128)S(1)}, u32[]{:S(2)}, u32[]{:S(2)}) collective-permute-start(f32[5,16,128]{2,1,0:T(8,128)S(1)} %broadcast_select_fusion.5), channel_id=1, source_target_pairs={{1,0},{2,1},{3,2},{4,3},{5,4},{6,5},{7,6},{8,7},{9,8},{10,9},{11,1... | collective-permute-start | bytes 122888 | tf_op jit(solution)/shard_map/while/body/eval_jaxpr/ppermute | solution.py:10
  551.1 8.3 %collective-permute-start.1 = (f32[5,16,128]{2,1,0:T(8,128)S(1)}, f32[5,16,128]{2,1,0:T(8,128)S(1)}, u32[]{:S(2)}, u32[]{:S(2)}) collective-permute-start(f32[5,16,128]{2,1,0:T(8,128)S(1)} %broadcast_select_fusion.5), channel_id=1, source_target_pairs={{1,0},{2,1},{3,2},{4,3},{5,4},{6,5},{7,6},{8,7},{9,8},{10,9},{11,1... | collective-permute-start | bytes 122888 | tf_op jit(solution)/shard_map/while/body/eval_jaxpr/ppermute | solution.py:10
  560.8 7.7 %collective-permute-start.1 = (f32[5,16,128]{2,1,0:T(8,128)S(1)}, f32[5,16,128]{2,1,0:T(8,128)S(1)}, u32[]{:S(2)}, u32[]{:S(2)}) collective-permute-start(f32[5,16,128]{2,1,0:T(8,128)S(1)} %broadcast_select_fusion.5), channel_id=1, source_target_pairs={{1,0},{2,1},{3,2},{4,3},{5,4},{6,5},{7,6},{8,7},{9,8},{10,9},{11,1... | collective-permute-start | bytes 122888 | tf_op jit(solution)/shard_map/while/body/eval_jaxpr/ppermute | solution.py:10
  569.9 7.7 %collective-permute-start.1 = (f32[5,16,128]{2,1,0:T(8,128)S(1)}, f32[5,16,128]{2,1,0:T(8,128)S(1)}, u32[]{:S(2)}, u32[]{:S(2)}) collective-permute-start(f32[5,16,128]{2,1,0:T(8,128)S(1)} %broadcast_select_fusion.5), channel_id=1, source_target_pairs={{1,0},{2,1},{3,2},{4,3},{5,4},{6,5},{7,6},{8,7},{9,8},{10,9},{11,1... | collective-permute-start | bytes 122888 | tf_op jit(solution)/shard_map/while/body/eval_jaxpr/ppermute | solution.py:10
  579.0 7.7 %collective-permute-start.1 = (f32[5,16,128]{2,1,0:T(8,128)S(1)}, f32[5,16,128]{2,1,0:T(8,128)S(1)}, u32[]{:S(2)}, u32[]{:S(2)}) collective-permute-start(f32[5,16,128]{2,1,0:T(8,128)S(1)} %broadcast_select_fusion.5), channel_id=1, source_target_pairs={{1,0},{2,1},{3,2},{4,3},{5,4},{6,5},{7,6},{8,7},{9,8},{10,9},{11,1... | collective-permute-start | bytes 122888 | tf_op jit(solution)/shard_map/while/body/eval_jaxpr/ppermute | solution.py:10
  588.2 7.7 %collective-permute-start.1 = (f32[5,16,128]{2,1,0:T(8,128)S(1)}, f32[5,16,128]{2,1,0:T(8,128)S(1)}, u32[]{:S(2)}, u32[]{:S(2)}) collective-permute-start(f32[5,16,128]{2,1,0:T(8,128)S(1)} %broadcast_select_fusion.5), channel_id=1, source_target_pairs={{1,0},{2,1},{3,2},{4,3},{5,4},{6,5},{7,6},{8,7},{9,8},{10,9},{11,1... | collective-permute-start | bytes 122888 | tf_op jit(solution)/shard_map/while/body/eval_jaxpr/ppermute | solution.py:10
  597.3 7.7 %collective-permute-start.1 = (f32[5,16,128]{2,1,0:T(8,128)S(1)}, f32[5,16,128]{2,1,0:T(8,128)S(1)}, u32[]{:S(2)}, u32[]{:S(2)}) collective-permute-start(f32[5,16,128]{2,1,0:T(8,128)S(1)} %broadcast_select_fusion.5), channel_id=1, source_target_pairs={{1,0},{2,1},{3,2},{4,3},{5,4},{6,5},{7,6},{8,7},{9,8},{10,9},{11,1... | collective-permute-start | bytes 122888 | tf_op jit(solution)/shard_map/while/body/eval_jaxpr/ppermute | solution.py:10
  606.4 7.7 %collective-permute-start.1 = (f32[5,16,128]{2,1,0:T(8,128)S(1)}, f32[5,16,128]{2,1,0:T(8,128)S(1)}, u32[]{:S(2)}, u32[]{:S(2)}) collective-permute-start(f32[5,16,128]{2,1,0:T(8,128)S(1)} %broadcast_select_fusion.5), channel_id=1, source_target_pairs={{1,0},{2,1},{3,2},{4,3},{5,4},{6,5},{7,6},{8,7},{9,8},{10,9},{11,1... | collective-permute-start | bytes 122888 | tf_op jit(solution)/shard_map/while/body/eval_jaxpr/ppermute | solution.py:10
  615.5 7.7 %collective-permute-start.1 = (f32[5,16,128]{2,1,0:T(8,128)S(1)}, f32[5,16,128]{2,1,0:T(8,128)S(1)}, u32[]{:S(2)}, u32[]{:S(2)}) collective-permute-start(f32[5,16,128]{2,1,0:T(8,128)S(1)} %broadcast_select_fusion.5), channel_id=1, source_target_pairs={{1,0},{2,1},{3,2},{4,3},{5,4},{6,5},{7,6},{8,7},{9,8},{10,9},{11,1... | collective-permute-start | bytes 122888 | tf_op jit(solution)/shard_map/while/body/eval_jaxpr/ppermute | solution.py:10
  624.6 7.7 %collective-permute-start.1 = (f32[5,16,128]{2,1,0:T(8,128)S(1)}, f32[5,16,128]{2,1,0:T(8,128)S(1)}, u32[]{:S(2)}, u32[]{:S(2)}) collective-permute-start(f32[5,16,128]{2,1,0:T(8,128)S(1)} %broadcast_select_fusion.5), channel_id=1, source_target_pairs={{1,0},{2,1},{3,2},{4,3},{5,4},{6,5},{7,6},{8,7},{9,8},{10,9},{11,1... | collective-permute-start | bytes 122888 | tf_op jit(solution)/shard_map/while/body/eval_jaxpr/ppermute | solution.py:10
  633.8 7.7 %collective-permute-start.1 = (f32[5,16,128]{2,1,0:T(8,128)S(1)}, f32[5,16,128]{2,1,0:T(8,128)S(1)}, u32[]{:S(2)}, u32[]{:S(2)}) collective-permute-start(f32[5,16,128]{2,1,0:T(8,128)S(1)} %broadcast_select_fusion.5), channel_id=1, source_target_pairs={{1,0},{2,1},{3,2},{4,3},{5,4},{6,5},{7,6},{8,7},{9,8},{10,9},{11,1... | collective-permute-start | bytes 122888 | tf_op jit(solution)/shard_map/while/body/eval_jaxpr/ppermute | solution.py:10
  642.9 7.7 %collective-permute-start.1 = (f32[5,16,128]{2,1,0:T(8,128)S(1)}, f32[5,16,128]{2,1,0:T(8,128)S(1)}, u32[]{:S(2)}, u32[]{:S(2)}) collective-permute-start(f32[5,16,128]{2,1,0:T(8,128)S(1)} %broadcast_select_fusion.5), channel_id=1, source_target_pairs={{1,0},{2,1},{3,2},{4,3},{5,4},{6,5},{7,6},{8,7},{9,8},{10,9},{11,1... | collective-permute-start | bytes 122888 | tf_op jit(solution)/shard_map/while/body/eval_jaxpr/ppermute | solution.py:10
  652.0 7.7 %collective-permute-start.1 = (f32[5,16,128]{2,1,0:T(8,128)S(1)}, f32[5,16,128]{2,1,0:T(8,128)S(1)}, u32[]{:S(2)}, u32[]{:S(2)}) collective-permute-start(f32[5,16,128]{2,1,0:T(8,128)S(1)} %broadcast_select_fusion.5), channel_id=1, source_target_pairs={{1,0},{2,1},{3,2},{4,3},{5,4},{6,5},{7,6},{8,7},{9,8},{10,9},{11,1... | collective-permute-start | bytes 122888 | tf_op jit(solution)/shard_map/while/body/eval_jaxpr/ppermute | solution.py:10
  661.1 7.7 %collective-permute-start.1 = (f32[5,16,128]{2,1,0:T(8,128)S(1)}, f32[5,16,128]{2,1,0:T(8,128)S(1)}, u32[]{:S(2)}, u32[]{:S(2)}) collective-permute-start(f32[5,16,128]{2,1,0:T(8,128)S(1)} %broadcast_select_fusion.5), channel_id=1, source_target_pairs={{1,0},{2,1},{3,2},{4,3},{5,4},{6,5},{7,6},{8,7},{9,8},{10,9},{11,1... | collective-permute-start | bytes 122888 | tf_op jit(solution)/shard_map/while/body/eval_jaxpr/ppermute | solution.py:10
  670.3 7.7 %collective-permute-start.1 = (f32[5,16,128]{2,1,0:T(8,128)S(1)}, f32[5,16,128]{2,1,0:T(8,128)S(1)}, u32[]{:S(2)}, u32[]{:S(2)}) collective-permute-start(f32[5,16,128]{2,1,0:T(8,128)S(1)} %broadcast_select_fusion.5), channel_id=1, source_target_pairs={{1,0},{2,1},{3,2},{4,3},{5,4},{6,5},{7,6},{8,7},{9,8},{10,9},{11,1... | collective-permute-start | bytes 122888 | tf_op jit(solution)/shard_map/while/body/eval_jaxpr/ppermute | solution.py:10
  (74 other events, 554.9 us)
Sparse Core Ops, SparseCore 0:
  24.0 328.9 all-gather.2
where the time goes:
time: 698 us; the launch traced here: 690 us
  waiting for transfers between devices  423 us (61%)
  starting transfers between devices  136 us (19%)
  other arithmetic  67.8 us (10%)
  local copies, waits for them, and re-layouts  33.9 us (5%)
  matrix products  15 us (2%)
  between operations  14.4 us (2%)
    all_gather x1, waiting for transfers between devices, local(): field_piece = lax.all_gather(flattened, 'mode', axis=0, tiled=True)  311 us
    ppermute x32, starting transfers between devices, shifted(): lax.ppermute(value, axis, [(source, source + steps) for source in range(f...  127 us
    ppermute x32, waiting for transfers between devices, shifted(): lax.ppermute(value, axis, [(source, source + steps) for source in range(f...  111 us
    while x32, other arithmetic  23.5 us
    add x32, other arithmetic, relay_turn(): return (state_in, ratio_last * state_in + source_last)  20.2 us
    unnamed x63, local copies, waits for them, and re-layouts  19.2 us
    dot_general x1, matrix products, local(): jnp.dot(own_rows.reshape(-1, field_piece.shape[0]), field_piece, precisio...  14.4 us
  transfers between devices with their start and end apart: 35, of which 34 were waited for; matrix products, arithmetic and copies ran while one was open for 2% of the time, Pallas kernels for 0%

commit v1 on v0

v1 whole, which is shorter than its diff:
```python
import jax
import jax.numpy as jnp
from jax import lax
from jax.experimental import pallas as pl
from jax.experimental.pallas import tpu as pltpu
from jax.sharding import PartitionSpec as P


def with_halo(cells, sides, width):
    for axis, dim in sides:
        count = lax.axis_size(axis)
        ends = count - 1
        head = lax.slice_in_dim(cells, 0, width, axis=dim)
        tail = lax.slice_in_dim(cells, cells.shape[dim] - width, cells.shape[dim], axis=dim)
        cells = jnp.concatenate(
            [
                lax.ppermute(tail, axis, [(i, (i + 1) % count) for i in range(ends)]),
                cells,
                lax.ppermute(head, axis, [((i + 1) % count, i) for i in range(ends)]),
            ],
            axis=dim,
        )
    return cells


def laplace(padded):
    lateral = jnp.pad(padded, ((0, 0), (0, 0), (1, 1), (1, 1)))
    centre = lateral[:, 1:-1, 1:-1, 1:-1]
    beside = lateral[:, 2:, 1:-1, 1:-1] + lateral[:, :-2, 1:-1, 1:-1]
    beside = beside + lateral[:, 1:-1, 2:, 1:-1] + lateral[:, 1:-1, :-2, 1:-1]
    beside = beside + lateral[:, 1:-1, 1:-1, 2:] + lateral[:, 1:-1, 1:-1, :-2]
    return 6.0 * centre - beside


def sweep_kernel(mixed_ref, decay_ref, back_ref, coupled_ref, tail_ref, forward_ref):
    rows = decay_ref.shape[0]

    def forward_row(z, carried):
        state, ratio = carried
        d = decay_ref[z]
        g = jnp.sqrt(1.0 - d * d)
        state = d[None] * state + g[None] * mixed_ref[:, z]
        ratio = d * ratio
        back_ref[:, z] = g[None] * state
        coupled_ref[z] = g * ratio
        return state, ratio

    lateral = decay_ref.shape[1:]
    modes = mixed_ref.shape[0]
    state, _ = lax.fori_loop(
        0,
        rows,
        forward_row,
        (jnp.zeros((modes,) + lateral, jnp.float32), jnp.ones(lateral, jnp.float32)),
    )
    forward_ref[...] = state

    def backward_row(i, carried):
        z = rows - 1 - i
        back, coupled, tail = carried
        d = decay_ref[z]
        back = d[None] * back + back_ref[:, z]
        coupled = d * coupled + coupled_ref[z]
        tail = d * tail
        back_ref[:, z] = back
        coupled_ref[z] = coupled
        tail_ref[z] = tail
        return back, coupled, tail

    lax.fori_loop(
        0,
        rows,
        backward_row,
        (
            jnp.zeros((modes,) + lateral, jnp.float32),
            jnp.zeros(lateral, jnp.float32),
            jnp.ones(lateral, jnp.float32),
        ),
    )


def local_sweeps(mixed, decay):
    modes, rows = mixed.shape[0], mixed.shape[1]
    lateral = mixed.shape[2:]
    return pl.pallas_call(
        sweep_kernel,
        out_shape=(
            jax.ShapeDtypeStruct(mixed.shape, jnp.float32),
            jax.ShapeDtypeStruct(decay.shape, jnp.float32),
            jax.ShapeDtypeStruct(decay.shape, jnp.float32),
            jax.ShapeDtypeStruct((modes,) + lateral, jnp.float32),
        ),
    )(mixed, decay)


def local(fields, mean_field, kl_modes, decay, coupling, pattern, mode_order):
    local_modes = fields.shape[0]
    rows = fields.shape[1]
    lateral = fields.shape[2:]
    mode_total = mode_order.shape[0]
    groups = lax.axis_size("mode")
    chunk = rows // groups
    masked = coupling * pattern.astype(jnp.float32)
    coupling_table = jnp.take(jnp.take(masked, mode_order, axis=0), mode_order, axis=1)
    term_total = coupling_table.shape[2]

    padded = with_halo(fields, (("depth", 1),), 1)
    stencil = laplace(padded)
    stencil_rows = lax.all_to_all(stencil, "mode", 1, 0, tiled=True)
    cell_count = chunk * lateral[0] * lateral[1]
    stencil_rows = stencil_rows.reshape(mode_total, cell_count)

    coefficients = jnp.concatenate([mean_field[None], kl_modes], axis=0)
    my_chunk = lax.axis_index("mode") * chunk
    coefficients = lax.dynamic_slice_in_dim(coefficients, my_chunk, chunk, axis=1)
    coefficients = coefficients.reshape(term_total, 1, cell_count)

    table_rows = jnp.transpose(coupling_table, (2, 0, 1)).reshape(term_total * mode_total, mode_total)
    accumulated = jnp.dot(
        table_rows,
        stencil_rows,
        precision=lax.Precision.HIGHEST,
        preferred_element_type=jnp.float32,
    ).reshape(term_total, mode_total, cell_count)
    mixed_rows = jnp.sum(coefficients * accumulated, axis=0)
    mixed_rows = mixed_rows.reshape((mode_total, chunk) + lateral)
    mixed_field = lax.all_to_all(mixed_rows, "mode", 0, 1, tiled=True)

    back, coupled, tail, forward_end = local_sweeps(mixed_field, decay)
    summary = jnp.concatenate(
        [tail[:1], coupled[:1], forward_end, back[:, 0]], axis=0
    )
    summaries = lax.all_gather(summary, "depth", axis=0, tiled=False)
    slabs = summaries.shape[0]
    ratio_all = summaries[:, 0]
    coupled_all = summaries[:, 1]
    forward_all = summaries[:, 2 : 2 + local_modes]
    back_all = summaries[:, 2 + local_modes :]

    state_low = [jnp.zeros_like(forward_all[0])]
    for slab in range(slabs - 1):
        state_low.append(ratio_all[slab][None] * state_low[-1] + forward_all[slab])
    state_high = [jnp.zeros_like(forward_all[0])]
    for slab in range(slabs - 1, 0, -1):
        state_high.append(
            back_all[slab]
            + coupled_all[slab][None] * state_low[slab]
            + ratio_all[slab][None] * state_high[-1]
        )
    state_high = state_high[::-1]
    me = lax.axis_index("depth")
    low = lax.dynamic_index_in_dim(jnp.stack(state_low), me, 0, keepdims=False)
    high = lax.dynamic_index_in_dim(jnp.stack(state_high), me, 0, keepdims=False)
    return back + coupled[None] * low[:, None] + tail[None] * high[:, None]


def solution(mesh):
    in_specs = (
        P("mode", "depth", None, None),
        P("depth", None, None),
        P(None, "depth", None, None),
        P("depth", None, None),
        P(),
        P(),
        P(),
    )
    out_specs = P("mode", "depth", None, None)
    return jax.shard_map(local, mesh=mesh, in_specs=in_specs, out_specs=out_specs, check_vma=False)
```

time: 698 us -> 157 us (0.22)
  waiting for transfers between devices: 423 us -> 66.8 us
  starting transfers between devices: 136 us -> 13.6 us
  other arithmetic: 67.8 us -> 18.5 us
  local copies, waits for them, and re-layouts: 33.9 us -> 9.78 us
  blocking collectives: 0 us -> 20.9 us
    all_gather x1, waiting for transfers between devices: 311 us -> 51.2 us  [local(): summaries = lax.all_gather(summary, 'depth', axis=0, tiled=False)]
    ppermute x32 -> x0, starting transfers between devices: 127 us -> none  [shifted(): lax.ppermute(value, axis, [(source, source + steps) for source in range(f...]
    ppermute x32 -> x0, waiting for transfers between devices: 111 us -> none  [shifted(): lax.ppermute(value, axis, [(source, source + steps) for source in range(f...]
    while x32 -> x0, other arithmetic: 23.5 us -> none
    add x65 -> x1, other arithmetic: 24.3 us -> 1.24 us  [local(): return back + coupled[None] * low[:, None] + tail[None] * high[:, None]]
    all_to_all x0 -> x1, blocking collectives: none -> 20.9 us  [local(): mixed_field = lax.all_to_all(mixed_rows, 'mode', 0, 1, tiled=True)]
    all_to_all x0 -> x1, waiting for transfers between devices: none -> 15.6 us  [local(): stencil_rows = lax.all_to_all(stencil, 'mode', 1, 0, tiled=True)]
    unnamed x63 -> x37, local copies, waits for them, and re-layouts: 19.2 us -> 3.91 us
  transfers between devices with their start and end apart: 35 -> 4, of which waited for: 34 -> 2; matrix products, arithmetic and copies ran while one was open for 2% -> 3% of each run, Pallas kernels for 0% -> 0%
where the time goes in v1:
time: 157 us; the launch traced here: 156 us
  waiting for transfers between devices  66.8 us (43%)
  blocking collectives  20.9 us (13%)
  other arithmetic  18.5 us (12%)
  between operations  13.8 us (9%)
  starting transfers between devices  13.6 us (9%)
  local copies, waits for them, and re-layouts  9.78 us (6%)
  matrix products  8.97 us (6%)
  Pallas kernels  3.4 us (2%)
    all_gather x1, waiting for transfers between devices, local(): summaries = lax.all_gather(summary, 'depth', axis=0, tiled=False)  51.2 us
    all_to_all x1, blocking collectives, local(): mixed_field = lax.all_to_all(mixed_rows, 'mode', 0, 1, tiled=True)  20.9 us
    all_to_all x1, waiting for transfers between devices, local(): stencil_rows = lax.all_to_all(stencil, 'mode', 1, 0, tiled=True)  15.6 us
    unnamed x15, other arithmetic  9.68 us
    dot_general x1, matrix products, local(): jnp.dot(table_rows, stencil_rows, precision=lax.Precision.HIGHEST, prefer...  8.97 us
    ppermute x1, starting transfers between devices, with_halo(): lax.ppermute(tail, axis, [(i, (i + 1) % count) for i in range(ends)])  5.49 us
    all_to_all x1, starting transfers between devices, local(): stencil_rows = lax.all_to_all(stencil, 'mode', 1, 0, tiled=True)  4.78 us
    unnamed x37, local copies, waits for them, and re-layouts  3.91 us
  transfers between devices with their start and end apart: 4, of which 2 were waited for; matrix products, arithmetic and copies ran while one was open for 3% of the time, Pallas kernels for 0%

profile of v1, /device:TPU:1, one launch (start us, length us, event | category | flops | bytes accessed | tf_op | source)
XLA Modules:
  0.0 155.8 jit_solution(8389152297096570443)
XLA Ops:
  6.5 0.8 fusion.38
  7.3 3.3 %collective-permute-start = (f32[5,1,16,128]{3,2,0,1:T(8,128)S(1)}, f32[5,1,16,128]{3,2,0,1:T(8,128)S(1)}, u32[]{:S(2)}, u32[]{:S(2)}) collective-permute-start(f32[5,1,16,128]{3,2,0,1:T(8,128)S(1)} %get-tuple-element.87), channel_id=1, source_target_pairs={{1,0},{2,1},{3,2},{4,3},{5,4},{6,5},{7,6},{8,7},{9,8},{10,9},{11,1... | collective-permute-start | bytes 122888 | tf_op jit(solution)/shard_map/ppermute | solution.py:19
  10.7 5.5 %collective-permute-start.1 = (f32[5,1,16,128]{3,2,0,1:T(8,128)S(1)}, f32[5,1,16,128]{3,2,0,1:T(8,128)S(1)}, u32[]{:S(2)}, u32[]{:S(2)}) collective-permute-start(f32[5,1,16,128]{3,2,0,1:T(8,128)S(1)} %get-tuple-element.86), channel_id=1, source_target_pairs={{0,1},{1,2},{2,3},{3,4},{4,5},{5,6},{6,7},{7,8},{8,9},{9,10},{10,1... | collective-permute-start | bytes 122888 | tf_op jit(solution)/shard_map/ppermute | solution.py:17
  16.8 1.5 copy.19
  18.5 1.1 select_maximum_fusion
  19.7 2.2 %fusion.4 = f32[5,32,16,128]{3,2,0,1:T(8,128)} fusion(f32[5,34,18,130]{3,2,0,1:T(8,128)S(1)} %select_maximum_fusion, f32[5,32,16,128]{3,2,0,1:T(8,128)S(1)} %copy.19, f32[5,1,16,128]{3,2,0,1:T(8,128)S(1)} %collective-permute-done.1, f32[5,1,16,128]{3,2,0,1:T(8,128)S(1)} %collective-permute-done), kind=kLoop, calls=%fused_computation.16 | loop fusion | flops 2949120 | bytes 7946240 | tf_op jit(solution)/shard_map/sub | solution.py:32
  21.9 4.8 %all-to-all-start = ((f32[5,32,16,128]{3,2,0,1:T(8,128)}), f32[5,32,16,128]{3,2,0,1:T(8,128)S(1)}, u32[]{:S(2)}, u32[]{:S(2)}) async-start(f32[5,32,16,128]{3,2,0,1:T(8,128)} %fusion.4), calls=%async_computation | async-start | bytes 2621440 | tf_op jit(solution)/shard_map/all_to_all | solution.py:109
  29.3 15.6 %all-to-all-done = f32[5,32,16,128]{3,2,0,1:T(8,128)S(1)} async-done(((f32[5,32,16,128]{3,2,0,1:T(8,128)}), f32[5,32,16,128]{3,2,0,1:T(8,128)S(1)}, u32[]{:S(2)}, u32[]{:S(2)}) %all-to-all-start) | async-done | bytes 1310752 | tf_op jit(solution)/shard_map/all_to_all | solution.py:109
  45.3 9.0 %fusion.3 = f32[40,8192]{1,0:T(8,128)S(1)} fusion(f32[40,8192,1]{1,0,2:T(8,128)S(1)} %reshape.111, f32[8,8192]{1,0:T(8,128)S(1)} %bitcast.117, f32[8,40,40]{1,0,2:T(8,128)S(1)} %select_bitcast_fusion), kind=kOutput, calls=%fused_computation.12 | convolution fusion | flops 1263206400 | bytes 2934784 | tf_op jit(solution)/shard_map/dot_general | solution.py:119
  54.6 20.9 %all_to_all.33 = f32[40,4,16,128]{3,2,1,0:T(8,128)S(1)} all-to-all(f32[40,4,16,128]{3,2,1,0:T(8,128)S(1)} %bitcast.94), channel_id=1, replica_groups=mesh['mode'=8,'depth'=16] {'mode'}, dimensions={0} | all-to-all | bytes 2621440 | tf_op jit(solution)/shard_map/all_to_all | solution.py:127
  75.5 1.2 copy.27
  76.7 3.4 %shard_map.73 = (f32[5,32,16,128]{3,2,1,0:T(8,128)}, f32[32,16,128]{2,1,0:T(8,128)}, f32[32,16,128]{2,1,0:T(8,128)}, f32[5,16,128]{2,1,0:T(8,128)}) custom-call(f32[5,32,16,128]{3,2,1,0:T(8,128)} %bitcast.92, f32[32,16,128]{2,1,0:T(8,128)} %decay_ref.1), custom_call_target="tpu_custom_call" | custom-call | tf_op jit(solution)/shard_map/pallas_call | solution.py:85
  82.2 1.4 pad_maximum_fusion.2
  83.7 51.2 %all-gather.3.cloned.1.call-done = f32[192,16,128]{2,1,0:T(8,128)} async-done(((f32[12,16,128]{2,1,0:T(8,128)}), f32[192,16,128]{2,1,0:T(8,128)}) %all-gather.3.cloned.1.call-update) | async-done | bytes 1572880 | tf_op jit(solution)/shard_map/all_gather | solution.py:133
  134.9 1.0 slice_bitcast_fusion.19
  135.8 0.9 slice_bitcast_fusion.2
  137.5 0.8 constant_dynamic-update-slice_fusion.13
  138.3 0.8 constant_dynamic-update-slice_fusion.12
  139.9 0.8 constant_dynamic-update-slice_fusion.10
  141.5 0.8 constant_dynamic-update-slice_fusion.8
  143.1 0.8 constant_dynamic-update-slice_fusion.6
  144.6 0.8 constant_dynamic-update-slice_fusion.4
  146.7 0.9 copy-done.3
  147.7 1.2 multiply_add_fusion
  (66 shorter events, 11.4 us)
Async XLA Ops:
  7.3 11.0 %collective-permute-start = (f32[5,1,16,128]{3,2,0,1:T(8,128)S(1)}, f32[5,1,16,128]{3,2,0,1:T(8,128)S(1)}, u32[]{:S(2)}, u32[]{:S(2)}) collective-permute-start(f32[5,1,16,128]{3,2,0,1:T(8,128)S(1)} %get-tuple-element.87), channel_id=1, source_target_pairs={{1,0},{2,1},{3,2},{4,3},{5,4},{6,5},{7,6},{8,7},{9,8},{10,9},{11,1... | collective-permute-start | bytes 122888 | tf_op jit(solution)/shard_map/ppermute | solution.py:19
  10.7 7.7 %collective-permute-start.1 = (f32[5,1,16,128]{3,2,0,1:T(8,128)S(1)}, f32[5,1,16,128]{3,2,0,1:T(8,128)S(1)}, u32[]{:S(2)}, u32[]{:S(2)}) collective-permute-start(f32[5,1,16,128]{3,2,0,1:T(8,128)S(1)} %get-tuple-element.86), channel_id=1, source_target_pairs={{0,1},{1,2},{2,3},{3,4},{4,5},{5,6},{6,7},{7,8},{8,9},{9,10},{10,1... | collective-permute-start | bytes 122888 | tf_op jit(solution)/shard_map/ppermute | solution.py:17
  16.8 1.7 %copy-start = (f32[5,32,16,128]{3,2,1,0:T(8,128)S(1)}, f32[5,32,16,128]{3,2,1,0:T(8,128)}, u32[]{:S(2)}) copy-start(f32[5,32,16,128]{3,2,1,0:T(8,128)} %param.7) | copy-start | bytes 3932164
  21.9 4.8 %copy-start.1 = (f32[7,32,16,128]{3,2,1,0:T(8,128)S(1)}, f32[7,32,16,128]{3,2,1,0:T(8,128)}, u32[]{:S(2)}) copy-start(f32[7,32,16,128]{3,2,1,0:T(8,128)} %param.9) | copy-start | bytes 5505028
  21.9 4.8 %copy-start.6 = (f32[32,16,128]{2,1,0:T(8,128)S(1)}, f32[32,16,128]{2,1,0:T(8,128)}, u32[]{:S(2)}) copy-start(f32[32,16,128]{2,1,0:T(8,128)} %param.8) | copy-start | bytes 786436
  21.9 23.0 %all-to-all-start = ((f32[5,32,16,128]{3,2,0,1:T(8,128)}), f32[5,32,16,128]{3,2,0,1:T(8,128)S(1)}, u32[]{:S(2)}, u32[]{:S(2)}) async-start(f32[5,32,16,128]{3,2,0,1:T(8,128)} %fusion.4), calls=%async_computation | async-start | bytes 2621440 | tf_op jit(solution)/shard_map/all_to_all | solution.py:109
  26.7 108.2 %all-gather.3.cloned.1.call-start = ((), (), s32[]{:S(2)}) async-start(), calls=%async_computation.2 | async-start | bytes 1671168 | tf_op jit(solution)/shard_map/all_gather | solution.py:133
  26.7 0.9 copy-start.7
  26.7 1.0 copy-start.8
  26.8 1.6 %copy-start.9 = (s32[40]{0:T(128)S(1)}, s32[40]{0:T(128)}, u32[]{:S(2)}) copy-start(s32[40]{0:T(128)} %param.13) | copy-start | bytes 484
  134.9 11.3 %copy-start.2 = (f32[192,16,128]{2,1,0:T(8,128)S(1)}, f32[192,16,128]{2,1,0:T(8,128)}, u32[]{:S(2)}) copy-start(f32[192,16,128]{2,1,0:T(8,128)} %all-gather.3.cloned.1.call-done) | copy-start | bytes 4718596
  146.3 1.3 copy-start.3
  146.3 1.3 copy-start.4
  146.3 1.4 copy-start.5
Sparse Core Ops, SparseCore 0:
  83.8 51.0 all-gather.2

commit v2 on v1

--- a/solution.py
+++ b/solution.py
@@ -130,8 +130,9 @@
     summary = jnp.concatenate(
         [tail[:1], coupled[:1], forward_end, back[:, 0]], axis=0
     )
-    summaries = lax.all_gather(summary, "depth", axis=0, tiled=False)
-    slabs = summaries.shape[0]
+    slabs = lax.axis_size("depth")
+    copies = jnp.broadcast_to(summary[None], (slabs,) + summary.shape)
+    summaries = lax.all_to_all(copies, "depth", 0, 0, tiled=True)
     ratio_all = summaries[:, 0]
     coupled_all = summaries[:, 1]
     forward_all = summaries[:, 2 : 2 + local_modes]

time: 157 us -> 125 us (0.80)
  waiting for transfers between devices: 66.8 us -> 38.5 us
  between operations: 13.8 us -> 0.41 us
  starting transfers between devices: 13.6 us -> 25.2 us
  other arithmetic: 18.5 us -> 14.6 us
  local copies, waits for them, and re-layouts: 9.78 us -> 12.2 us
    all_gather x1 -> x0, waiting for transfers between devices: 51.2 us -> none  [local(): summaries = lax.all_gather(summary, 'depth', axis=0, tiled=False)]
    all_to_all x0 -> x1, waiting for transfers between devices: none -> 22.8 us  [local(): summaries = lax.all_to_all(copies, 'depth', 0, 0, tiled=True)]
    all_to_all x0 -> x1, starting transfers between devices: none -> 11.6 us  [local(): summaries = lax.all_to_all(copies, 'depth', 0, 0, tiled=True)]
    unnamed x37 -> x39, local copies, waits for them, and re-layouts: 3.91 us -> 5.01 us
where the time goes in v2:
time: 125 us; the launch traced here: 124 us
  waiting for transfers between devices  38.5 us (31%)
  starting transfers between devices  25.2 us (20%)
  blocking collectives  20.9 us (17%)
  other arithmetic  14.6 us (12%)
  local copies, waits for them, and re-layouts  12.2 us (10%)
  matrix products  8.97 us (7%)
  Pallas kernels  3.4 us (3%)
    all_to_all x1, waiting for transfers between devices, local(): summaries = lax.all_to_all(copies, 'depth', 0, 0, tiled=True)  22.8 us
    all_to_all x1, blocking collectives, local(): mixed_field = lax.all_to_all(mixed_rows, 'mode', 0, 1, tiled=True)  20.9 us
    all_to_all x1, waiting for transfers between devices, local(): stencil_rows = lax.all_to_all(stencil, 'mode', 1, 0, tiled=True)  15.6 us
    all_to_all x1, starting transfers between devices, local(): summaries = lax.all_to_all(copies, 'depth', 0, 0, tiled=True)  11.6 us
    dot_general x1, matrix products, local(): jnp.dot(table_rows, stencil_rows, precision=lax.Precision.HIGHEST, prefer...  8.97 us
    unnamed x15, other arithmetic  8.23 us
    ppermute x1, starting transfers between devices, with_halo(): lax.ppermute(tail, axis, [(i, (i + 1) % count) for i in range(ends)])  5.49 us
    unnamed x39, local copies, waits for them, and re-layouts  5.01 us
  transfers between devices with their start and end apart: 4, of which 2 were waited for; matrix products, arithmetic and copies ran while one was open for 3% of the time, Pallas kernels for 0%

profile of v2, /device:TPU:1, one launch (start us, length us, event | category | flops | bytes accessed | tf_op | source)
XLA Modules:
  0.0 124.2 jit_solution(17805463589357040634)
XLA Ops:
  0.0 0.8 fusion.38
  0.8 3.3 %collective-permute-start = (f32[5,1,16,128]{3,2,0,1:T(8,128)S(1)}, f32[5,1,16,128]{3,2,0,1:T(8,128)S(1)}, u32[]{:S(2)}, u32[]{:S(2)}) collective-permute-start(f32[5,1,16,128]{3,2,0,1:T(8,128)S(1)} %get-tuple-element.87), channel_id=1, source_target_pairs={{1,0},{2,1},{3,2},{4,3},{5,4},{6,5},{7,6},{8,7},{9,8},{10,9},{11,1... | collective-permute-start | bytes 122888 | tf_op jit(solution)/shard_map/ppermute | solution.py:19
  4.1 5.5 %collective-permute-start.1 = (f32[5,1,16,128]{3,2,0,1:T(8,128)S(1)}, f32[5,1,16,128]{3,2,0,1:T(8,128)S(1)}, u32[]{:S(2)}, u32[]{:S(2)}) collective-permute-start(f32[5,1,16,128]{3,2,0,1:T(8,128)S(1)} %get-tuple-element.86), channel_id=1, source_target_pairs={{0,1},{1,2},{2,3},{3,4},{4,5},{5,6},{6,7},{7,8},{8,9},{9,10},{10,1... | collective-permute-start | bytes 122888 | tf_op jit(solution)/shard_map/ppermute | solution.py:17
  10.3 1.5 %copy.19 = f32[5,32,16,128]{3,2,0,1:T(8,128)S(1)} copy(f32[5,32,16,128]{3,2,1,0:T(8,128)} %param.7) | data formatting | bytes 2621440 | tf_op args[0]
  12.0 1.1 select_maximum_fusion
  13.2 2.2 %fusion.4 = f32[5,32,16,128]{3,2,0,1:T(8,128)} fusion(f32[5,34,18,130]{3,2,0,1:T(8,128)S(1)} %select_maximum_fusion, f32[5,32,16,128]{3,2,0,1:T(8,128)S(1)} %copy.19, f32[5,1,16,128]{3,2,0,1:T(8,128)S(1)} %collective-permute-done.1, f32[5,1,16,128]{3,2,0,1:T(8,128)S(1)} %collective-permute-done), kind=kLoop, calls=%fused_computation.16 | loop fusion | flops 2949120 | bytes 7946240 | tf_op jit(solution)/shard_map/sub | solution.py:32
  15.3 4.8 %all-to-all-start = ((f32[5,32,16,128]{3,2,0,1:T(8,128)}), f32[5,32,16,128]{3,2,0,1:T(8,128)S(1)}, u32[]{:S(2)}, u32[]{:S(2)}) async-start(f32[5,32,16,128]{3,2,0,1:T(8,128)} %fusion.4), calls=%async_computation | async-start | bytes 2621440 | tf_op jit(solution)/shard_map/all_to_all | solution.py:109
  22.8 15.6 %all-to-all-done = f32[5,32,16,128]{3,2,0,1:T(8,128)S(1)} async-done(((f32[5,32,16,128]{3,2,0,1:T(8,128)}), f32[5,32,16,128]{3,2,0,1:T(8,128)S(1)}, u32[]{:S(2)}, u32[]{:S(2)}) %all-to-all-start) | async-done | bytes 1310752 | tf_op jit(solution)/shard_map/all_to_all | solution.py:109
  38.8 9.0 %fusion.3 = f32[40,8192]{1,0:T(8,128)S(1)} fusion(f32[40,8192,1]{1,0,2:T(8,128)S(1)} %reshape.111, f32[8,8192]{1,0:T(8,128)S(1)} %bitcast.98, f32[8,40,40]{1,0,2:T(8,128)S(1)} %select_bitcast_fusion), kind=kOutput, calls=%fused_computation.12 | convolution fusion | flops 1263206400 | bytes 2934784 | tf_op jit(solution)/shard_map/dot_general | solution.py:119
  48.0 20.9 %all_to_all.38 = f32[40,4,16,128]{3,2,1,0:T(8,128)S(1)} all-to-all(f32[40,4,16,128]{3,2,1,0:T(8,128)S(1)} %bitcast.93), channel_id=1, replica_groups=mesh['mode'=8,'depth'=16] {'mode'}, dimensions={0} | all-to-all | bytes 2621440 | tf_op jit(solution)/shard_map/all_to_all | solution.py:127
  69.0 1.2 copy.27
  70.1 3.4 %shard_map.73 = (f32[5,32,16,128]{3,2,1,0:T(8,128)}, f32[32,16,128]{2,1,0:T(8,128)}, f32[32,16,128]{2,1,0:T(8,128)}, f32[5,16,128]{2,1,0:T(8,128)}) custom-call(f32[5,32,16,128]{3,2,1,0:T(8,128)} %bitcast.91, f32[32,16,128]{2,1,0:T(8,128)} %decay_ref.1), custom_call_target="tpu_custom_call" | custom-call | tf_op jit(solution)/shard_map/pallas_call | solution.py:85
  76.5 1.3 %broadcast_in_dim.38 = f32[16,12,16,128]{3,2,1,0:T(8,128)} broadcast(f32[12,16,128]{2,1,0:T(8,128)S(1)} %pad_maximum_fusion.2), dimensions={1,2,3} | broadcast | bytes 1671168 | tf_op jit(solution)/shard_map/broadcast_in_dim | solution.py:134
  77.8 11.6 %all-to-all-start.2 = ((f32[16,12,16,128]{3,2,1,0:T(8,128)}), f32[16,12,16,128]{3,2,1,0:T(8,128)S(1)}, u32[]{:S(2)}, u32[]{:S(2)}) async-start(f32[16,12,16,128]{3,2,1,0:T(8,128)} %broadcast_in_dim.38), calls=%async_computation.2 | async-start | bytes 3145728 | tf_op jit(solution)/shard_map/all_to_all | solution.py:135
  89.5 22.8 %all-to-all-done.2 = f32[16,12,16,128]{3,2,1,0:T(8,128)S(1)} async-done(((f32[16,12,16,128]{3,2,1,0:T(8,128)}), f32[16,12,16,128]{3,2,1,0:T(8,128)S(1)}, u32[]{:S(2)}, u32[]{:S(2)}) %all-to-all-start.2) | async-done | bytes 1572896 | tf_op jit(solution)/shard_map/all_to_all | solution.py:135
  112.3 1.1 copy-done
  113.5 0.8 constant_dynamic-update-slice_fusion.12
  114.3 0.9 constant_dynamic-update-slice_fusion.11
  115.2 0.8 constant_dynamic-update-slice_fusion.10
  116.7 0.8 constant_dynamic-update-slice_fusion.8
  118.3 0.8 constant_dynamic-update-slice_fusion.6
  119.9 0.8 constant_dynamic-update-slice_fusion.4
  122.0 0.9 copy-done.4
  122.9 1.2 multiply_add_fusion
  (68 shorter events, 10.6 us)
Async XLA Ops:
  0.8 11.0 %collective-permute-start = (f32[5,1,16,128]{3,2,0,1:T(8,128)S(1)}, f32[5,1,16,128]{3,2,0,1:T(8,128)S(1)}, u32[]{:S(2)}, u32[]{:S(2)}) collective-permute-start(f32[5,1,16,128]{3,2,0,1:T(8,128)S(1)} %get-tuple-element.87), channel_id=1, source_target_pairs={{1,0},{2,1},{3,2},{4,3},{5,4},{6,5},{7,6},{8,7},{9,8},{10,9},{11,1... | collective-permute-start | bytes 122888 | tf_op jit(solution)/shard_map/ppermute | solution.py:19
  4.1 7.7 %collective-permute-start.1 = (f32[5,1,16,128]{3,2,0,1:T(8,128)S(1)}, f32[5,1,16,128]{3,2,0,1:T(8,128)S(1)}, u32[]{:S(2)}, u32[]{:S(2)}) collective-permute-start(f32[5,1,16,128]{3,2,0,1:T(8,128)S(1)} %get-tuple-element.86), channel_id=1, source_target_pairs={{0,1},{1,2},{2,3},{3,4},{4,5},{5,6},{6,7},{7,8},{8,9},{9,10},{10,1... | collective-permute-start | bytes 122888 | tf_op jit(solution)/shard_map/ppermute | solution.py:17
  10.3 1.7 %copy-start.2 = (f32[5,32,16,128]{3,2,1,0:T(8,128)S(1)}, f32[5,32,16,128]{3,2,1,0:T(8,128)}, u32[]{:S(2)}) copy-start(f32[5,32,16,128]{3,2,1,0:T(8,128)} %param.7) | copy-start | bytes 3932164
  15.3 4.8 %copy-start.3 = (f32[7,32,16,128]{3,2,1,0:T(8,128)S(1)}, f32[7,32,16,128]{3,2,1,0:T(8,128)}, u32[]{:S(2)}) copy-start(f32[7,32,16,128]{3,2,1,0:T(8,128)} %param.9) | copy-start | bytes 5505028
  15.3 4.8 %copy-start.7 = (f32[32,16,128]{2,1,0:T(8,128)S(1)}, f32[32,16,128]{2,1,0:T(8,128)}, u32[]{:S(2)}) copy-start(f32[32,16,128]{2,1,0:T(8,128)} %param.8) | copy-start | bytes 786436
  15.3 23.0 %all-to-all-start = ((f32[5,32,16,128]{3,2,0,1:T(8,128)}), f32[5,32,16,128]{3,2,0,1:T(8,128)S(1)}, u32[]{:S(2)}, u32[]{:S(2)}) async-start(f32[5,32,16,128]{3,2,0,1:T(8,128)} %fusion.4), calls=%async_computation | async-start | bytes 2621440 | tf_op jit(solution)/shard_map/all_to_all | solution.py:109
  20.1 0.9 copy-start.8
  20.1 1.0 copy-start.9
  20.2 1.6 %copy-start.10 = (s32[40]{0:T(128)S(1)}, s32[40]{0:T(128)}, u32[]{:S(2)}) copy-start(s32[40]{0:T(128)} %param.13) | copy-start | bytes 484
  77.8 34.5 %all-to-all-start.2 = ((f32[16,12,16,128]{3,2,1,0:T(8,128)}), f32[16,12,16,128]{3,2,1,0:T(8,128)S(1)}, u32[]{:S(2)}, u32[]{:S(2)}) async-start(f32[16,12,16,128]{3,2,1,0:T(8,128)} %broadcast_in_dim.38), calls=%async_computation.2 | async-start | bytes 3145728 | tf_op jit(solution)/shard_map/all_to_all | solution.py:135
  112.3 1.2 copy-start
  114.2 7.2 %copy-start.1 = (f32[16,12,16,128]{3,2,1,0:T(8,128)S(1)}, f32[16,12,16,128]{3,2,1,0:T(8,128)}, u32[]{:S(2)}) copy-start(f32[16,12,16,128]{3,2,1,0:T(8,128)} %copy-done) | copy-start | bytes 4718596
  121.5 1.3 %copy-start.4 = (f32[5,32,16,128]{3,2,1,0:T(8,128)S(1)}, f32[5,32,16,128]{3,2,1,0:T(8,128)}, u32[]{:S(2)}) copy-start(f32[5,32,16,128]{3,2,1,0:T(8,128)} %get-tuple-element.9) | copy-start | bytes 3932164
  121.5 1.3 %copy-start.5 = (f32[32,16,128]{2,1,0:T(8,128)S(1)}, f32[32,16,128]{2,1,0:T(8,128)}, u32[]{:S(2)}) copy-start(f32[32,16,128]{2,1,0:T(8,128)} %get-tuple-element.10) | copy-start | bytes 786436
  121.5 1.4 %copy-start.6 = (f32[32,16,128]{2,1,0:T(8,128)S(1)}, f32[32,16,128]{2,1,0:T(8,128)}, u32[]{:S(2)}) copy-start(f32[32,16,128]{2,1,0:T(8,128)} %get-tuple-element.11) | copy-start | bytes 786436

commit v3 on v2

--- a/solution.py
+++ b/solution.py
@@ -32,7 +32,7 @@
     return 6.0 * centre - beside
 
 
-def sweep_kernel(mixed_ref, decay_ref, back_ref, coupled_ref, tail_ref, forward_ref):
+def sweep_kernel(mixed_ref, decay_ref, back_ref, coupled_ref, tail_ref, summary_ref):
     rows = decay_ref.shape[0]
 
     def forward_row(z, carried):
@@ -53,7 +53,6 @@
         forward_row,
         (jnp.zeros((modes,) + lateral, jnp.float32), jnp.ones(lateral, jnp.float32)),
     )
-    forward_ref[...] = state
 
     def backward_row(i, carried):
         z = rows - 1 - i
@@ -67,7 +66,7 @@
         tail_ref[z] = tail
         return back, coupled, tail
 
-    lax.fori_loop(
+    back, coupled, tail = lax.fori_loop(
         0,
         rows,
         backward_row,
@@ -77,9 +76,14 @@
             jnp.ones(lateral, jnp.float32),
         ),
     )
+    for copy in range(summary_ref.shape[0]):
+        summary_ref[copy, 0] = tail
+        summary_ref[copy, 1] = coupled
+        summary_ref[copy, 2 : 2 + modes] = state
+        summary_ref[copy, 2 + modes :] = back
 
 
-def local_sweeps(mixed, decay):
+def local_sweeps(mixed, decay, copies):
     modes, rows = mixed.shape[0], mixed.shape[1]
     lateral = mixed.shape[2:]
     return pl.pallas_call(
@@ -88,7 +92,7 @@
             jax.ShapeDtypeStruct(mixed.shape, jnp.float32),
             jax.ShapeDtypeStruct(decay.shape, jnp.float32),
             jax.ShapeDtypeStruct(decay.shape, jnp.float32),
-            jax.ShapeDtypeStruct((modes,) + lateral, jnp.float32),
+            jax.ShapeDtypeStruct((copies, 2 + 2 * modes) + lateral, jnp.float32),
         ),
     )(mixed, decay)
 
@@ -126,32 +130,30 @@
     mixed_rows = mixed_rows.reshape((mode_total, chunk) + lateral)
     mixed_field = lax.all_to_all(mixed_rows, "mode", 0, 1, tiled=True)
 
-    back, coupled, tail, forward_end = local_sweeps(mixed_field, decay)
-    summary = jnp.concatenate(
-        [tail[:1], coupled[:1], forward_end, back[:, 0]], axis=0
-    )
     slabs = lax.axis_size("depth")
-    copies = jnp.broadcast_to(summary[None], (slabs,) + summary.shape)
+    back, coupled, tail, copies = local_sweeps(mixed_field, decay, slabs)
     summaries = lax.all_to_all(copies, "depth", 0, 0, tiled=True)
     ratio_all = summaries[:, 0]
     coupled_all = summaries[:, 1]
     forward_all = summaries[:, 2 : 2 + local_modes]
     back_all = summaries[:, 2 + local_modes :]
 
-    state_low = [jnp.zeros_like(forward_all[0])]
+    me = lax.axis_index("depth")
+    entering = [jnp.zeros_like(forward_all[0])]
     for slab in range(slabs - 1):
-        state_low.append(ratio_all[slab][None] * state_low[-1] + forward_all[slab])
-    state_high = [jnp.zeros_like(forward_all[0])]
+        entering.append(ratio_all[slab][None] * entering[-1] + forward_all[slab])
+    low = entering[0]
+    for slab in range(1, slabs):
+        low = jnp.where(me == slab, entering[slab], low)
+    above = jnp.zeros_like(forward_all[0])
+    high = above
     for slab in range(slabs - 1, 0, -1):
-        state_high.append(
+        above = (
             back_all[slab]
-            + coupled_all[slab][None] * state_low[slab]
-            + ratio_all[slab][None] * state_high[-1]
+            + coupled_all[slab][None] * entering[slab]
+            + ratio_all[slab][None] * above
         )
-    state_high = state_high[::-1]
-    me = lax.axis_index("depth")
-    low = lax.dynamic_index_in_dim(jnp.stack(state_low), me, 0, keepdims=False)
-    high = lax.dynamic_index_in_dim(jnp.stack(state_high), me, 0, keepdims=False)
+        high = jnp.where(me == slab - 1, above, high)
     return back + coupled[None] * low[:, None] + tail[None] * high[:, None]
 
 

time: 125 us -> 112 us (0.90)
  other arithmetic: 14.6 us -> 5.86 us
  local copies, waits for them, and re-layouts: 12.2 us -> 7.58 us
    unnamed x15 -> x0, other arithmetic: 8.23 us -> none
    slice x2 -> x0, local copies, waits for them, and re-layouts: 1.39 us -> none  [the longest x1 0.7 us: local(): coupled[:1]]
    broadcast_in_dim x1 -> x0, local copies, waits for them, and re-layouts: 1.33 us -> none  [local(): copies = jnp.broadcast_to(summary[None], (slabs,) + summary.shape)]
    unnamed x39 -> x21, local copies, waits for them, and re-layouts: 5.01 us -> 3.89 us
  transfers between devices with their start and end apart: 4 -> 4, of which waited for: 2 -> 2; matrix products, arithmetic and copies ran while one was open for 3% -> 4% of each run, Pallas kernels for 0% -> 0%
where the time goes in v3:
time: 112 us; the launch traced here: 111 us
  waiting for transfers between devices  38.5 us (34%)
  starting transfers between devices  25.2 us (22%)
  blocking collectives  20.9 us (19%)
  matrix products  8.97 us (8%)
  local copies, waits for them, and re-layouts  7.58 us (7%)
  other arithmetic  5.86 us (5%)
  Pallas kernels  3.98 us (4%)
    all_to_all x1, waiting for transfers between devices, local(): summaries = lax.all_to_all(copies, 'depth', 0, 0, tiled=True)  22.8 us
    all_to_all x1, blocking collectives, local(): mixed_field = lax.all_to_all(mixed_rows, 'mode', 0, 1, tiled=True)  20.9 us
    all_to_all x1, waiting for transfers between devices, local(): stencil_rows = lax.all_to_all(stencil, 'mode', 1, 0, tiled=True)  15.6 us
    all_to_all x1, starting transfers between devices, local(): summaries = lax.all_to_all(copies, 'depth', 0, 0, tiled=True)  11.6 us
    dot_general x1, matrix products, local(): jnp.dot(table_rows, stencil_rows, precision=lax.Precision.HIGHEST, prefer...  8.97 us
    ppermute x1, starting transfers between devices, with_halo(): lax.ppermute(tail, axis, [(i, (i + 1) % count) for i in range(ends)])  5.49 us
    all_to_all x1, starting transfers between devices, local(): stencil_rows = lax.all_to_all(stencil, 'mode', 1, 0, tiled=True)  4.78 us
    pallas_call x1, Pallas kernels, local_sweeps(): pl.pallas_call(sweep_kernel, out_shape=(jax.ShapeDtypeStruct(mixed.shape,...  3.98 us
  transfers between devices with their start and end apart: 4, of which 2 were waited for; matrix products, arithmetic and copies ran while one was open for 4% of the time, Pallas kernels for 0%

profile of v3, /device:TPU:1, one launch (start us, length us, event | category | flops | bytes accessed | tf_op | source)
XLA Modules:
  0.0 111.2 jit_solution(8369192401879605202)
XLA Ops:
  0.0 0.8 fusion.56
  0.8 3.3 %collective-permute-start = (f32[5,1,16,128]{3,2,0,1:T(8,128)S(1)}, f32[5,1,16,128]{3,2,0,1:T(8,128)S(1)}, u32[]{:S(2)}, u32[]{:S(2)}) collective-permute-start(f32[5,1,16,128]{3,2,0,1:T(8,128)S(1)} %get-tuple-element.45), channel_id=1, source_target_pairs={{1,0},{2,1},{3,2},{4,3},{5,4},{6,5},{7,6},{8,7},{9,8},{10,9},{11,1... | collective-permute-start | bytes 122888 | tf_op jit(solution)/shard_map/ppermute | solution.py:19
  4.1 5.5 %collective-permute-start.1 = (f32[5,1,16,128]{3,2,0,1:T(8,128)S(1)}, f32[5,1,16,128]{3,2,0,1:T(8,128)S(1)}, u32[]{:S(2)}, u32[]{:S(2)}) collective-permute-start(f32[5,1,16,128]{3,2,0,1:T(8,128)S(1)} %get-tuple-element.44), channel_id=1, source_target_pairs={{0,1},{1,2},{2,3},{3,4},{4,5},{5,6},{6,7},{7,8},{8,9},{9,10},{10,1... | collective-permute-start | bytes 122888 | tf_op jit(solution)/shard_map/ppermute | solution.py:17
  9.6 0.7 compare_select_fusion
  10.3 1.5 %copy.17 = f32[5,32,16,128]{3,2,0,1:T(8,128)S(1)} copy(f32[5,32,16,128]{3,2,1,0:T(8,128)} %param.7) | data formatting | bytes 2621440 | tf_op args[0]
  11.8 0.2 copy-done
  12.0 1.1 %select_maximum_fusion = f32[5,34,18,130]{3,2,0,1:T(8,128)S(1)} fusion(f32[5,1,16,128]{3,2,0,1:T(8,128)S(1)} %collective-permute-done, f32[5,1,16,128]{3,2,0,1:T(8,128)S(1)} %collective-permute-done.1, f32[5,32,16,128]{3,2,1,0:T(8,128)S(1)} %copy-done), kind=kLoop, calls=%fused_computation.7 | loop fusion | flops 5967000 | bytes 2983840 | tf_op jit(solution)/shard_map/concatenate | solution.py:15
  13.2 2.2 %fusion.4 = f32[5,32,16,128]{3,2,0,1:T(8,128)} fusion(f32[5,34,18,130]{3,2,0,1:T(8,128)S(1)} %select_maximum_fusion, f32[5,32,16,128]{3,2,0,1:T(8,128)S(1)} %copy.17, f32[5,1,16,128]{3,2,0,1:T(8,128)S(1)} %collective-permute-done.1, f32[5,1,16,128]{3,2,0,1:T(8,128)S(1)} %collective-permute-done), kind=kLoop, calls=%fused_computation.16 | loop fusion | flops 2949120 | bytes 7946240 | tf_op jit(solution)/shard_map/sub | solution.py:32
  15.3 4.8 %all-to-all-start = ((f32[5,32,16,128]{3,2,0,1:T(8,128)}), f32[5,32,16,128]{3,2,0,1:T(8,128)S(1)}, u32[]{:S(2)}, u32[]{:S(2)}) async-start(f32[5,32,16,128]{3,2,0,1:T(8,128)} %fusion.4), calls=%async_computation | async-start | bytes 2621440 | tf_op jit(solution)/shard_map/all_to_all | solution.py:113
  20.4 0.7 copy-done.6
  21.2 0.6 gather_fusion
  22.0 0.6 gather_fusion.1
  22.8 15.6 %all-to-all-done = f32[5,32,16,128]{3,2,0,1:T(8,128)S(1)} async-done(((f32[5,32,16,128]{3,2,0,1:T(8,128)}), f32[5,32,16,128]{3,2,0,1:T(8,128)S(1)}, u32[]{:S(2)}, u32[]{:S(2)}) %all-to-all-start) | async-done | bytes 1310752 | tf_op jit(solution)/shard_map/all_to_all | solution.py:113
  38.6 0.2 reshape.389
  38.8 9.0 %fusion.3 = f32[40,8192]{1,0:T(8,128)S(1)} fusion(f32[40,8192,1]{1,0,2:T(8,128)S(1)} %reshape.389, f32[8,8192]{1,0:T(8,128)S(1)} %bitcast.332, f32[8,40,40]{1,0,2:T(8,128)S(1)} %select_bitcast_fusion), kind=kOutput, calls=%fused_computation.12 | convolution fusion | flops 1263206400 | bytes 2934784 | tf_op jit(solution)/shard_map/dot_general | solution.py:123
  47.8 0.2 copy.27
  48.0 20.9 %all_to_all.38 = f32[40,4,16,128]{3,2,1,0:T(8,128)S(1)} all-to-all(f32[40,4,16,128]{3,2,1,0:T(8,128)S(1)} %bitcast.327), channel_id=1, replica_groups=mesh['mode'=8,'depth'=16] {'mode'}, dimensions={0} | all-to-all | bytes 2621440 | tf_op jit(solution)/shard_map/all_to_all | solution.py:131
  69.0 1.2 %copy.25 = f32[5,8,4,16,128]{4,3,2,1,0:T(8,128)} copy(f32[5,8,4,16,128]{4,3,2,0,1:T(8,128)S(1)} %bitcast.328) | data formatting | bytes 2621440 | tf_op jit(solution)/shard_map/all_to_all | solution.py:131
  70.1 4.0 %shard_map.73 = (f32[5,32,16,128]{3,2,1,0:T(8,128)}, f32[32,16,128]{2,1,0:T(8,128)}, f32[32,16,128]{2,1,0:T(8,128)}, f32[16,12,16,128]{3,2,1,0:T(8,128)}) custom-call(f32[5,32,16,128]{3,2,1,0:T(8,128)} %bitcast.325, f32[32,16,128]{2,1,0:T(8,128)} %decay_ref.1), custom_call_target="tpu_custom_call" | custom-call | tf_op jit(solution)/shard_map/pallas_call | solution.py:89
  74.1 11.6 %all-to-all-start.2 = ((f32[16,12,16,128]{3,2,1,0:T(8,128)}), f32[16,12,16,128]{3,2,1,0:T(8,128)S(1)}, u32[]{:S(2)}, u32[]{:S(2)}) async-start(f32[16,12,16,128]{3,2,1,0:T(8,128)} %get-tuple-element.11), calls=%async_computation.2 | async-start | bytes 3145728 | tf_op jit(solution)/shard_map/all_to_all | solution.py:135
  85.7 22.8 %all-to-all-done.2 = f32[16,12,16,128]{3,2,1,0:T(8,128)S(1)} async-done(((f32[16,12,16,128]{3,2,1,0:T(8,128)}), f32[16,12,16,128]{3,2,1,0:T(8,128)S(1)}, u32[]{:S(2)}, u32[]{:S(2)}) %all-to-all-start.2) | async-done | bytes 1572896 | tf_op jit(solution)/shard_map/all_to_all | solution.py:135
  108.7 0.2 fusion.38
  109.0 0.9 copy-done.2
  110.0 1.2 %multiply_add_fusion = f32[5,32,16,128]{3,2,1,0:T(8,128)} fusion(f32[5,32,16,128]{3,2,1,0:T(8,128)S(1)} %copy-done.2, f32[5,16,128]{2,1,0:T(8,128)S(1)} %fusion.38, f32[32,16,128]{2,1,0:T(8,128)S(1)} %copy-done.5, f32[5,16,128]{2,1,0:T(8,128)S(1)} %select_select_fusion, f32[32,16,128]{2,1,0:T(8,128)S(1)} %copy-done.4), kind=kLoop, calls=%fused_computation.24 | loop fusion | flops 1310720 | bytes 3227648 | tf_op jit(solution)/shard_map/add | solution.py:157
  (29 shorter events, 1.1 us)
Async XLA Ops:
  0.8 11.0 %collective-permute-start = (f32[5,1,16,128]{3,2,0,1:T(8,128)S(1)}, f32[5,1,16,128]{3,2,0,1:T(8,128)S(1)}, u32[]{:S(2)}, u32[]{:S(2)}) collective-permute-start(f32[5,1,16,128]{3,2,0,1:T(8,128)S(1)} %get-tuple-element.45), channel_id=1, source_target_pairs={{1,0},{2,1},{3,2},{4,3},{5,4},{6,5},{7,6},{8,7},{9,8},{10,9},{11,1... | collective-permute-start | bytes 122888 | tf_op jit(solution)/shard_map/ppermute | solution.py:19
  4.1 7.7 %collective-permute-start.1 = (f32[5,1,16,128]{3,2,0,1:T(8,128)S(1)}, f32[5,1,16,128]{3,2,0,1:T(8,128)S(1)}, u32[]{:S(2)}, u32[]{:S(2)}) collective-permute-start(f32[5,1,16,128]{3,2,0,1:T(8,128)S(1)} %get-tuple-element.44), channel_id=1, source_target_pairs={{0,1},{1,2},{2,3},{3,4},{4,5},{5,6},{6,7},{7,8},{8,9},{9,10},{10,1... | collective-permute-start | bytes 122888 | tf_op jit(solution)/shard_map/ppermute | solution.py:17
  10.3 1.7 %copy-start = (f32[5,32,16,128]{3,2,1,0:T(8,128)S(1)}, f32[5,32,16,128]{3,2,1,0:T(8,128)}, u32[]{:S(2)}) copy-start(f32[5,32,16,128]{3,2,1,0:T(8,128)} %param.7) | copy-start | bytes 3932164
  15.3 4.8 %copy-start.1 = (f32[7,32,16,128]{3,2,1,0:T(8,128)S(1)}, f32[7,32,16,128]{3,2,1,0:T(8,128)}, u32[]{:S(2)}) copy-start(f32[7,32,16,128]{3,2,1,0:T(8,128)} %param.9) | copy-start | bytes 5505028
  15.3 4.8 %copy-start.3 = (f32[32,16,128]{2,1,0:T(8,128)S(1)}, f32[32,16,128]{2,1,0:T(8,128)}, u32[]{:S(2)}) copy-start(f32[32,16,128]{2,1,0:T(8,128)} %param.8) | copy-start | bytes 786436
  15.3 23.0 %all-to-all-start = ((f32[5,32,16,128]{3,2,0,1:T(8,128)}), f32[5,32,16,128]{3,2,0,1:T(8,128)S(1)}, u32[]{:S(2)}, u32[]{:S(2)}) async-start(f32[5,32,16,128]{3,2,0,1:T(8,128)} %fusion.4), calls=%async_computation | async-start | bytes 2621440 | tf_op jit(solution)/shard_map/all_to_all | solution.py:113
  20.1 0.9 copy-start.6
  20.1 1.0 copy-start.7
  20.2 1.6 %copy-start.8 = (s32[40]{0:T(128)S(1)}, s32[40]{0:T(128)}, u32[]{:S(2)}) copy-start(s32[40]{0:T(128)} %param.13) | copy-start | bytes 484
  74.1 34.5 %all-to-all-start.2 = ((f32[16,12,16,128]{3,2,1,0:T(8,128)}), f32[16,12,16,128]{3,2,1,0:T(8,128)S(1)}, u32[]{:S(2)}, u32[]{:S(2)}) async-start(f32[16,12,16,128]{3,2,1,0:T(8,128)} %get-tuple-element.11), calls=%async_computation.2 | async-start | bytes 3145728 | tf_op jit(solution)/shard_map/all_to_all | solution.py:135
  108.6 1.3 %copy-start.2 = (f32[5,32,16,128]{3,2,1,0:T(8,128)S(1)}, f32[5,32,16,128]{3,2,1,0:T(8,128)}, u32[]{:S(2)}) copy-start(f32[5,32,16,128]{3,2,1,0:T(8,128)} %get-tuple-element.9) | copy-start | bytes 3932164
  108.6 1.3 %copy-start.4 = (f32[32,16,128]{2,1,0:T(8,128)S(1)}, f32[32,16,128]{2,1,0:T(8,128)}, u32[]{:S(2)}) copy-start(f32[32,16,128]{2,1,0:T(8,128)} %get-tuple-element.10) | copy-start | bytes 786436
  108.6 1.4 %copy-start.5 = (f32[32,16,128]{2,1,0:T(8,128)S(1)}, f32[32,16,128]{2,1,0:T(8,128)}, u32[]{:S(2)}) copy-start(f32[32,16,128]{2,1,0:T(8,128)} %get-tuple-element.12) | copy-start | bytes 786436

commit v4 on v3

--- a/solution.py
+++ b/solution.py
@@ -117,16 +117,15 @@
     coefficients = jnp.concatenate([mean_field[None], kl_modes], axis=0)
     my_chunk = lax.axis_index("mode") * chunk
     coefficients = lax.dynamic_slice_in_dim(coefficients, my_chunk, chunk, axis=1)
-    coefficients = coefficients.reshape(term_total, 1, cell_count)
-
-    table_rows = jnp.transpose(coupling_table, (2, 0, 1)).reshape(term_total * mode_total, mode_total)
-    accumulated = jnp.dot(
+    coefficients = coefficients.reshape(1, term_total, cell_count)
+    weighted = (stencil_rows[:, None, :] * coefficients).reshape(mode_total * term_total, cell_count)
+    table_rows = coupling_table.reshape(mode_total, mode_total * term_total)
+    mixed_rows = jnp.dot(
         table_rows,
-        stencil_rows,
-        precision=lax.Precision.HIGHEST,
+        weighted,
+        precision=lax.Precision.HIGH,
         preferred_element_type=jnp.float32,
-    ).reshape(term_total, mode_total, cell_count)
-    mixed_rows = jnp.sum(coefficients * accumulated, axis=0)
+    )
     mixed_rows = mixed_rows.reshape((mode_total, chunk) + lateral)
     mixed_field = lax.all_to_all(mixed_rows, "mode", 0, 1, tiled=True)
 

time: 112 us -> 122 us (1.089)
  local copies, waits for them, and re-layouts: 7.58 us -> 13.8 us
  other arithmetic: 5.86 us -> 10.3 us
    unnamed x21, local copies, waits for them, and re-layouts: 3.89 us -> 9.81 us
    unnamed x0 -> x1, other arithmetic: none -> 5.23 us
  transfers between devices with their start and end apart: 4 -> 4, of which waited for: 2 -> 2; matrix products, arithmetic and copies ran while one was open for 4% -> 3% of each run, Pallas kernels for 0% -> 0%
where the time goes in v4:
time: 122 us
  waiting for transfers between devices  38.6 us (32%)
  starting transfers between devices  25.1 us (21%)
  blocking collectives  20.9 us (17%)
  local copies, waits for them, and re-layouts  13.8 us (11%)
  other arithmetic  10.3 us (8%)
  matrix products  8.65 us (7%)
  Pallas kernels  3.97 us (3%)
    all_to_all x1, waiting for transfers between devices, local(): summaries = lax.all_to_all(copies, 'depth', 0, 0, tiled=True)  22.8 us
    all_to_all x1, blocking collectives, local(): mixed_field = lax.all_to_all(mixed_rows, 'mode', 0, 1, tiled=True)  20.9 us
    all_to_all x1, waiting for transfers between devices, local(): stencil_rows = lax.all_to_all(stencil, 'mode', 1, 0, tiled=True)  15.7 us
    all_to_all x1, starting transfers between devices, local(): summaries = lax.all_to_all(copies, 'depth', 0, 0, tiled=True)  11.6 us
    unnamed x21, local copies, waits for them, and re-layouts  9.81 us
    dot_general x1, matrix products, local(): jnp.dot(table_rows, weighted, precision=lax.Precision.HIGH, preferred_ele...  8.65 us
    ppermute x1, starting transfers between devices, with_halo(): lax.ppermute(tail, axis, [(i, (i + 1) % count) for i in range(ends)])  5.49 us
    unnamed x1, other arithmetic  5.23 us
  transfers between devices with their start and end apart: 4, of which 2 were waited for; matrix products, arithmetic and copies ran while one was open for 3% of the time, Pallas kernels for 0%

profile of v4, /device:TPU:1, one launch (start us, length us, event | category | flops | bytes accessed | tf_op | source)
XLA Modules:
  0.0 121.6 jit_solution(2862278860867360908)
XLA Ops:
  0.0 0.8 fusion.61
  0.8 3.3 %collective-permute-start = (f32[5,1,16,128]{3,2,0,1:T(8,128)S(1)}, f32[5,1,16,128]{3,2,0,1:T(8,128)S(1)}, u32[]{:S(2)}, u32[]{:S(2)}) collective-permute-start(f32[5,1,16,128]{3,2,0,1:T(8,128)S(1)} %get-tuple-element.45), channel_id=1, source_target_pairs={{1,0},{2,1},{3,2},{4,3},{5,4},{6,5},{7,6},{8,7},{9,8},{10,9},{11,1... | collective-permute-start | bytes 122888 | tf_op jit(solution)/shard_map/ppermute | solution.py:19
  4.1 5.5 %collective-permute-start.1 = (f32[5,1,16,128]{3,2,0,1:T(8,128)S(1)}, f32[5,1,16,128]{3,2,0,1:T(8,128)S(1)}, u32[]{:S(2)}, u32[]{:S(2)}) collective-permute-start(f32[5,1,16,128]{3,2,0,1:T(8,128)S(1)} %get-tuple-element.44), channel_id=1, source_target_pairs={{0,1},{1,2},{2,3},{3,4},{4,5},{5,6},{6,7},{7,8},{8,9},{9,10},{10,1... | collective-permute-start | bytes 122888 | tf_op jit(solution)/shard_map/ppermute | solution.py:17
  9.6 1.5 %copy.18 = f32[5,32,16,128]{3,2,0,1:T(8,128)S(1)} copy(f32[5,32,16,128]{3,2,1,0:T(8,128)} %param.7) | data formatting | bytes 2621440 | tf_op args[0]
  11.3 1.1 select_maximum_fusion
  12.5 2.2 %fusion.5 = f32[5,32,16,128]{3,2,0,1:T(8,128)} fusion(f32[5,34,18,130]{3,2,0,1:T(8,128)S(1)} %select_maximum_fusion, f32[5,32,16,128]{3,2,0,1:T(8,128)S(1)} %copy.18, f32[5,1,16,128]{3,2,0,1:T(8,128)S(1)} %collective-permute-done.1, f32[5,1,16,128]{3,2,0,1:T(8,128)S(1)} %collective-permute-done), kind=kLoop, calls=%fused_computation.17 | loop fusion | flops 2949120 | bytes 7946240 | tf_op jit(solution)/shard_map/sub | solution.py:32
  14.7 4.8 %all-to-all-start = ((f32[5,32,16,128]{3,2,0,1:T(8,128)}), f32[5,32,16,128]{3,2,0,1:T(8,128)S(1)}, u32[]{:S(2)}, u32[]{:S(2)}) async-start(f32[5,32,16,128]{3,2,0,1:T(8,128)} %fusion.5), calls=%async_computation | async-start | bytes 2621440 | tf_op jit(solution)/shard_map/all_to_all | solution.py:113
  19.7 0.4 copy-done.8
  20.2 0.3 copy-done.6
  20.5 0.6 gather_fusion
  21.4 0.6 gather_fusion.1
  22.0 15.7 %all-to-all-done = f32[5,32,16,128]{3,2,0,1:T(8,128)S(1)} async-done(((f32[5,32,16,128]{3,2,0,1:T(8,128)}), f32[5,32,16,128]{3,2,0,1:T(8,128)S(1)}, u32[]{:S(2)}, u32[]{:S(2)}) %all-to-all-start) | async-done | bytes 1310752 | tf_op jit(solution)/shard_map/all_to_all | solution.py:113
  37.9 0.2 mul.674
  38.1 5.2 %multiply_bitcast_fusion = f32[40,8,64,128]{3,1,2,0:T(8,128)} fusion(f32[8,8192]{1,0:T(8,128)S(1)} %bitcast.339, f32[40,8192]{1,0:T(8,128)S(1)} %mul.674), kind=kLoop, calls=%fused_computation.4 | loop fusion | flops 2621440 | bytes 12058624
  43.4 6.1 %copy.32 = f32[40,8,64,128]{3,2,1,0:T(8,128)S(1)} copy(f32[40,8,64,128]{3,1,2,0:T(8,128)} %multiply_bitcast_fusion) | data formatting | bytes 20971520
  49.5 8.6 %fusion = f32[40,4,16,128]{3,0,2,1:T(8,128)S(1)} fusion(f32[4,16,128,320]{2,1,0,3:T(8,128)S(1)} %bitcast.334, f32[40,40,8]{1,2,0:T(8,128)S(1)} %gather_fusion.1, pred[40]{0:T(512)(128)(4,1)S(1)} %compare_and_fusion), kind=kOutput, calls=%fused_computation.2 | convolution fusion | flops 629158400 | bytes 11847720 | tf_op jit(solution)/shard_map/dot_general | solution.py:123
  58.2 0.3 copy.27
  58.5 20.9 %all_to_all.38 = f32[40,4,16,128]{3,2,1,0:T(8,128)S(1)} all-to-all(f32[40,4,16,128]{3,2,1,0:T(8,128)S(1)} %copy.27), channel_id=1, replica_groups=mesh['mode'=8,'depth'=16] {'mode'}, dimensions={0} | all-to-all | bytes 2621440 | tf_op jit(solution)/shard_map/all_to_all | solution.py:130
  79.4 1.2 copy.28
  80.6 4.0 %shard_map.73 = (f32[5,32,16,128]{3,2,1,0:T(8,128)}, f32[32,16,128]{2,1,0:T(8,128)}, f32[32,16,128]{2,1,0:T(8,128)}, f32[16,12,16,128]{3,2,1,0:T(8,128)}) custom-call(f32[5,32,16,128]{3,2,1,0:T(8,128)} %bitcast.336, f32[32,16,128]{2,1,0:T(8,128)} %decay_ref.1), custom_call_target="tpu_custom_call" | custom-call | tf_op jit(solution)/shard_map/pallas_call | solution.py:89
  84.5 11.6 %all-to-all-start.2 = ((f32[16,12,16,128]{3,2,1,0:T(8,128)}), f32[16,12,16,128]{3,2,1,0:T(8,128)S(1)}, u32[]{:S(2)}, u32[]{:S(2)}) async-start(f32[16,12,16,128]{3,2,1,0:T(8,128)} %get-tuple-element.11), calls=%async_computation.2 | async-start | bytes 3145728 | tf_op jit(solution)/shard_map/all_to_all | solution.py:134
  96.1 22.8 %all-to-all-done.2 = f32[16,12,16,128]{3,2,1,0:T(8,128)S(1)} async-done(((f32[16,12,16,128]{3,2,1,0:T(8,128)}), f32[16,12,16,128]{3,2,1,0:T(8,128)S(1)}, u32[]{:S(2)}, u32[]{:S(2)}) %all-to-all-start.2) | async-done | bytes 1572896 | tf_op jit(solution)/shard_map/all_to_all | solution.py:134
  119.3 0.9 copy-done.2
  120.3 1.2 %multiply_add_fusion = f32[5,32,16,128]{3,2,1,0:T(8,128)} fusion(f32[5,32,16,128]{3,2,1,0:T(8,128)S(1)} %copy-done.2, f32[5,16,128]{2,1,0:T(8,128)S(1)} %fusion.42, f32[32,16,128]{2,1,0:T(8,128)S(1)} %copy-done.5, f32[5,16,128]{2,1,0:T(8,128)S(1)} %select_select_fusion, f32[32,16,128]{2,1,0:T(8,128)S(1)} %copy-done.4), kind=kLoop, calls=%fused_computation.25 | loop fusion | flops 1310720 | bytes 3227648 | tf_op jit(solution)/shard_map/add | solution.py:156
  (30 shorter events, 1.4 us)
Async XLA Ops:
  0.8 10.3 %collective-permute-start = (f32[5,1,16,128]{3,2,0,1:T(8,128)S(1)}, f32[5,1,16,128]{3,2,0,1:T(8,128)S(1)}, u32[]{:S(2)}, u32[]{:S(2)}) collective-permute-start(f32[5,1,16,128]{3,2,0,1:T(8,128)S(1)} %get-tuple-element.45), channel_id=1, source_target_pairs={{1,0},{2,1},{3,2},{4,3},{5,4},{6,5},{7,6},{8,7},{9,8},{10,9},{11,1... | collective-permute-start | bytes 122888 | tf_op jit(solution)/shard_map/ppermute | solution.py:19
  4.1 7.0 %collective-permute-start.1 = (f32[5,1,16,128]{3,2,0,1:T(8,128)S(1)}, f32[5,1,16,128]{3,2,0,1:T(8,128)S(1)}, u32[]{:S(2)}, u32[]{:S(2)}) collective-permute-start(f32[5,1,16,128]{3,2,0,1:T(8,128)S(1)} %get-tuple-element.44), channel_id=1, source_target_pairs={{0,1},{1,2},{2,3},{3,4},{4,5},{5,6},{6,7},{7,8},{8,9},{9,10},{10,1... | collective-permute-start | bytes 122888 | tf_op jit(solution)/shard_map/ppermute | solution.py:17
  9.6 1.7 %copy-start = (f32[5,32,16,128]{3,2,1,0:T(8,128)S(1)}, f32[5,32,16,128]{3,2,1,0:T(8,128)}, u32[]{:S(2)}) copy-start(f32[5,32,16,128]{3,2,1,0:T(8,128)} %param.7) | copy-start | bytes 3932164
  14.7 4.8 %copy-start.1 = (f32[7,32,16,128]{3,2,1,0:T(8,128)S(1)}, f32[7,32,16,128]{3,2,1,0:T(8,128)}, u32[]{:S(2)}) copy-start(f32[7,32,16,128]{3,2,1,0:T(8,128)} %param.9) | copy-start | bytes 5505028
  14.7 4.8 %copy-start.3 = (f32[32,16,128]{2,1,0:T(8,128)S(1)}, f32[32,16,128]{2,1,0:T(8,128)}, u32[]{:S(2)}) copy-start(f32[32,16,128]{2,1,0:T(8,128)} %param.8) | copy-start | bytes 786436
  14.7 23.0 %all-to-all-start = ((f32[5,32,16,128]{3,2,0,1:T(8,128)}), f32[5,32,16,128]{3,2,0,1:T(8,128)S(1)}, u32[]{:S(2)}, u32[]{:S(2)}) async-start(f32[5,32,16,128]{3,2,0,1:T(8,128)} %fusion.5), calls=%async_computation | async-start | bytes 2621440 | tf_op jit(solution)/shard_map/all_to_all | solution.py:113
  19.5 0.7 copy-start.8
  19.5 0.9 copy-start.6
  19.5 1.0 copy-start.7
  84.5 34.4 %all-to-all-start.2 = ((f32[16,12,16,128]{3,2,1,0:T(8,128)}), f32[16,12,16,128]{3,2,1,0:T(8,128)S(1)}, u32[]{:S(2)}, u32[]{:S(2)}) async-start(f32[16,12,16,128]{3,2,1,0:T(8,128)} %get-tuple-element.11), calls=%async_computation.2 | async-start | bytes 3145728 | tf_op jit(solution)/shard_map/all_to_all | solution.py:134
  118.9 1.3 %copy-start.2 = (f32[5,32,16,128]{3,2,1,0:T(8,128)S(1)}, f32[5,32,16,128]{3,2,1,0:T(8,128)}, u32[]{:S(2)}) copy-start(f32[5,32,16,128]{3,2,1,0:T(8,128)} %get-tuple-element.9) | copy-start | bytes 3932164
  118.9 1.3 %copy-start.4 = (f32[32,16,128]{2,1,0:T(8,128)S(1)}, f32[32,16,128]{2,1,0:T(8,128)}, u32[]{:S(2)}) copy-start(f32[32,16,128]{2,1,0:T(8,128)} %get-tuple-element.10) | copy-start | bytes 786436
  118.9 1.4 %copy-start.5 = (f32[32,16,128]{2,1,0:T(8,128)S(1)}, f32[32,16,128]{2,1,0:T(8,128)}, u32[]{:S(2)}) copy-start(f32[32,16,128]{2,1,0:T(8,128)} %get-tuple-element.12) | copy-start | bytes 786436

commit v5 on v3

--- a/solution.py
+++ b/solution.py
@@ -123,7 +123,7 @@
     accumulated = jnp.dot(
         table_rows,
         stencil_rows,
-        precision=lax.Precision.HIGHEST,
+        precision=lax.Precision.HIGH,
         preferred_element_type=jnp.float32,
     ).reshape(term_total, mode_total, cell_count)
     mixed_rows = jnp.sum(coefficients * accumulated, axis=0)

time: 112 us -> 108 us (0.964)
  matrix products: 8.97 us -> 4.91 us
    dot_general x1, matrix products: 8.97 us -> 4.91 us  [local(): jnp.dot(table_rows, stencil_rows, precision=lax.Precision.HIGH, preferred...]
where the time goes in v5:
time: 108 us; the launch traced here: 107 us
  waiting for transfers between devices  38.5 us (36%)
  starting transfers between devices  25.2 us (23%)
  blocking collectives  20.9 us (19%)
  local copies, waits for them, and re-layouts  7.58 us (7%)
  other arithmetic  5.86 us (5%)
  matrix products  4.91 us (5%)
  Pallas kernels  3.98 us (4%)
    all_to_all x1, waiting for transfers between devices, local(): summaries = lax.all_to_all(copies, 'depth', 0, 0, tiled=True)  22.8 us
    all_to_all x1, blocking collectives, local(): mixed_field = lax.all_to_all(mixed_rows, 'mode', 0, 1, tiled=True)  20.9 us
    all_to_all x1, waiting for transfers between devices, local(): stencil_rows = lax.all_to_all(stencil, 'mode', 1, 0, tiled=True)  15.6 us
    all_to_all x1, starting transfers between devices, local(): summaries = lax.all_to_all(copies, 'depth', 0, 0, tiled=True)  11.6 us
    ppermute x1, starting transfers between devices, with_halo(): lax.ppermute(tail, axis, [(i, (i + 1) % count) for i in range(ends)])  5.49 us
    dot_general x1, matrix products, local(): jnp.dot(table_rows, stencil_rows, precision=lax.Precision.HIGH, preferred...  4.91 us
    all_to_all x1, starting transfers between devices, local(): stencil_rows = lax.all_to_all(stencil, 'mode', 1, 0, tiled=True)  4.78 us
    pallas_call x1, Pallas kernels, local_sweeps(): pl.pallas_call(sweep_kernel, out_shape=(jax.ShapeDtypeStruct(mixed.shape,...  3.98 us
  transfers between devices with their start and end apart: 4, of which 2 were waited for; matrix products, arithmetic and copies ran while one was open for 4% of the time, Pallas kernels for 0%

profile of v5, /device:TPU:1, one launch (start us, length us, event | category | flops | bytes accessed | tf_op | source)
XLA Modules:
  0.0 107.2 jit_solution(15472082268378375122)
XLA Ops:
  0.0 0.8 fusion.56
  0.8 3.3 %collective-permute-start = (f32[5,1,16,128]{3,2,0,1:T(8,128)S(1)}, f32[5,1,16,128]{3,2,0,1:T(8,128)S(1)}, u32[]{:S(2)}, u32[]{:S(2)}) collective-permute-start(f32[5,1,16,128]{3,2,0,1:T(8,128)S(1)} %get-tuple-element.45), channel_id=1, source_target_pairs={{1,0},{2,1},{3,2},{4,3},{5,4},{6,5},{7,6},{8,7},{9,8},{10,9},{11,1... | collective-permute-start | bytes 122888 | tf_op jit(solution)/shard_map/ppermute | solution.py:19
  4.1 5.5 %collective-permute-start.1 = (f32[5,1,16,128]{3,2,0,1:T(8,128)S(1)}, f32[5,1,16,128]{3,2,0,1:T(8,128)S(1)}, u32[]{:S(2)}, u32[]{:S(2)}) collective-permute-start(f32[5,1,16,128]{3,2,0,1:T(8,128)S(1)} %get-tuple-element.44), channel_id=1, source_target_pairs={{0,1},{1,2},{2,3},{3,4},{4,5},{5,6},{6,7},{7,8},{8,9},{9,10},{10,1... | collective-permute-start | bytes 122888 | tf_op jit(solution)/shard_map/ppermute | solution.py:17
  9.6 0.7 compare_select_fusion
  10.3 1.5 %copy.17 = f32[5,32,16,128]{3,2,0,1:T(8,128)S(1)} copy(f32[5,32,16,128]{3,2,1,0:T(8,128)} %param.7) | data formatting | bytes 2621440 | tf_op args[0]
  11.8 0.2 copy-done
  12.0 1.1 %select_maximum_fusion = f32[5,34,18,130]{3,2,0,1:T(8,128)S(1)} fusion(f32[5,1,16,128]{3,2,0,1:T(8,128)S(1)} %collective-permute-done, f32[5,1,16,128]{3,2,0,1:T(8,128)S(1)} %collective-permute-done.1, f32[5,32,16,128]{3,2,1,0:T(8,128)S(1)} %copy-done), kind=kLoop, calls=%fused_computation.7 | loop fusion | flops 5967000 | bytes 2983840 | tf_op jit(solution)/shard_map/concatenate | solution.py:15
  13.2 2.2 %fusion.4 = f32[5,32,16,128]{3,2,0,1:T(8,128)} fusion(f32[5,34,18,130]{3,2,0,1:T(8,128)S(1)} %select_maximum_fusion, f32[5,32,16,128]{3,2,0,1:T(8,128)S(1)} %copy.17, f32[5,1,16,128]{3,2,0,1:T(8,128)S(1)} %collective-permute-done.1, f32[5,1,16,128]{3,2,0,1:T(8,128)S(1)} %collective-permute-done), kind=kLoop, calls=%fused_computation.16 | loop fusion | flops 2949120 | bytes 7946240 | tf_op jit(solution)/shard_map/sub | solution.py:32
  15.3 4.8 %all-to-all-start = ((f32[5,32,16,128]{3,2,0,1:T(8,128)}), f32[5,32,16,128]{3,2,0,1:T(8,128)S(1)}, u32[]{:S(2)}, u32[]{:S(2)}) async-start(f32[5,32,16,128]{3,2,0,1:T(8,128)} %fusion.4), calls=%async_computation | async-start | bytes 2621440 | tf_op jit(solution)/shard_map/all_to_all | solution.py:113
  20.4 0.7 copy-done.6
  21.2 0.6 gather_fusion
  22.0 0.6 gather_fusion.1
  22.8 15.6 %all-to-all-done = f32[5,32,16,128]{3,2,0,1:T(8,128)S(1)} async-done(((f32[5,32,16,128]{3,2,0,1:T(8,128)}), f32[5,32,16,128]{3,2,0,1:T(8,128)S(1)}, u32[]{:S(2)}, u32[]{:S(2)}) %all-to-all-start) | async-done | bytes 1310752 | tf_op jit(solution)/shard_map/all_to_all | solution.py:113
  38.6 0.2 reshape.389
  38.8 4.9 %fusion.3 = f32[40,8192]{1,0:T(8,128)S(1)} fusion(f32[40,8192,1]{1,0,2:T(8,128)S(1)} %reshape.389, f32[8,8192]{1,0:T(8,128)S(1)} %bitcast.332, f32[8,40,40]{1,0,2:T(8,128)S(1)} %select_bitcast_fusion), kind=kOutput, calls=%fused_computation.12 | convolution fusion | flops 634060800 | bytes 2934784 | tf_op jit(solution)/shard_map/dot_general | solution.py:123
  43.7 0.2 copy.27
  44.0 20.9 %all_to_all.38 = f32[40,4,16,128]{3,2,1,0:T(8,128)S(1)} all-to-all(f32[40,4,16,128]{3,2,1,0:T(8,128)S(1)} %bitcast.327), channel_id=1, replica_groups=mesh['mode'=8,'depth'=16] {'mode'}, dimensions={0} | all-to-all | bytes 2621440 | tf_op jit(solution)/shard_map/all_to_all | solution.py:131
  64.9 1.2 %copy.25 = f32[5,8,4,16,128]{4,3,2,1,0:T(8,128)} copy(f32[5,8,4,16,128]{4,3,2,0,1:T(8,128)S(1)} %bitcast.328) | data formatting | bytes 2621440 | tf_op jit(solution)/shard_map/all_to_all | solution.py:131
  66.1 4.0 %shard_map.73 = (f32[5,32,16,128]{3,2,1,0:T(8,128)}, f32[32,16,128]{2,1,0:T(8,128)}, f32[32,16,128]{2,1,0:T(8,128)}, f32[16,12,16,128]{3,2,1,0:T(8,128)}) custom-call(f32[5,32,16,128]{3,2,1,0:T(8,128)} %bitcast.325, f32[32,16,128]{2,1,0:T(8,128)} %decay_ref.1), custom_call_target="tpu_custom_call" | custom-call | tf_op jit(solution)/shard_map/pallas_call | solution.py:89
  70.0 11.6 %all-to-all-start.2 = ((f32[16,12,16,128]{3,2,1,0:T(8,128)}), f32[16,12,16,128]{3,2,1,0:T(8,128)S(1)}, u32[]{:S(2)}, u32[]{:S(2)}) async-start(f32[16,12,16,128]{3,2,1,0:T(8,128)} %get-tuple-element.11), calls=%async_computation.2 | async-start | bytes 3145728 | tf_op jit(solution)/shard_map/all_to_all | solution.py:135
  81.7 22.8 %all-to-all-done.2 = f32[16,12,16,128]{3,2,1,0:T(8,128)S(1)} async-done(((f32[16,12,16,128]{3,2,1,0:T(8,128)}), f32[16,12,16,128]{3,2,1,0:T(8,128)S(1)}, u32[]{:S(2)}, u32[]{:S(2)}) %all-to-all-start.2) | async-done | bytes 1572896 | tf_op jit(solution)/shard_map/all_to_all | solution.py:135
  104.7 0.2 fusion.38
  104.9 0.9 copy-done.2
  105.9 1.2 %multiply_add_fusion = f32[5,32,16,128]{3,2,1,0:T(8,128)} fusion(f32[5,32,16,128]{3,2,1,0:T(8,128)S(1)} %copy-done.2, f32[5,16,128]{2,1,0:T(8,128)S(1)} %fusion.38, f32[32,16,128]{2,1,0:T(8,128)S(1)} %copy-done.5, f32[5,16,128]{2,1,0:T(8,128)S(1)} %select_select_fusion, f32[32,16,128]{2,1,0:T(8,128)S(1)} %copy-done.4), kind=kLoop, calls=%fused_computation.24 | loop fusion | flops 1310720 | bytes 3227648 | tf_op jit(solution)/shard_map/add | solution.py:157
  (29 shorter events, 1.1 us)
Async XLA Ops:
  0.8 11.0 %collective-permute-start = (f32[5,1,16,128]{3,2,0,1:T(8,128)S(1)}, f32[5,1,16,128]{3,2,0,1:T(8,128)S(1)}, u32[]{:S(2)}, u32[]{:S(2)}) collective-permute-start(f32[5,1,16,128]{3,2,0,1:T(8,128)S(1)} %get-tuple-element.45), channel_id=1, source_target_pairs={{1,0},{2,1},{3,2},{4,3},{5,4},{6,5},{7,6},{8,7},{9,8},{10,9},{11,1... | collective-permute-start | bytes 122888 | tf_op jit(solution)/shard_map/ppermute | solution.py:19
  4.1 7.7 %collective-permute-start.1 = (f32[5,1,16,128]{3,2,0,1:T(8,128)S(1)}, f32[5,1,16,128]{3,2,0,1:T(8,128)S(1)}, u32[]{:S(2)}, u32[]{:S(2)}) collective-permute-start(f32[5,1,16,128]{3,2,0,1:T(8,128)S(1)} %get-tuple-element.44), channel_id=1, source_target_pairs={{0,1},{1,2},{2,3},{3,4},{4,5},{5,6},{6,7},{7,8},{8,9},{9,10},{10,1... | collective-permute-start | bytes 122888 | tf_op jit(solution)/shard_map/ppermute | solution.py:17
  10.3 1.7 %copy-start = (f32[5,32,16,128]{3,2,1,0:T(8,128)S(1)}, f32[5,32,16,128]{3,2,1,0:T(8,128)}, u32[]{:S(2)}) copy-start(f32[5,32,16,128]{3,2,1,0:T(8,128)} %param.7) | copy-start | bytes 3932164
  15.3 4.8 %copy-start.1 = (f32[7,32,16,128]{3,2,1,0:T(8,128)S(1)}, f32[7,32,16,128]{3,2,1,0:T(8,128)}, u32[]{:S(2)}) copy-start(f32[7,32,16,128]{3,2,1,0:T(8,128)} %param.9) | copy-start | bytes 5505028
  15.3 4.8 %copy-start.3 = (f32[32,16,128]{2,1,0:T(8,128)S(1)}, f32[32,16,128]{2,1,0:T(8,128)}, u32[]{:S(2)}) copy-start(f32[32,16,128]{2,1,0:T(8,128)} %param.8) | copy-start | bytes 786436
  15.3 23.0 %all-to-all-start = ((f32[5,32,16,128]{3,2,0,1:T(8,128)}), f32[5,32,16,128]{3,2,0,1:T(8,128)S(1)}, u32[]{:S(2)}, u32[]{:S(2)}) async-start(f32[5,32,16,128]{3,2,0,1:T(8,128)} %fusion.4), calls=%async_computation | async-start | bytes 2621440 | tf_op jit(solution)/shard_map/all_to_all | solution.py:113
  20.1 0.9 copy-start.6
  20.1 1.0 copy-start.7
  20.2 1.6 %copy-start.8 = (s32[40]{0:T(128)S(1)}, s32[40]{0:T(128)}, u32[]{:S(2)}) copy-start(s32[40]{0:T(128)} %param.13) | copy-start | bytes 484
  70.0 34.5 %all-to-all-start.2 = ((f32[16,12,16,128]{3,2,1,0:T(8,128)}), f32[16,12,16,128]{3,2,1,0:T(8,128)S(1)}, u32[]{:S(2)}, u32[]{:S(2)}) async-start(f32[16,12,16,128]{3,2,1,0:T(8,128)} %get-tuple-element.11), calls=%async_computation.2 | async-start | bytes 3145728 | tf_op jit(solution)/shard_map/all_to_all | solution.py:135
  104.5 1.3 %copy-start.2 = (f32[5,32,16,128]{3,2,1,0:T(8,128)S(1)}, f32[5,32,16,128]{3,2,1,0:T(8,128)}, u32[]{:S(2)}) copy-start(f32[5,32,16,128]{3,2,1,0:T(8,128)} %get-tuple-element.9) | copy-start | bytes 3932164
  104.5 1.3 %copy-start.4 = (f32[32,16,128]{2,1,0:T(8,128)S(1)}, f32[32,16,128]{2,1,0:T(8,128)}, u32[]{:S(2)}) copy-start(f32[32,16,128]{2,1,0:T(8,128)} %get-tuple-element.10) | copy-start | bytes 786436
  104.5 1.4 %copy-start.5 = (f32[32,16,128]{2,1,0:T(8,128)S(1)}, f32[32,16,128]{2,1,0:T(8,128)}, u32[]{:S(2)}) copy-start(f32[32,16,128]{2,1,0:T(8,128)} %get-tuple-element.12) | copy-start | bytes 786436

commit v6 on v5

--- a/solution.py
+++ b/solution.py
@@ -6,30 +6,40 @@
 from jax.sharding import PartitionSpec as P
 
 
-def with_halo(cells, sides, width):
-    for axis, dim in sides:
-        count = lax.axis_size(axis)
-        ends = count - 1
-        head = lax.slice_in_dim(cells, 0, width, axis=dim)
-        tail = lax.slice_in_dim(cells, cells.shape[dim] - width, cells.shape[dim], axis=dim)
-        cells = jnp.concatenate(
-            [
-                lax.ppermute(tail, axis, [(i, (i + 1) % count) for i in range(ends)]),
-                cells,
-                lax.ppermute(head, axis, [((i + 1) % count, i) for i in range(ends)]),
-            ],
-            axis=dim,
-        )
-    return cells
+def neighbour_sum(x, axis):
+    size = x.shape[axis]
+    where_from = lax.broadcasted_iota(jnp.int32, x.shape, axis)
+    total = jnp.zeros_like(x)
+    for shift in (1, size - 1):
+        rolled = pltpu.roll(x, shift, axis)
+        source = pltpu.roll(where_from, shift, axis)
+        inside = jnp.abs(source - where_from) == 1
+        total = total + jnp.where(inside, rolled, 0.0)
+    return total
 
 
-def laplace(padded):
-    lateral = jnp.pad(padded, ((0, 0), (0, 0), (1, 1), (1, 1)))
-    centre = lateral[:, 1:-1, 1:-1, 1:-1]
-    beside = lateral[:, 2:, 1:-1, 1:-1] + lateral[:, :-2, 1:-1, 1:-1]
-    beside = beside + lateral[:, 1:-1, 2:, 1:-1] + lateral[:, 1:-1, :-2, 1:-1]
-    beside = beside + lateral[:, 1:-1, 1:-1, 2:] + lateral[:, 1:-1, 1:-1, :-2]
-    return 6.0 * centre - beside
+def stencil_kernel(fields_ref, out_ref):
+    rows = fields_ref.shape[1]
+
+    def one_row(z, carried):
+        centre = fields_ref[:, z]
+        above = fields_ref[:, jnp.minimum(z + 1, rows - 1)]
+        below = fields_ref[:, jnp.maximum(z - 1, 0)]
+        beside = jnp.where(z + 1 < rows, above, 0.0) + jnp.where(z > 0, below, 0.0)
+        beside = beside + neighbour_sum(centre, 1)
+        beside = beside + neighbour_sum(centre, 2)
+        out_ref[z] = 6.0 * centre - beside
+        return carried
+
+    lax.fori_loop(0, rows, one_row, 0)
+
+
+def slab_stencil(fields):
+    modes, rows = fields.shape[0], fields.shape[1]
+    return pl.pallas_call(
+        stencil_kernel,
+        out_shape=jax.ShapeDtypeStruct((rows, modes) + fields.shape[2:], jnp.float32),
+    )(fields)
 
 
 def sweep_kernel(mixed_ref, decay_ref, back_ref, coupled_ref, tail_ref, summary_ref):
@@ -108,8 +118,12 @@
     coupling_table = jnp.take(jnp.take(masked, mode_order, axis=0), mode_order, axis=1)
     term_total = coupling_table.shape[2]
 
-    padded = with_halo(fields, (("depth", 1),), 1)
-    stencil = laplace(padded)
+    slabs = lax.axis_size("depth")
+    from_below = lax.ppermute(fields[:, -1], "depth", [(i, i + 1) for i in range(slabs - 1)])
+    from_above = lax.ppermute(fields[:, 0], "depth", [(i + 1, i) for i in range(slabs - 1)])
+    stencil = slab_stencil(fields)
+    stencil = stencil.at[0].add(-from_below).at[-1].add(-from_above)
+    stencil = jnp.transpose(stencil, (1, 0, 2, 3))
     stencil_rows = lax.all_to_all(stencil, "mode", 1, 0, tiled=True)
     cell_count = chunk * lateral[0] * lateral[1]
     stencil_rows = stencil_rows.reshape(mode_total, cell_count)
@@ -130,7 +144,6 @@
     mixed_rows = mixed_rows.reshape((mode_total, chunk) + lateral)
     mixed_field = lax.all_to_all(mixed_rows, "mode", 0, 1, tiled=True)
 
-    slabs = lax.axis_size("depth")
     back, coupled, tail, copies = local_sweeps(mixed_field, decay, slabs)
     summaries = lax.all_to_all(copies, "depth", 0, 0, tiled=True)
     ratio_all = summaries[:, 0]

time: 108 us -> 105 us (0.972)
  Pallas kernels: 3.98 us -> 9.37 us
  starting transfers between devices: 25.2 us -> 21.9 us
  waiting for transfers between devices: 38.5 us -> 36.6 us
  local copies, waits for them, and re-layouts: 7.58 us -> 5.9 us
    pallas_call x0 -> x1, Pallas kernels: none -> 5.4 us  [slab_stencil(): pl.pallas_call(stencil_kernel, out_shape=jax.ShapeDtypeStruct((rows, mode...]
    all_to_all x1, starting transfers between devices: 11.6 us -> 8.34 us  [local(): summaries = lax.all_to_all(copies, 'depth', 0, 0, tiled=True)]
    scatter-add x0 -> x2, other arithmetic: none -> 2.81 us  [local(): stencil = stencil.at[0].add(-from_below).at[-1].add(-from_above)]
    sub x1 -> x0, other arithmetic: 2.19 us -> none  [laplace(): return 6.0 * centre - beside]
    all_to_all x1, waiting for transfers between devices: 15.6 us -> 13.7 us  [local(): stencil_rows = lax.all_to_all(stencil, 'mode', 1, 0, tiled=True)]
    unnamed x21 -> x18, local copies, waits for them, and re-layouts: 3.89 us -> 2.21 us
    concatenate x1 -> x0, other arithmetic: 1.15 us -> none  [with_halo(): jnp.concatenate([lax.ppermute(tail, axis, [(i, (i + 1) % count) for i in...]
  transfers between devices with their start and end apart: 4 -> 4, of which waited for: 2 -> 2; matrix products, arithmetic and copies ran while one was open for 4% -> 4% of each run, Pallas kernels for 0% -> 5%
where the time goes in v6:
time: 105 us
  waiting for transfers between devices  36.6 us (35%)
  starting transfers between devices  21.9 us (21%)
  blocking collectives  20.6 us (20%)
  Pallas kernels  9.37 us (9%)
  local copies, waits for them, and re-layouts  5.9 us (6%)
  other arithmetic  5.33 us (5%)
  matrix products  4.91 us (5%)
    all_to_all x1, waiting for transfers between devices, local(): summaries = lax.all_to_all(copies, 'depth', 0, 0, tiled=True)  22.8 us
    all_to_all x1, blocking collectives, local(): mixed_field = lax.all_to_all(mixed_rows, 'mode', 0, 1, tiled=True)  20.6 us
    all_to_all x1, waiting for transfers between devices, local(): stencil_rows = lax.all_to_all(stencil, 'mode', 1, 0, tiled=True)  13.7 us
    all_to_all x1, starting transfers between devices, local(): summaries = lax.all_to_all(copies, 'depth', 0, 0, tiled=True)  8.34 us
    ppermute x1, starting transfers between devices, local(): lax.ppermute(fields[:, -1], 'depth', [(i, i + 1) for i in range(slabs - 1)])  6.88 us
    pallas_call x1, Pallas kernels, slab_stencil(): pl.pallas_call(stencil_kernel, out_shape=jax.ShapeDtypeStruct((rows, mode...  5.4 us
    dot_general x1, matrix products, local(): jnp.dot(table_rows, stencil_rows, precision=lax.Precision.HIGH, preferred...  4.91 us
    all_to_all x1, starting transfers between devices, local(): stencil_rows = lax.all_to_all(stencil, 'mode', 1, 0, tiled=True)  4.78 us
  transfers between devices with their start and end apart: 4, of which 2 were waited for; matrix products, arithmetic and copies ran while one was open for 4% of the time, Pallas kernels for 5%

profile of v6, /device:TPU:1, one launch (start us, length us, event | category | flops | bytes accessed | tf_op | source)
XLA Modules:
  0.0 104.8 jit_solution(1213452777823061609)
XLA Ops:
  0.0 0.8 slice_bitcast_fusion.30
  0.8 6.9 %collective-permute-start = (f32[5,16,128]{2,1,0:T(8,128)S(1)}, f32[5,16,128]{2,1,0:T(8,128)S(1)}, u32[]{:S(2)}, u32[]{:S(2)}) collective-permute-start(f32[5,16,128]{2,1,0:T(8,128)S(1)} %get-tuple-element.69), channel_id=1, source_target_pairs={{0,1},{1,2},{2,3},{3,4},{4,5},{5,6},{6,7},{7,8},{8,9},{9,10},{10,1... | collective-permute-start | bytes 122888 | tf_op jit(solution)/shard_map/ppermute | solution.py:122
  7.7 1.9 %collective-permute-start.1 = (f32[5,16,128]{2,1,0:T(8,128)S(1)}, f32[5,16,128]{2,1,0:T(8,128)S(1)}, u32[]{:S(2)}, u32[]{:S(2)}) collective-permute-start(f32[5,16,128]{2,1,0:T(8,128)S(1)} %get-tuple-element.68), channel_id=1, source_target_pairs={{1,0},{2,1},{3,2},{4,3},{5,4},{6,5},{7,6},{8,7},{9,8},{10,9},{11,1... | collective-permute-start | bytes 122888 | tf_op jit(solution)/shard_map/ppermute | solution.py:123
  9.6 0.7 compare_select_fusion
  10.3 5.4 %shard_map.73 = f32[32,5,16,128]{3,2,1,0:T(8,128)} custom-call(f32[5,32,16,128]{3,2,1,0:T(8,128)} %fields_ref.1), custom_call_target="tpu_custom_call" | custom-call | tf_op jit(solution)/shard_map/pallas_call | solution.py:39
  15.7 1.4 %fusion.50 = f32[32,5,16,128]{3,2,1,0:T(8,128)} fusion(f32[32,5,16,128]{3,2,1,0:T(8,128)} %shard_map.73, f32[5,16,128]{2,1,0:T(8,128)S(1)} %collective-permute-done), kind=kLoop, calls=%fused_computation.92 | loop fusion | flops 20480 | bytes 122880 | tf_op jit(solution)/shard_map/scatter-add | solution.py:125
  17.1 1.4 %fusion.49 = f32[32,5,16,128]{3,2,1,0:T(8,128)} fusion(f32[32,5,16,128]{3,2,1,0:T(8,128)} %fusion.50, f32[5,16,128]{2,1,0:T(8,128)S(1)} %collective-permute-done.1), kind=kLoop, calls=%fused_computation.90 | loop fusion | flops 20480 | bytes 122880 | tf_op jit(solution)/shard_map/scatter-add | solution.py:125
  18.5 4.8 %all-to-all-start = ((f32[5,32,16,128]{3,2,0,1:T(8,128)}), f32[5,32,16,128]{3,2,0,1:T(8,128)S(1)}, u32[]{:S(2)}, u32[]{:S(2)}) async-start(f32[5,32,16,128]{3,2,0,1:T(8,128)} %bitcast.336), calls=%async_computation | async-start | bytes 2621440 | tf_op jit(solution)/shard_map/all_to_all | solution.py:127
  23.4 0.2 copy.27
  23.5 0.7 copy-done.5
  24.3 0.6 gather_fusion
  25.2 0.6 gather_fusion.1
  25.9 13.7 %all-to-all-done = f32[5,32,16,128]{3,2,0,1:T(8,128)S(1)} async-done(((f32[5,32,16,128]{3,2,0,1:T(8,128)}), f32[5,32,16,128]{3,2,0,1:T(8,128)S(1)}, u32[]{:S(2)}, u32[]{:S(2)}) %all-to-all-start) | async-done | bytes 1310752 | tf_op jit(solution)/shard_map/all_to_all | solution.py:127
  39.8 0.2 reshape.463
  40.1 4.9 %fusion = f32[40,8192]{1,0:T(8,128)S(1)} fusion(f32[40,8192,1]{1,0,2:T(8,128)S(1)} %reshape.463, f32[8,8192]{1,0:T(8,128)S(1)} %bitcast.344, f32[8,40,40]{1,0,2:T(8,128)S(1)} %select_bitcast_fusion), kind=kOutput, calls=%fused_computation.3 | convolution fusion | flops 634060800 | bytes 2934784 | tf_op jit(solution)/shard_map/dot_general | solution.py:137
  45.0 0.2 copy.23
  45.2 20.6 %all_to_all.38 = f32[40,4,16,128]{3,2,1,0:T(8,128)S(1)} all-to-all(f32[40,4,16,128]{3,2,1,0:T(8,128)S(1)} %bitcast.339), channel_id=1, replica_groups=mesh['mode'=8,'depth'=16] {'mode'}, dimensions={0} | all-to-all | bytes 2621440 | tf_op jit(solution)/shard_map/all_to_all | solution.py:145
  65.8 1.2 %copy.19 = f32[5,8,4,16,128]{4,3,2,1,0:T(8,128)} copy(f32[5,8,4,16,128]{4,3,2,0,1:T(8,128)S(1)} %bitcast.340) | data formatting | bytes 2621440 | tf_op jit(solution)/shard_map/all_to_all | solution.py:145
  66.9 4.0 %shard_map.74 = (f32[5,32,16,128]{3,2,1,0:T(8,128)}, f32[32,16,128]{2,1,0:T(8,128)}, f32[32,16,128]{2,1,0:T(8,128)}, f32[16,12,16,128]{3,2,1,0:T(8,128)}) custom-call(f32[5,32,16,128]{3,2,1,0:T(8,128)} %bitcast.338, f32[32,16,128]{2,1,0:T(8,128)} %decay_ref.1), custom_call_target="tpu_custom_call" | custom-call | tf_op jit(solution)/shard_map/pallas_call | solution.py:99
  70.9 8.3 %all-to-all-start.2 = ((f32[16,12,16,128]{3,2,1,0:T(8,128)}), f32[16,12,16,128]{3,2,1,0:T(8,128)S(1)}, u32[]{:S(2)}, u32[]{:S(2)}) async-start(f32[16,12,16,128]{3,2,1,0:T(8,128)} %get-tuple-element.35), calls=%async_computation.2 | async-start | bytes 3145728 | tf_op jit(solution)/shard_map/all_to_all | solution.py:148
  79.3 22.8 %all-to-all-done.2 = f32[16,12,16,128]{3,2,1,0:T(8,128)S(1)} async-done(((f32[16,12,16,128]{3,2,1,0:T(8,128)}), f32[16,12,16,128]{3,2,1,0:T(8,128)S(1)}, u32[]{:S(2)}, u32[]{:S(2)}) %all-to-all-start.2) | async-done | bytes 1572896 | tf_op jit(solution)/shard_map/all_to_all | solution.py:148
  102.3 0.2 fusion.33
  102.5 0.9 copy-done.1
  103.5 1.2 %multiply_add_fusion = f32[5,32,16,128]{3,2,1,0:T(8,128)} fusion(f32[5,32,16,128]{3,2,1,0:T(8,128)S(1)} %copy-done.1, f32[5,16,128]{2,1,0:T(8,128)S(1)} %fusion.33, f32[32,16,128]{2,1,0:T(8,128)S(1)} %copy-done.4, f32[5,16,128]{2,1,0:T(8,128)S(1)} %select_select_fusion, f32[32,16,128]{2,1,0:T(8,128)S(1)} %copy-done.3), kind=kLoop, calls=%fused_computation.6 | loop fusion | flops 1310720 | bytes 3227648 | tf_op jit(solution)/shard_map/add | solution.py:170
  (27 shorter events, 0.9 us)
Async XLA Ops:
  0.8 14.9 %collective-permute-start = (f32[5,16,128]{2,1,0:T(8,128)S(1)}, f32[5,16,128]{2,1,0:T(8,128)S(1)}, u32[]{:S(2)}, u32[]{:S(2)}) collective-permute-start(f32[5,16,128]{2,1,0:T(8,128)S(1)} %get-tuple-element.69), channel_id=1, source_target_pairs={{0,1},{1,2},{2,3},{3,4},{4,5},{5,6},{6,7},{7,8},{8,9},{9,10},{10,1... | collective-permute-start | bytes 122888 | tf_op jit(solution)/shard_map/ppermute | solution.py:122
  7.7 9.4 %collective-permute-start.1 = (f32[5,16,128]{2,1,0:T(8,128)S(1)}, f32[5,16,128]{2,1,0:T(8,128)S(1)}, u32[]{:S(2)}, u32[]{:S(2)}) collective-permute-start(f32[5,16,128]{2,1,0:T(8,128)S(1)} %get-tuple-element.68), channel_id=1, source_target_pairs={{1,0},{2,1},{3,2},{4,3},{5,4},{6,5},{7,6},{8,7},{9,8},{10,9},{11,1... | collective-permute-start | bytes 122888 | tf_op jit(solution)/shard_map/ppermute | solution.py:123
  18.5 4.8 %copy-start = (f32[7,32,16,128]{3,2,1,0:T(8,128)S(1)}, f32[7,32,16,128]{3,2,1,0:T(8,128)}, u32[]{:S(2)}) copy-start(f32[7,32,16,128]{3,2,1,0:T(8,128)} %param.13) | copy-start | bytes 5505028
  18.5 4.8 %copy-start.2 = (f32[32,16,128]{2,1,0:T(8,128)S(1)}, f32[32,16,128]{2,1,0:T(8,128)}, u32[]{:S(2)}) copy-start(f32[32,16,128]{2,1,0:T(8,128)} %param.12) | copy-start | bytes 786436
  18.5 21.1 %all-to-all-start = ((f32[5,32,16,128]{3,2,0,1:T(8,128)}), f32[5,32,16,128]{3,2,0,1:T(8,128)S(1)}, u32[]{:S(2)}, u32[]{:S(2)}) async-start(f32[5,32,16,128]{3,2,0,1:T(8,128)} %bitcast.336), calls=%async_computation | async-start | bytes 2621440 | tf_op jit(solution)/shard_map/all_to_all | solution.py:127
  23.3 0.9 copy-start.5
  23.3 1.0 copy-start.6
  23.4 1.6 %copy-start.7 = (s32[40]{0:T(128)S(1)}, s32[40]{0:T(128)}, u32[]{:S(2)}) copy-start(s32[40]{0:T(128)} %param.17) | copy-start | bytes 484
  70.9 31.2 %all-to-all-start.2 = ((f32[16,12,16,128]{3,2,1,0:T(8,128)}), f32[16,12,16,128]{3,2,1,0:T(8,128)S(1)}, u32[]{:S(2)}, u32[]{:S(2)}) async-start(f32[16,12,16,128]{3,2,1,0:T(8,128)} %get-tuple-element.35), calls=%async_computation.2 | async-start | bytes 3145728 | tf_op jit(solution)/shard_map/all_to_all | solution.py:148
  102.1 1.3 %copy-start.1 = (f32[5,32,16,128]{3,2,1,0:T(8,128)S(1)}, f32[5,32,16,128]{3,2,1,0:T(8,128)}, u32[]{:S(2)}) copy-start(f32[5,32,16,128]{3,2,1,0:T(8,128)} %get-tuple-element.33) | copy-start | bytes 3932164
  102.1 1.3 %copy-start.3 = (f32[32,16,128]{2,1,0:T(8,128)S(1)}, f32[32,16,128]{2,1,0:T(8,128)}, u32[]{:S(2)}) copy-start(f32[32,16,128]{2,1,0:T(8,128)} %get-tuple-element.34) | copy-start | bytes 786436
  102.1 1.4 %copy-start.4 = (f32[32,16,128]{2,1,0:T(8,128)S(1)}, f32[32,16,128]{2,1,0:T(8,128)}, u32[]{:S(2)}) copy-start(f32[32,16,128]{2,1,0:T(8,128)} %get-tuple-element.36) | copy-start | bytes 786436

commit v7 on v6

--- a/solution.py
+++ b/solution.py
@@ -6,57 +6,62 @@
 from jax.sharding import PartitionSpec as P
 
 
-def neighbour_sum(x, axis):
-    size = x.shape[axis]
-    where_from = lax.broadcasted_iota(jnp.int32, x.shape, axis)
-    total = jnp.zeros_like(x)
-    for shift in (1, size - 1):
-        rolled = pltpu.roll(x, shift, axis)
-        source = pltpu.roll(where_from, shift, axis)
-        inside = jnp.abs(source - where_from) == 1
-        total = total + jnp.where(inside, rolled, 0.0)
-    return total
+def neighbour_masks(shape, axis):
+    size = shape[axis]
+    where_from = lax.broadcasted_iota(jnp.int32, shape, axis)
+    return [
+        (shift, jnp.abs(pltpu.roll(where_from, shift, axis) - where_from) == 1)
+        for shift in (1, size - 1)
+    ]
 
 
-def stencil_kernel(fields_ref, out_ref):
+def stencil_kernel(fields_ref, below_ref, above_ref, out_ref):
     rows = fields_ref.shape[1]
-
-    def one_row(z, carried):
-        centre = fields_ref[:, z]
-        above = fields_ref[:, jnp.minimum(z + 1, rows - 1)]
-        below = fields_ref[:, jnp.maximum(z - 1, 0)]
-        beside = jnp.where(z + 1 < rows, above, 0.0) + jnp.where(z > 0, below, 0.0)
-        beside = beside + neighbour_sum(centre, 1)
-        beside = beside + neighbour_sum(centre, 2)
-        out_ref[z] = 6.0 * centre - beside
-        return carried
-
-    lax.fori_loop(0, rows, one_row, 0)
+    plane = fields_ref.shape[2:]
+    masks = neighbour_masks(plane, 0) + [(s, m) for s, m in neighbour_masks(plane, 1)]
+    axes = [0, 0, 1, 1]
+    for z in range(rows):
+        centre = fields_ref[0, z]
+        up = fields_ref[0, z + 1] if z + 1 < rows else above_ref[0]
+        down = fields_ref[0, z - 1] if z > 0 else below_ref[0]
+        beside = up + down
+        for axis, (shift, inside) in zip(axes, masks):
+            beside = beside + jnp.where(inside, pltpu.roll(centre, shift, axis), 0.0)
+        out_ref[z, 0] = 6.0 * centre - beside
 
 
-def slab_stencil(fields):
+def slab_stencil(fields, below, above):
     modes, rows = fields.shape[0], fields.shape[1]
+    plane = fields.shape[2:]
     return pl.pallas_call(
         stencil_kernel,
-        out_shape=jax.ShapeDtypeStruct((rows, modes) + fields.shape[2:], jnp.float32),
-    )(fields)
+        grid=(modes,),
+        in_specs=[
+            pl.BlockSpec((1, rows) + plane, lambda i: (i, 0, 0, 0)),
+            pl.BlockSpec((1,) + plane, lambda i: (i, 0, 0)),
+            pl.BlockSpec((1,) + plane, lambda i: (i, 0, 0)),
+        ],
+        out_specs=pl.BlockSpec((rows, 1) + plane, lambda i: (0, i, 0, 0)),
+        out_shape=jax.ShapeDtypeStruct((rows, modes) + plane, jnp.float32),
+    )(fields, below, above)
 
 
 def sweep_kernel(mixed_ref, decay_ref, back_ref, coupled_ref, tail_ref, summary_ref):
     rows = decay_ref.shape[0]
+    chunk = mixed_ref.shape[2]
 
     def forward_row(z, carried):
         state, ratio = carried
         d = decay_ref[z]
         g = jnp.sqrt(1.0 - d * d)
-        state = d[None] * state + g[None] * mixed_ref[:, z]
+        state = d[None] * state + g[None] * mixed_ref[z // chunk, :, z % chunk]
         ratio = d * ratio
         back_ref[:, z] = g[None] * state
         coupled_ref[z] = g * ratio
         return state, ratio
 
     lateral = decay_ref.shape[1:]
-    modes = mixed_ref.shape[0]
+    modes = mixed_ref.shape[1]
     state, _ = lax.fori_loop(
         0,
         rows,
@@ -94,12 +99,13 @@
 
 
 def local_sweeps(mixed, decay, copies):
-    modes, rows = mixed.shape[0], mixed.shape[1]
-    lateral = mixed.shape[2:]
+    modes = mixed.shape[1]
+    rows = decay.shape[0]
+    lateral = decay.shape[1:]
     return pl.pallas_call(
         sweep_kernel,
         out_shape=(
-            jax.ShapeDtypeStruct(mixed.shape, jnp.float32),
+            jax.ShapeDtypeStruct((modes, rows) + lateral, jnp.float32),
             jax.ShapeDtypeStruct(decay.shape, jnp.float32),
             jax.ShapeDtypeStruct(decay.shape, jnp.float32),
             jax.ShapeDtypeStruct((copies, 2 + 2 * modes) + lateral, jnp.float32),
@@ -121,8 +127,7 @@
     slabs = lax.axis_size("depth")
     from_below = lax.ppermute(fields[:, -1], "depth", [(i, i + 1) for i in range(slabs - 1)])
     from_above = lax.ppermute(fields[:, 0], "depth", [(i + 1, i) for i in range(slabs - 1)])
-    stencil = slab_stencil(fields)
-    stencil = stencil.at[0].add(-from_below).at[-1].add(-from_above)
+    stencil = slab_stencil(fields, from_below, from_above)
     stencil = jnp.transpose(stencil, (1, 0, 2, 3))
     stencil_rows = lax.all_to_all(stencil, "mode", 1, 0, tiled=True)
     cell_count = chunk * lateral[0] * lateral[1]
@@ -142,7 +147,8 @@
     ).reshape(term_total, mode_total, cell_count)
     mixed_rows = jnp.sum(coefficients * accumulated, axis=0)
     mixed_rows = mixed_rows.reshape((mode_total, chunk) + lateral)
-    mixed_field = lax.all_to_all(mixed_rows, "mode", 0, 1, tiled=True)
+    mixed_field = lax.all_to_all(mixed_rows, "mode", 0, 0, tiled=True)
+    mixed_field = mixed_field.reshape((groups, local_modes, chunk) + lateral)
 
     back, coupled, tail, copies = local_sweeps(mixed_field, decay, slabs)
     summaries = lax.all_to_all(copies, "depth", 0, 0, tiled=True)

time: 105 us -> 108 us (1.029)
  waiting for transfers between devices: 36.6 us -> 40.5 us
  other arithmetic: 5.33 us -> 2.52 us
  starting transfers between devices: 21.9 us -> 24.2 us
    ppermute x1, waiting for transfers between devices: 0.01 us -> 4.23 us  [local(): lax.ppermute(fields[:, 0], 'depth', [(i + 1, i) for i in range(slabs - 1)])]
    scatter-add x2 -> x0, other arithmetic: 2.81 us -> none  [local(): stencil = stencil.at[0].add(-from_below).at[-1].add(-from_above)]
    all_to_all x1, starting transfers between devices: 8.34 us -> 10.6 us  [local(): summaries = lax.all_to_all(copies, 'depth', 0, 0, tiled=True)]
    all_to_all x1 -> x0, local copies, waits for them, and re-layouts: 1.15 us -> none  [local(): mixed_field = lax.all_to_all(mixed_rows, 'mode', 0, 1, tiled=True)]
    unnamed x18 -> x22, local copies, waits for them, and re-layouts: 2.21 us -> 2.82 us
  transfers between devices with their start and end apart: 4 -> 4, of which waited for: 2 -> 3; matrix products, arithmetic and copies ran while one was open for 4% -> 2% of each run, Pallas kernels for 5% -> 0%
where the time goes in v7:
time: 108 us; the launch traced here: 107 us
  waiting for transfers between devices  40.5 us (38%)
  starting transfers between devices  24.2 us (22%)
  blocking collectives  21 us (19%)
  Pallas kernels  8.57 us (8%)
  local copies, waits for them, and re-layouts  5.36 us (5%)
  matrix products  4.91 us (5%)
  other arithmetic  2.52 us (2%)
    all_to_all x1, waiting for transfers between devices, local(): summaries = lax.all_to_all(copies, 'depth', 0, 0, tiled=True)  22.8 us
    all_to_all x1, blocking collectives, local(): mixed_field = lax.all_to_all(mixed_rows, 'mode', 0, 0, tiled=True)  21 us
    all_to_all x1, waiting for transfers between devices, local(): stencil_rows = lax.all_to_all(stencil, 'mode', 1, 0, tiled=True)  13.4 us
    all_to_all x1, starting transfers between devices, local(): summaries = lax.all_to_all(copies, 'depth', 0, 0, tiled=True)  10.6 us
    ppermute x1, starting transfers between devices, local(): lax.ppermute(fields[:, -1], 'depth', [(i, i + 1) for i in range(slabs - 1)])  6.88 us
    dot_general x1, matrix products, local(): jnp.dot(table_rows, stencil_rows, precision=lax.Precision.HIGH, preferred...  4.91 us
    all_to_all x1, starting transfers between devices, local(): stencil_rows = lax.all_to_all(stencil, 'mode', 1, 0, tiled=True)  4.78 us
    pallas_call x1, Pallas kernels, slab_stencil(): pl.pallas_call(stencil_kernel, grid=(modes,), in_specs=[pl.BlockSpec((1,...  4.49 us
  transfers between devices with their start and end apart: 4, of which 3 were waited for; matrix products, arithmetic and copies ran while one was open for 2% of the time, Pallas kernels for 0%

profile of v7, /device:TPU:1, one launch (start us, length us, event | category | flops | bytes accessed | tf_op | source)
XLA Modules:
  0.0 107.3 jit_solution(9161771651567227634)
XLA Ops:
  0.0 0.8 slice_bitcast_fusion.30
  0.8 6.9 %collective-permute-start = (f32[5,16,128]{2,1,0:T(8,128)S(1)}, f32[5,16,128]{2,1,0:T(8,128)S(1)}, u32[]{:S(2)}, u32[]{:S(2)}) collective-permute-start(f32[5,16,128]{2,1,0:T(8,128)S(1)} %get-tuple-element.45), channel_id=1, source_target_pairs={{0,1},{1,2},{2,3},{3,4},{4,5},{5,6},{6,7},{7,8},{8,9},{9,10},{10,1... | collective-permute-start | bytes 122888 | tf_op jit(solution)/shard_map/ppermute | solution.py:128
  7.7 1.9 %collective-permute-start.1 = (f32[5,16,128]{2,1,0:T(8,128)S(1)}, f32[5,16,128]{2,1,0:T(8,128)S(1)}, u32[]{:S(2)}, u32[]{:S(2)}) collective-permute-start(f32[5,16,128]{2,1,0:T(8,128)S(1)} %get-tuple-element.44), channel_id=1, source_target_pairs={{1,0},{2,1},{3,2},{4,3},{5,4},{6,5},{7,6},{8,7},{9,8},{10,9},{11,1... | collective-permute-start | bytes 122888 | tf_op jit(solution)/shard_map/ppermute | solution.py:129
  9.6 0.7 compare_select_fusion
  10.3 4.2 %collective-permute-done.1.above_ref = f32[5,16,128]{2,1,0:T(8,128)S(1)} collective-permute-done((f32[5,16,128]{2,1,0:T(8,128)S(1)}, f32[5,16,128]{2,1,0:T(8,128)S(1)}, u32[]{:S(2)}, u32[]{:S(2)}) %collective-permute-start.1) | collective-permute-done | bytes 40992 | tf_op jit(solution)/shard_map/ppermute | solution.py:129
  14.5 0.6 copy-done.8
  15.1 4.5 %shard_map.73 = f32[32,5,16,128]{3,2,1,0:T(8,128)} custom-call(f32[5,32,16,128]{3,2,1,0:T(8,128)} %fields_ref.1, f32[5,16,128]{2,1,0:T(8,128)} %copy-done.7, f32[5,16,128]{2,1,0:T(8,128)} %copy-done.8), custom_call_target="tpu_custom_call" | custom-call | tf_op jit(solution)/shard_map/pallas_call | solution.py:36
  19.6 4.8 %all-to-all-start = ((f32[5,32,16,128]{3,2,0,1:T(8,128)}), f32[5,32,16,128]{3,2,0,1:T(8,128)S(1)}, u32[]{:S(2)}, u32[]{:S(2)}) async-start(f32[5,32,16,128]{3,2,0,1:T(8,128)} %bitcast.330), calls=%async_computation | async-start | bytes 2621440 | tf_op jit(solution)/shard_map/all_to_all | solution.py:132
  24.5 0.2 copy.26
  24.7 0.7 copy-done.5
  25.4 0.6 gather_fusion
  26.3 0.6 gather_fusion.1
  27.1 13.4 %all-to-all-done = f32[5,32,16,128]{3,2,0,1:T(8,128)S(1)} async-done(((f32[5,32,16,128]{3,2,0,1:T(8,128)}), f32[5,32,16,128]{3,2,0,1:T(8,128)S(1)}, u32[]{:S(2)}, u32[]{:S(2)}) %all-to-all-start) | async-done | bytes 1310752 | tf_op jit(solution)/shard_map/all_to_all | solution.py:132
  40.5 0.2 copy.17
  40.6 0.2 reshape.393
  40.9 4.9 %fusion = f32[40,8192]{1,0:T(8,128)S(1)} fusion(f32[40,8192,1]{1,0,2:T(8,128)S(1)} %reshape.393, f32[8,8192]{1,0:T(8,128)S(1)} %bitcast.336, f32[8,40,40]{1,0,2:T(8,128)S(1)} %select_bitcast_fusion), kind=kOutput, calls=%fused_computation.3 | convolution fusion | flops 634060800 | bytes 2934784 | tf_op jit(solution)/shard_map/dot_general | solution.py:142
  45.8 0.2 copy.22
  46.0 21.0 %all_to_all.25 = f32[40,4,16,128]{3,2,1,0:T(8,128)} all-to-all(f32[40,4,16,128]{3,2,1,0:T(8,128)S(1)} %bitcast.332), channel_id=1, replica_groups=mesh['mode'=8,'depth'=16] {'mode'}, dimensions={0} | all-to-all | bytes 2621440 | tf_op jit(solution)/shard_map/all_to_all | solution.py:150
  67.1 4.1 %shard_map.74 = (f32[5,32,16,128]{3,2,1,0:T(8,128)}, f32[32,16,128]{2,1,0:T(8,128)}, f32[32,16,128]{2,1,0:T(8,128)}, f32[16,12,16,128]{3,2,1,0:T(8,128)}) custom-call(f32[8,5,4,16,128]{4,3,2,1,0:T(8,128)} %bitcast.331, f32[32,16,128]{2,1,0:T(8,128)} %decay_ref.1), custom_call_target="tpu_custom_call" | custom-call | tf_op jit(solution)/shard_map/pallas_call | solution.py:105
  71.1 10.6 %all-to-all-start.2 = ((f32[16,12,16,128]{3,2,1,0:T(8,128)}), f32[16,12,16,128]{3,2,1,0:T(8,128)S(1)}, u32[]{:S(2)}, u32[]{:S(2)}) async-start(f32[16,12,16,128]{3,2,1,0:T(8,128)} %get-tuple-element.11), calls=%async_computation.2 | async-start | bytes 3145728 | tf_op jit(solution)/shard_map/all_to_all | solution.py:154
  81.7 22.8 %all-to-all-done.2 = f32[16,12,16,128]{3,2,1,0:T(8,128)S(1)} async-done(((f32[16,12,16,128]{3,2,1,0:T(8,128)}), f32[16,12,16,128]{3,2,1,0:T(8,128)S(1)}, u32[]{:S(2)}, u32[]{:S(2)}) %all-to-all-start.2) | async-done | bytes 1572896 | tf_op jit(solution)/shard_map/all_to_all | solution.py:154
  104.7 0.2 fusion.33
  105.0 0.9 copy-done.1
  106.0 1.2 %multiply_add_fusion = f32[5,32,16,128]{3,2,1,0:T(8,128)} fusion(f32[5,32,16,128]{3,2,1,0:T(8,128)S(1)} %copy-done.1, f32[5,16,128]{2,1,0:T(8,128)S(1)} %fusion.33, f32[32,16,128]{2,1,0:T(8,128)S(1)} %copy-done.4, f32[5,16,128]{2,1,0:T(8,128)S(1)} %select_select_fusion, f32[32,16,128]{2,1,0:T(8,128)S(1)} %copy-done.3), kind=kLoop, calls=%fused_computation.6 | loop fusion | flops 1310720 | bytes 3227648 | tf_op jit(solution)/shard_map/add | solution.py:176
  (28 shorter events, 0.8 us)
Async XLA Ops:
  0.8 9.5 %collective-permute-start = (f32[5,16,128]{2,1,0:T(8,128)S(1)}, f32[5,16,128]{2,1,0:T(8,128)S(1)}, u32[]{:S(2)}, u32[]{:S(2)}) collective-permute-start(f32[5,16,128]{2,1,0:T(8,128)S(1)} %get-tuple-element.45), channel_id=1, source_target_pairs={{0,1},{1,2},{2,3},{3,4},{4,5},{5,6},{6,7},{7,8},{8,9},{9,10},{10,1... | collective-permute-start | bytes 122888 | tf_op jit(solution)/shard_map/ppermute | solution.py:128
  7.7 6.8 %collective-permute-start.1 = (f32[5,16,128]{2,1,0:T(8,128)S(1)}, f32[5,16,128]{2,1,0:T(8,128)S(1)}, u32[]{:S(2)}, u32[]{:S(2)}) collective-permute-start(f32[5,16,128]{2,1,0:T(8,128)S(1)} %get-tuple-element.44), channel_id=1, source_target_pairs={{1,0},{2,1},{3,2},{4,3},{5,4},{6,5},{7,6},{8,7},{9,8},{10,9},{11,1... | collective-permute-start | bytes 122888 | tf_op jit(solution)/shard_map/ppermute | solution.py:129
  10.3 4.2 %copy-start.7 = (f32[5,16,128]{2,1,0:T(8,128)}, f32[5,16,128]{2,1,0:T(8,128)S(1)}, u32[]{:S(2)}) copy-start(f32[5,16,128]{2,1,0:T(8,128)S(1)} %collective-permute-done.below_ref) | copy-start | bytes 122884
  14.5 0.6 copy-start.8
  19.6 4.8 %copy-start = (f32[7,32,16,128]{3,2,1,0:T(8,128)S(1)}, f32[7,32,16,128]{3,2,1,0:T(8,128)}, u32[]{:S(2)}) copy-start(f32[7,32,16,128]{3,2,1,0:T(8,128)} %param.9) | copy-start | bytes 5505028
  19.6 4.8 %copy-start.2 = (f32[32,16,128]{2,1,0:T(8,128)S(1)}, f32[32,16,128]{2,1,0:T(8,128)}, u32[]{:S(2)}) copy-start(f32[32,16,128]{2,1,0:T(8,128)} %param.8) | copy-start | bytes 786436
  19.6 20.8 %all-to-all-start = ((f32[5,32,16,128]{3,2,0,1:T(8,128)}), f32[5,32,16,128]{3,2,0,1:T(8,128)S(1)}, u32[]{:S(2)}, u32[]{:S(2)}) async-start(f32[5,32,16,128]{3,2,0,1:T(8,128)} %bitcast.330), calls=%async_computation | async-start | bytes 2621440 | tf_op jit(solution)/shard_map/all_to_all | solution.py:132
  24.4 0.9 copy-start.5
  24.4 1.0 copy-start.6
  24.5 1.6 %copy-start.9 = (s32[40]{0:T(128)S(1)}, s32[40]{0:T(128)}, u32[]{:S(2)}) copy-start(s32[40]{0:T(128)} %param.13) | copy-start | bytes 484
  71.1 33.4 %all-to-all-start.2 = ((f32[16,12,16,128]{3,2,1,0:T(8,128)}), f32[16,12,16,128]{3,2,1,0:T(8,128)S(1)}, u32[]{:S(2)}, u32[]{:S(2)}) async-start(f32[16,12,16,128]{3,2,1,0:T(8,128)} %get-tuple-element.11), calls=%async_computation.2 | async-start | bytes 3145728 | tf_op jit(solution)/shard_map/all_to_all | solution.py:154
  104.6 1.3 %copy-start.1 = (f32[5,32,16,128]{3,2,1,0:T(8,128)S(1)}, f32[5,32,16,128]{3,2,1,0:T(8,128)}, u32[]{:S(2)}) copy-start(f32[5,32,16,128]{3,2,1,0:T(8,128)} %get-tuple-element.9) | copy-start | bytes 3932164
  104.6 1.3 %copy-start.3 = (f32[32,16,128]{2,1,0:T(8,128)S(1)}, f32[32,16,128]{2,1,0:T(8,128)}, u32[]{:S(2)}) copy-start(f32[32,16,128]{2,1,0:T(8,128)} %get-tuple-element.10) | copy-start | bytes 786436
  104.6 1.4 %copy-start.4 = (f32[32,16,128]{2,1,0:T(8,128)S(1)}, f32[32,16,128]{2,1,0:T(8,128)}, u32[]{:S(2)}) copy-start(f32[32,16,128]{2,1,0:T(8,128)} %get-tuple-element.12) | copy-start | bytes 786436

commit v8 on v7

--- a/solution.py
+++ b/solution.py
@@ -15,35 +15,56 @@
     ]
 
 
-def stencil_kernel(fields_ref, below_ref, above_ref, out_ref):
+def stencil_kernel(fields_ref, out_ref):
     rows = fields_ref.shape[1]
     plane = fields_ref.shape[2:]
-    masks = neighbour_masks(plane, 0) + [(s, m) for s, m in neighbour_masks(plane, 1)]
+    masks = neighbour_masks(plane, 0) + neighbour_masks(plane, 1)
     axes = [0, 0, 1, 1]
     for z in range(rows):
         centre = fields_ref[0, z]
-        up = fields_ref[0, z + 1] if z + 1 < rows else above_ref[0]
-        down = fields_ref[0, z - 1] if z > 0 else below_ref[0]
-        beside = up + down
+        beside = jnp.zeros_like(centre)
+        if z + 1 < rows:
+            beside = beside + fields_ref[0, z + 1]
+        if z > 0:
+            beside = beside + fields_ref[0, z - 1]
         for axis, (shift, inside) in zip(axes, masks):
             beside = beside + jnp.where(inside, pltpu.roll(centre, shift, axis), 0.0)
         out_ref[z, 0] = 6.0 * centre - beside
 
 
-def slab_stencil(fields, below, above):
+def slab_stencil(fields):
     modes, rows = fields.shape[0], fields.shape[1]
     plane = fields.shape[2:]
     return pl.pallas_call(
         stencil_kernel,
         grid=(modes,),
-        in_specs=[
-            pl.BlockSpec((1, rows) + plane, lambda i: (i, 0, 0, 0)),
-            pl.BlockSpec((1,) + plane, lambda i: (i, 0, 0)),
-            pl.BlockSpec((1,) + plane, lambda i: (i, 0, 0)),
-        ],
+        in_specs=[pl.BlockSpec((1, rows) + plane, lambda i: (i, 0, 0, 0))],
         out_specs=pl.BlockSpec((rows, 1) + plane, lambda i: (0, i, 0, 0)),
         out_shape=jax.ShapeDtypeStruct((rows, modes) + plane, jnp.float32),
-    )(fields, below, above)
+    )(fields)
+
+
+def edge_kernel(stencil_ref, below_ref, above_ref, out_ref):
+    halo = jnp.where(pl.program_id(0) == 0, below_ref[...], above_ref[...])
+    out_ref[...] = stencil_ref[...] - halo[None]
+
+
+def add_edges(stencil, below, above):
+    rows = stencil.shape[0]
+    edge = (1,) + stencil.shape[1:]
+    at_edge = lambda i: (i * (rows - 1), 0, 0, 0)
+    return pl.pallas_call(
+        edge_kernel,
+        grid=(2,),
+        in_specs=[
+            pl.BlockSpec(edge, at_edge),
+            pl.BlockSpec(below.shape, lambda i: (0, 0, 0)),
+            pl.BlockSpec(above.shape, lambda i: (0, 0, 0)),
+        ],
+        out_specs=pl.BlockSpec(edge, at_edge),
+        out_shape=jax.ShapeDtypeStruct(stencil.shape, jnp.float32),
+        input_output_aliases={0: 0},
+    )(stencil, below, above)
 
 
 def sweep_kernel(mixed_ref, decay_ref, back_ref, coupled_ref, tail_ref, summary_ref):
@@ -127,7 +148,7 @@
     slabs = lax.axis_size("depth")
     from_below = lax.ppermute(fields[:, -1], "depth", [(i, i + 1) for i in range(slabs - 1)])
     from_above = lax.ppermute(fields[:, 0], "depth", [(i + 1, i) for i in range(slabs - 1)])
-    stencil = slab_stencil(fields, from_below, from_above)
+    stencil = add_edges(slab_stencil(fields), from_below, from_above)
     stencil = jnp.transpose(stencil, (1, 0, 2, 3))
     stencil_rows = lax.all_to_all(stencil, "mode", 1, 0, tiled=True)
     cell_count = chunk * lateral[0] * lateral[1]

time: 108 us -> 103 us (0.954)
  waiting for transfers between devices: 40.5 us -> 36.6 us
  starting transfers between devices: 24.2 us -> 21.7 us
  Pallas kernels: 8.57 us -> 9.95 us
    ppermute x1, waiting for transfers between devices: 4.23 us -> 0.01 us  [local(): lax.ppermute(fields[:, 0], 'depth', [(i + 1, i) for i in range(slabs - 1)])]
    all_to_all x1, starting transfers between devices: 10.6 us -> 8.09 us  [local(): summaries = lax.all_to_all(copies, 'depth', 0, 0, tiled=True)]
    pallas_call x0 -> x1, Pallas kernels: none -> 1.47 us  [add_edges(): pl.pallas_call(edge_kernel, grid=(2,), in_specs=[pl.BlockSpec(edge, at_ed...]
  transfers between devices with their start and end apart: 4 -> 4, of which waited for: 3 -> 2; matrix products, arithmetic and copies ran while one was open for 2% -> 2% of each run, Pallas kernels for 0% -> 4%
where the time goes in v8:
time: 103 us
  waiting for transfers between devices  36.6 us (36%)
  starting transfers between devices  21.7 us (21%)
  blocking collectives  21 us (20%)
  Pallas kernels  9.95 us (10%)
  local copies, waits for them, and re-layouts  5.96 us (6%)
  matrix products  4.91 us (5%)
  other arithmetic  2.52 us (2%)
    all_to_all x1, waiting for transfers between devices, local(): summaries = lax.all_to_all(copies, 'depth', 0, 0, tiled=True)  22.8 us
    all_to_all x1, blocking collectives, local(): mixed_field = lax.all_to_all(mixed_rows, 'mode', 0, 0, tiled=True)  21 us
    all_to_all x1, waiting for transfers between devices, local(): stencil_rows = lax.all_to_all(stencil, 'mode', 1, 0, tiled=True)  13.7 us
    all_to_all x1, starting transfers between devices, local(): summaries = lax.all_to_all(copies, 'depth', 0, 0, tiled=True)  8.09 us
    ppermute x1, starting transfers between devices, local(): lax.ppermute(fields[:, -1], 'depth', [(i, i + 1) for i in range(slabs - 1)])  6.88 us
    dot_general x1, matrix products, local(): jnp.dot(table_rows, stencil_rows, precision=lax.Precision.HIGH, preferred...  4.91 us
    all_to_all x1, starting transfers between devices, local(): stencil_rows = lax.all_to_all(stencil, 'mode', 1, 0, tiled=True)  4.78 us
    pallas_call x1, Pallas kernels, slab_stencil(): pl.pallas_call(stencil_kernel, grid=(modes,), in_specs=[pl.BlockSpec((1,...  4.41 us
  transfers between devices with their start and end apart: 4, of which 2 were waited for; matrix products, arithmetic and copies ran while one was open for 2% of the time, Pallas kernels for 4%

profile of v8, /device:TPU:1, one launch (start us, length us, event | category | flops | bytes accessed | tf_op | source)
XLA Modules:
  0.0 102.8 jit_solution(6575046482409112858)
XLA Ops:
  0.0 0.8 slice_bitcast_fusion.30
  0.8 6.9 %collective-permute-start = (f32[5,16,128]{2,1,0:T(8,128)S(1)}, f32[5,16,128]{2,1,0:T(8,128)S(1)}, u32[]{:S(2)}, u32[]{:S(2)}) collective-permute-start(f32[5,16,128]{2,1,0:T(8,128)S(1)} %get-tuple-element.45), channel_id=1, source_target_pairs={{0,1},{1,2},{2,3},{3,4},{4,5},{5,6},{6,7},{7,8},{8,9},{9,10},{10,1... | collective-permute-start | bytes 122888 | tf_op jit(solution)/shard_map/ppermute | solution.py:149
  7.7 1.9 %collective-permute-start.1 = (f32[5,16,128]{2,1,0:T(8,128)S(1)}, f32[5,16,128]{2,1,0:T(8,128)S(1)}, u32[]{:S(2)}, u32[]{:S(2)}) collective-permute-start(f32[5,16,128]{2,1,0:T(8,128)S(1)} %get-tuple-element.44), channel_id=1, source_target_pairs={{1,0},{2,1},{3,2},{4,3},{5,4},{6,5},{7,6},{8,7},{9,8},{10,9},{11,1... | collective-permute-start | bytes 122888 | tf_op jit(solution)/shard_map/ppermute | solution.py:150
  9.6 0.7 compare_select_fusion
  10.3 4.4 %shard_map.73.stencil_ref = f32[32,5,16,128]{3,2,1,0:T(8,128)} custom-call(f32[5,32,16,128]{3,2,1,0:T(8,128)} %fields_ref.1), custom_call_target="tpu_custom_call" | custom-call | tf_op jit(solution)/shard_map/pallas_call | solution.py:38
  14.7 0.6 copy-done.7
  15.3 0.6 copy-done.8
  15.9 1.5 %shard_map.74 = f32[32,5,16,128]{3,2,1,0:T(8,128)} custom-call(f32[32,5,16,128]{3,2,1,0:T(8,128)} %shard_map.73.stencil_ref, f32[5,16,128]{2,1,0:T(8,128)} %copy-done.7, f32[5,16,128]{2,1,0:T(8,128)} %copy-done.8), custom_call_target="tpu_custom_call", output_to_operand_aliasing={{}: (0, {})} | custom-call | tf_op jit(solution)/shard_map/pallas_call | solution.py:56
  17.4 4.8 %all-to-all-start = ((f32[5,32,16,128]{3,2,0,1:T(8,128)}), f32[5,32,16,128]{3,2,0,1:T(8,128)S(1)}, u32[]{:S(2)}, u32[]{:S(2)}) async-start(f32[5,32,16,128]{3,2,0,1:T(8,128)} %bitcast.329), calls=%async_computation | async-start | bytes 2621440 | tf_op jit(solution)/shard_map/all_to_all | solution.py:153
  22.3 0.2 copy.27
  22.4 0.7 copy-done.5
  23.2 0.6 gather_fusion
  24.1 0.6 gather_fusion.1
  24.8 13.7 %all-to-all-done = f32[5,32,16,128]{3,2,0,1:T(8,128)S(1)} async-done(((f32[5,32,16,128]{3,2,0,1:T(8,128)}), f32[5,32,16,128]{3,2,0,1:T(8,128)S(1)}, u32[]{:S(2)}, u32[]{:S(2)}) %all-to-all-start) | async-done | bytes 1310752 | tf_op jit(solution)/shard_map/all_to_all | solution.py:153
  38.7 0.2 reshape.393
  39.0 4.9 %fusion = f32[40,8192]{1,0:T(8,128)S(1)} fusion(f32[40,8192,1]{1,0,2:T(8,128)S(1)} %reshape.393, f32[8,8192]{1,0:T(8,128)S(1)} %bitcast.336, f32[8,40,40]{1,0,2:T(8,128)S(1)} %select_bitcast_fusion), kind=kOutput, calls=%fused_computation.3 | convolution fusion | flops 634060800 | bytes 2934784 | tf_op jit(solution)/shard_map/dot_general | solution.py:163
  43.9 0.2 copy.23
  44.1 21.0 %all_to_all.25 = f32[40,4,16,128]{3,2,1,0:T(8,128)} all-to-all(f32[40,4,16,128]{3,2,1,0:T(8,128)S(1)} %bitcast.332), channel_id=1, replica_groups=mesh['mode'=8,'depth'=16] {'mode'}, dimensions={0} | all-to-all | bytes 2621440 | tf_op jit(solution)/shard_map/all_to_all | solution.py:171
  65.1 4.1 %shard_map.75 = (f32[5,32,16,128]{3,2,1,0:T(8,128)}, f32[32,16,128]{2,1,0:T(8,128)}, f32[32,16,128]{2,1,0:T(8,128)}, f32[16,12,16,128]{3,2,1,0:T(8,128)}) custom-call(f32[8,5,4,16,128]{4,3,2,1,0:T(8,128)} %bitcast.331, f32[32,16,128]{2,1,0:T(8,128)} %decay_ref.1), custom_call_target="tpu_custom_call" | custom-call | tf_op jit(solution)/shard_map/pallas_call | solution.py:126
  69.2 8.1 %all-to-all-start.2 = ((f32[16,12,16,128]{3,2,1,0:T(8,128)}), f32[16,12,16,128]{3,2,1,0:T(8,128)S(1)}, u32[]{:S(2)}, u32[]{:S(2)}) async-start(f32[16,12,16,128]{3,2,1,0:T(8,128)} %get-tuple-element.11), calls=%async_computation.2 | async-start | bytes 3145728 | tf_op jit(solution)/shard_map/all_to_all | solution.py:175
  77.3 22.8 %all-to-all-done.2 = f32[16,12,16,128]{3,2,1,0:T(8,128)S(1)} async-done(((f32[16,12,16,128]{3,2,1,0:T(8,128)}), f32[16,12,16,128]{3,2,1,0:T(8,128)S(1)}, u32[]{:S(2)}, u32[]{:S(2)}) %all-to-all-start.2) | async-done | bytes 1572896 | tf_op jit(solution)/shard_map/all_to_all | solution.py:175
  100.3 0.2 fusion.33
  100.5 0.9 copy-done.1
  101.6 1.2 %multiply_add_fusion = f32[5,32,16,128]{3,2,1,0:T(8,128)} fusion(f32[5,32,16,128]{3,2,1,0:T(8,128)S(1)} %copy-done.1, f32[5,16,128]{2,1,0:T(8,128)S(1)} %fusion.33, f32[32,16,128]{2,1,0:T(8,128)S(1)} %copy-done.4, f32[5,16,128]{2,1,0:T(8,128)S(1)} %select_select_fusion, f32[32,16,128]{2,1,0:T(8,128)S(1)} %copy-done.3), kind=kLoop, calls=%fused_computation.6 | loop fusion | flops 1310720 | bytes 3227648 | tf_op jit(solution)/shard_map/add | solution.py:197
  (29 shorter events, 0.9 us)
Async XLA Ops:
  0.8 13.9 %collective-permute-start = (f32[5,16,128]{2,1,0:T(8,128)S(1)}, f32[5,16,128]{2,1,0:T(8,128)S(1)}, u32[]{:S(2)}, u32[]{:S(2)}) collective-permute-start(f32[5,16,128]{2,1,0:T(8,128)S(1)} %get-tuple-element.45), channel_id=1, source_target_pairs={{0,1},{1,2},{2,3},{3,4},{4,5},{5,6},{6,7},{7,8},{8,9},{9,10},{10,1... | collective-permute-start | bytes 122888 | tf_op jit(solution)/shard_map/ppermute | solution.py:149
  7.7 7.0 %collective-permute-start.1 = (f32[5,16,128]{2,1,0:T(8,128)S(1)}, f32[5,16,128]{2,1,0:T(8,128)S(1)}, u32[]{:S(2)}, u32[]{:S(2)}) collective-permute-start(f32[5,16,128]{2,1,0:T(8,128)S(1)} %get-tuple-element.44), channel_id=1, source_target_pairs={{1,0},{2,1},{3,2},{4,3},{5,4},{6,5},{7,6},{8,7},{9,8},{10,9},{11,1... | collective-permute-start | bytes 122888 | tf_op jit(solution)/shard_map/ppermute | solution.py:150
  14.7 0.6 copy-start.7
  15.3 0.6 copy-start.8
  17.4 4.8 %copy-start = (f32[7,32,16,128]{3,2,1,0:T(8,128)S(1)}, f32[7,32,16,128]{3,2,1,0:T(8,128)}, u32[]{:S(2)}) copy-start(f32[7,32,16,128]{3,2,1,0:T(8,128)} %param.9) | copy-start | bytes 5505028
  17.4 4.8 %copy-start.2 = (f32[32,16,128]{2,1,0:T(8,128)S(1)}, f32[32,16,128]{2,1,0:T(8,128)}, u32[]{:S(2)}) copy-start(f32[32,16,128]{2,1,0:T(8,128)} %param.8) | copy-start | bytes 786436
  17.4 21.1 %all-to-all-start = ((f32[5,32,16,128]{3,2,0,1:T(8,128)}), f32[5,32,16,128]{3,2,0,1:T(8,128)S(1)}, u32[]{:S(2)}, u32[]{:S(2)}) async-start(f32[5,32,16,128]{3,2,0,1:T(8,128)} %bitcast.329), calls=%async_computation | async-start | bytes 2621440 | tf_op jit(solution)/shard_map/all_to_all | solution.py:153
  22.2 0.9 copy-start.5
  22.2 1.0 copy-start.6
  22.2 1.6 %copy-start.9 = (s32[40]{0:T(128)S(1)}, s32[40]{0:T(128)}, u32[]{:S(2)}) copy-start(s32[40]{0:T(128)} %param.13) | copy-start | bytes 484
  69.2 30.9 %all-to-all-start.2 = ((f32[16,12,16,128]{3,2,1,0:T(8,128)}), f32[16,12,16,128]{3,2,1,0:T(8,128)S(1)}, u32[]{:S(2)}, u32[]{:S(2)}) async-start(f32[16,12,16,128]{3,2,1,0:T(8,128)} %get-tuple-element.11), calls=%async_computation.2 | async-start | bytes 3145728 | tf_op jit(solution)/shard_map/all_to_all | solution.py:175
  100.2 1.3 %copy-start.1 = (f32[5,32,16,128]{3,2,1,0:T(8,128)S(1)}, f32[5,32,16,128]{3,2,1,0:T(8,128)}, u32[]{:S(2)}) copy-start(f32[5,32,16,128]{3,2,1,0:T(8,128)} %get-tuple-element.9) | copy-start | bytes 3932164
  100.2 1.3 %copy-start.3 = (f32[32,16,128]{2,1,0:T(8,128)S(1)}, f32[32,16,128]{2,1,0:T(8,128)}, u32[]{:S(2)}) copy-start(f32[32,16,128]{2,1,0:T(8,128)} %get-tuple-element.10) | copy-start | bytes 786436
  100.2 1.4 %copy-start.4 = (f32[32,16,128]{2,1,0:T(8,128)S(1)}, f32[32,16,128]{2,1,0:T(8,128)}, u32[]{:S(2)}) copy-start(f32[32,16,128]{2,1,0:T(8,128)} %get-tuple-element.12) | copy-start | bytes 786436

commit v9 on v8

--- a/solution.py
+++ b/solution.py
@@ -120,11 +120,24 @@
 
 
 def local_sweeps(mixed, decay, copies):
-    modes = mixed.shape[1]
+    groups, modes, chunk = mixed.shape[0], mixed.shape[1], mixed.shape[2]
     rows = decay.shape[0]
     lateral = decay.shape[1:]
+    parts = 2
+    half = (lateral[0] // parts, lateral[1])
     return pl.pallas_call(
         sweep_kernel,
+        grid=(parts,),
+        in_specs=[
+            pl.BlockSpec((groups, modes, chunk) + half, lambda i: (0, 0, 0, i, 0)),
+            pl.BlockSpec((rows,) + half, lambda i: (0, i, 0)),
+        ],
+        out_specs=(
+            pl.BlockSpec((modes, rows) + half, lambda i: (0, 0, i, 0)),
+            pl.BlockSpec((rows,) + half, lambda i: (0, i, 0)),
+            pl.BlockSpec((rows,) + half, lambda i: (0, i, 0)),
+            pl.BlockSpec((copies, 2 + 2 * modes) + half, lambda i: (0, 0, i, 0)),
+        ),
         out_shape=(
             jax.ShapeDtypeStruct((modes, rows) + lateral, jnp.float32),
             jax.ShapeDtypeStruct(decay.shape, jnp.float32),

time: 103 us -> 103 us (level)
  no operation moved by 1% of the time
where the time goes in v9:
time: 103 us
  waiting for transfers between devices  36.6 us (36%)
  starting transfers between devices  21.7 us (21%)
  blocking collectives  21 us (20%)
  Pallas kernels  9.92 us (10%)
  local copies, waits for them, and re-layouts  5.96 us (6%)
  matrix products  4.91 us (5%)
  other arithmetic  2.52 us (2%)
    all_to_all x1, waiting for transfers between devices, local(): summaries = lax.all_to_all(copies, 'depth', 0, 0, tiled=True)  22.8 us
    all_to_all x1, blocking collectives, local(): mixed_field = lax.all_to_all(mixed_rows, 'mode', 0, 0, tiled=True)  21 us
    all_to_all x1, waiting for transfers between devices, local(): stencil_rows = lax.all_to_all(stencil, 'mode', 1, 0, tiled=True)  13.7 us
    all_to_all x1, starting transfers between devices, local(): summaries = lax.all_to_all(copies, 'depth', 0, 0, tiled=True)  8.09 us
    ppermute x1, starting transfers between devices, local(): lax.ppermute(fields[:, -1], 'depth', [(i, i + 1) for i in range(slabs - 1)])  6.88 us
    dot_general x1, matrix products, local(): jnp.dot(table_rows, stencil_rows, precision=lax.Precision.HIGH, preferred...  4.91 us
    all_to_all x1, starting transfers between devices, local(): stencil_rows = lax.all_to_all(stencil, 'mode', 1, 0, tiled=True)  4.78 us
    pallas_call x1, Pallas kernels, slab_stencil(): pl.pallas_call(stencil_kernel, grid=(modes,), in_specs=[pl.BlockSpec((1,...  4.41 us
  transfers between devices with their start and end apart: 4, of which 2 were waited for; matrix products, arithmetic and copies ran while one was open for 2% of the time, Pallas kernels for 4%

profile of v9, /device:TPU:1, one launch (start us, length us, event | category | flops | bytes accessed | tf_op | source)
XLA Modules:
  0.0 102.8 jit_solution(10573302972825583794)
XLA Ops:
  0.0 0.8 slice_bitcast_fusion.30
  0.8 6.9 %collective-permute-start = (f32[5,16,128]{2,1,0:T(8,128)S(1)}, f32[5,16,128]{2,1,0:T(8,128)S(1)}, u32[]{:S(2)}, u32[]{:S(2)}) collective-permute-start(f32[5,16,128]{2,1,0:T(8,128)S(1)} %get-tuple-element.45), channel_id=1, source_target_pairs={{0,1},{1,2},{2,3},{3,4},{4,5},{5,6},{6,7},{7,8},{8,9},{9,10},{10,1... | collective-permute-start | bytes 122888 | tf_op jit(solution)/shard_map/ppermute | solution.py:162
  7.7 1.9 %collective-permute-start.1 = (f32[5,16,128]{2,1,0:T(8,128)S(1)}, f32[5,16,128]{2,1,0:T(8,128)S(1)}, u32[]{:S(2)}, u32[]{:S(2)}) collective-permute-start(f32[5,16,128]{2,1,0:T(8,128)S(1)} %get-tuple-element.44), channel_id=1, source_target_pairs={{1,0},{2,1},{3,2},{4,3},{5,4},{6,5},{7,6},{8,7},{9,8},{10,9},{11,1... | collective-permute-start | bytes 122888 | tf_op jit(solution)/shard_map/ppermute | solution.py:163
  9.6 0.7 compare_select_fusion
  10.3 4.4 %shard_map.73.stencil_ref = f32[32,5,16,128]{3,2,1,0:T(8,128)} custom-call(f32[5,32,16,128]{3,2,1,0:T(8,128)} %fields_ref.1), custom_call_target="tpu_custom_call" | custom-call | tf_op jit(solution)/shard_map/pallas_call | solution.py:38
  14.7 0.6 copy-done.7
  15.3 0.6 copy-done.8
  15.9 1.5 %shard_map.74 = f32[32,5,16,128]{3,2,1,0:T(8,128)} custom-call(f32[32,5,16,128]{3,2,1,0:T(8,128)} %shard_map.73.stencil_ref, f32[5,16,128]{2,1,0:T(8,128)} %copy-done.7, f32[5,16,128]{2,1,0:T(8,128)} %copy-done.8), custom_call_target="tpu_custom_call", output_to_operand_aliasing={{}: (0, {})} | custom-call | tf_op jit(solution)/shard_map/pallas_call | solution.py:56
  17.4 4.8 %all-to-all-start = ((f32[5,32,16,128]{3,2,0,1:T(8,128)}), f32[5,32,16,128]{3,2,0,1:T(8,128)S(1)}, u32[]{:S(2)}, u32[]{:S(2)}) async-start(f32[5,32,16,128]{3,2,0,1:T(8,128)} %bitcast.329), calls=%async_computation | async-start | bytes 2621440 | tf_op jit(solution)/shard_map/all_to_all | solution.py:166
  22.3 0.2 copy.27
  22.4 0.7 copy-done.5
  23.2 0.6 gather_fusion
  24.1 0.6 gather_fusion.1
  24.8 13.7 %all-to-all-done = f32[5,32,16,128]{3,2,0,1:T(8,128)S(1)} async-done(((f32[5,32,16,128]{3,2,0,1:T(8,128)}), f32[5,32,16,128]{3,2,0,1:T(8,128)S(1)}, u32[]{:S(2)}, u32[]{:S(2)}) %all-to-all-start) | async-done | bytes 1310752 | tf_op jit(solution)/shard_map/all_to_all | solution.py:166
  38.7 0.2 reshape.393
  39.0 4.9 %fusion = f32[40,8192]{1,0:T(8,128)S(1)} fusion(f32[40,8192,1]{1,0,2:T(8,128)S(1)} %reshape.393, f32[8,8192]{1,0:T(8,128)S(1)} %bitcast.336, f32[8,40,40]{1,0,2:T(8,128)S(1)} %select_bitcast_fusion), kind=kOutput, calls=%fused_computation.3 | convolution fusion | flops 634060800 | bytes 2934784 | tf_op jit(solution)/shard_map/dot_general | solution.py:176
  43.9 0.2 copy.23
  44.1 21.0 %all_to_all.25 = f32[40,4,16,128]{3,2,1,0:T(8,128)} all-to-all(f32[40,4,16,128]{3,2,1,0:T(8,128)S(1)} %bitcast.332), channel_id=1, replica_groups=mesh['mode'=8,'depth'=16] {'mode'}, dimensions={0} | all-to-all | bytes 2621440 | tf_op jit(solution)/shard_map/all_to_all | solution.py:184
  65.1 4.0 %shard_map.75 = (f32[5,32,16,128]{3,2,1,0:T(8,128)}, f32[32,16,128]{2,1,0:T(8,128)}, f32[32,16,128]{2,1,0:T(8,128)}, f32[16,12,16,128]{3,2,1,0:T(8,128)}) custom-call(f32[8,5,4,16,128]{4,3,2,1,0:T(8,128)} %bitcast.331, f32[32,16,128]{2,1,0:T(8,128)} %decay_ref.1), custom_call_target="tpu_custom_call" | custom-call | tf_op jit(solution)/shard_map/pallas_call | solution.py:128
  69.2 8.1 %all-to-all-start.2 = ((f32[16,12,16,128]{3,2,1,0:T(8,128)}), f32[16,12,16,128]{3,2,1,0:T(8,128)S(1)}, u32[]{:S(2)}, u32[]{:S(2)}) async-start(f32[16,12,16,128]{3,2,1,0:T(8,128)} %get-tuple-element.11), calls=%async_computation.2 | async-start | bytes 3145728 | tf_op jit(solution)/shard_map/all_to_all | solution.py:188
  77.3 22.8 %all-to-all-done.2 = f32[16,12,16,128]{3,2,1,0:T(8,128)S(1)} async-done(((f32[16,12,16,128]{3,2,1,0:T(8,128)}), f32[16,12,16,128]{3,2,1,0:T(8,128)S(1)}, u32[]{:S(2)}, u32[]{:S(2)}) %all-to-all-start.2) | async-done | bytes 1572896 | tf_op jit(solution)/shard_map/all_to_all | solution.py:188
  100.3 0.2 fusion.33
  100.5 0.9 copy-done.1
  101.5 1.2 %multiply_add_fusion = f32[5,32,16,128]{3,2,1,0:T(8,128)} fusion(f32[5,32,16,128]{3,2,1,0:T(8,128)S(1)} %copy-done.1, f32[5,16,128]{2,1,0:T(8,128)S(1)} %fusion.33, f32[32,16,128]{2,1,0:T(8,128)S(1)} %copy-done.4, f32[5,16,128]{2,1,0:T(8,128)S(1)} %select_select_fusion, f32[32,16,128]{2,1,0:T(8,128)S(1)} %copy-done.3), kind=kLoop, calls=%fused_computation.6 | loop fusion | flops 1310720 | bytes 3227648 | tf_op jit(solution)/shard_map/add | solution.py:210
  (29 shorter events, 0.9 us)
Async XLA Ops:
  0.8 13.9 %collective-permute-start = (f32[5,16,128]{2,1,0:T(8,128)S(1)}, f32[5,16,128]{2,1,0:T(8,128)S(1)}, u32[]{:S(2)}, u32[]{:S(2)}) collective-permute-start(f32[5,16,128]{2,1,0:T(8,128)S(1)} %get-tuple-element.45), channel_id=1, source_target_pairs={{0,1},{1,2},{2,3},{3,4},{4,5},{5,6},{6,7},{7,8},{8,9},{9,10},{10,1... | collective-permute-start | bytes 122888 | tf_op jit(solution)/shard_map/ppermute | solution.py:162
  7.7 7.0 %collective-permute-start.1 = (f32[5,16,128]{2,1,0:T(8,128)S(1)}, f32[5,16,128]{2,1,0:T(8,128)S(1)}, u32[]{:S(2)}, u32[]{:S(2)}) collective-permute-start(f32[5,16,128]{2,1,0:T(8,128)S(1)} %get-tuple-element.44), channel_id=1, source_target_pairs={{1,0},{2,1},{3,2},{4,3},{5,4},{6,5},{7,6},{8,7},{9,8},{10,9},{11,1... | collective-permute-start | bytes 122888 | tf_op jit(solution)/shard_map/ppermute | solution.py:163
  14.7 0.6 copy-start.7
  15.3 0.6 copy-start.8
  17.4 4.8 %copy-start = (f32[7,32,16,128]{3,2,1,0:T(8,128)S(1)}, f32[7,32,16,128]{3,2,1,0:T(8,128)}, u32[]{:S(2)}) copy-start(f32[7,32,16,128]{3,2,1,0:T(8,128)} %param.9) | copy-start | bytes 5505028
  17.4 4.8 %copy-start.2 = (f32[32,16,128]{2,1,0:T(8,128)S(1)}, f32[32,16,128]{2,1,0:T(8,128)}, u32[]{:S(2)}) copy-start(f32[32,16,128]{2,1,0:T(8,128)} %param.8) | copy-start | bytes 786436
  17.4 21.1 %all-to-all-start = ((f32[5,32,16,128]{3,2,0,1:T(8,128)}), f32[5,32,16,128]{3,2,0,1:T(8,128)S(1)}, u32[]{:S(2)}, u32[]{:S(2)}) async-start(f32[5,32,16,128]{3,2,0,1:T(8,128)} %bitcast.329), calls=%async_computation | async-start | bytes 2621440 | tf_op jit(solution)/shard_map/all_to_all | solution.py:166
  22.2 0.9 copy-start.5
  22.2 1.0 copy-start.6
  22.2 1.6 %copy-start.9 = (s32[40]{0:T(128)S(1)}, s32[40]{0:T(128)}, u32[]{:S(2)}) copy-start(s32[40]{0:T(128)} %param.13) | copy-start | bytes 484
  69.2 30.9 %all-to-all-start.2 = ((f32[16,12,16,128]{3,2,1,0:T(8,128)}), f32[16,12,16,128]{3,2,1,0:T(8,128)S(1)}, u32[]{:S(2)}, u32[]{:S(2)}) async-start(f32[16,12,16,128]{3,2,1,0:T(8,128)} %get-tuple-element.11), calls=%async_computation.2 | async-start | bytes 3145728 | tf_op jit(solution)/shard_map/all_to_all | solution.py:188
  100.1 1.3 %copy-start.1 = (f32[5,32,16,128]{3,2,1,0:T(8,128)S(1)}, f32[5,32,16,128]{3,2,1,0:T(8,128)}, u32[]{:S(2)}) copy-start(f32[5,32,16,128]{3,2,1,0:T(8,128)} %get-tuple-element.9) | copy-start | bytes 3932164
  100.1 1.3 %copy-start.3 = (f32[32,16,128]{2,1,0:T(8,128)S(1)}, f32[32,16,128]{2,1,0:T(8,128)}, u32[]{:S(2)}) copy-start(f32[32,16,128]{2,1,0:T(8,128)} %get-tuple-element.10) | copy-start | bytes 786436
  100.1 1.4 %copy-start.4 = (f32[32,16,128]{2,1,0:T(8,128)S(1)}, f32[32,16,128]{2,1,0:T(8,128)}, u32[]{:S(2)}) copy-start(f32[32,16,128]{2,1,0:T(8,128)} %get-tuple-element.12) | copy-start | bytes 786436

commit v10 on v9

--- a/solution.py
+++ b/solution.py
@@ -88,6 +88,7 @@
         rows,
         forward_row,
         (jnp.zeros((modes,) + lateral, jnp.float32), jnp.ones(lateral, jnp.float32)),
+        unroll=True,
     )
 
     def backward_row(i, carried):
@@ -111,6 +112,7 @@
             jnp.zeros(lateral, jnp.float32),
             jnp.ones(lateral, jnp.float32),
         ),
+        unroll=True,
     )
     for copy in range(summary_ref.shape[0]):
         summary_ref[copy, 0] = tail

time: 103 us -> 102 us (level)
  no operation moved by 1% of the time
where the time goes in v10:
time: 102 us
  waiting for transfers between devices  36.6 us (36%)
  starting transfers between devices  21.7 us (21%)
  blocking collectives  21 us (21%)
  Pallas kernels  8.92 us (9%)
  local copies, waits for them, and re-layouts  5.96 us (6%)
  matrix products  4.91 us (5%)
  other arithmetic  2.52 us (2%)
    all_to_all x1, waiting for transfers between devices, local(): summaries = lax.all_to_all(copies, 'depth', 0, 0, tiled=True)  22.8 us
    all_to_all x1, blocking collectives, local(): mixed_field = lax.all_to_all(mixed_rows, 'mode', 0, 0, tiled=True)  21 us
    all_to_all x1, waiting for transfers between devices, local(): stencil_rows = lax.all_to_all(stencil, 'mode', 1, 0, tiled=True)  13.7 us
    all_to_all x1, starting transfers between devices, local(): summaries = lax.all_to_all(copies, 'depth', 0, 0, tiled=True)  8.09 us
    ppermute x1, starting transfers between devices, local(): lax.ppermute(fields[:, -1], 'depth', [(i, i + 1) for i in range(slabs - 1)])  6.88 us
    dot_general x1, matrix products, local(): jnp.dot(table_rows, stencil_rows, precision=lax.Precision.HIGH, preferred...  4.91 us
    all_to_all x1, starting transfers between devices, local(): stencil_rows = lax.all_to_all(stencil, 'mode', 1, 0, tiled=True)  4.78 us
    pallas_call x1, Pallas kernels, slab_stencil(): pl.pallas_call(stencil_kernel, grid=(modes,), in_specs=[pl.BlockSpec((1,...  4.41 us
  transfers between devices with their start and end apart: 4, of which 2 were waited for; matrix products, arithmetic and copies ran while one was open for 2% of the time, Pallas kernels for 4%

profile of v10, /device:TPU:1, one launch (start us, length us, event | category | flops | bytes accessed | tf_op | source)
XLA Modules:
  0.0 101.8 jit_solution(2003270298000450051)
XLA Ops:
  0.0 0.8 slice_bitcast_fusion.30
  0.8 6.9 %collective-permute-start = (f32[5,16,128]{2,1,0:T(8,128)S(1)}, f32[5,16,128]{2,1,0:T(8,128)S(1)}, u32[]{:S(2)}, u32[]{:S(2)}) collective-permute-start(f32[5,16,128]{2,1,0:T(8,128)S(1)} %get-tuple-element.45), channel_id=1, source_target_pairs={{0,1},{1,2},{2,3},{3,4},{4,5},{5,6},{6,7},{7,8},{8,9},{9,10},{10,1... | collective-permute-start | bytes 122888 | tf_op jit(solution)/shard_map/ppermute | solution.py:164
  7.7 1.9 %collective-permute-start.1 = (f32[5,16,128]{2,1,0:T(8,128)S(1)}, f32[5,16,128]{2,1,0:T(8,128)S(1)}, u32[]{:S(2)}, u32[]{:S(2)}) collective-permute-start(f32[5,16,128]{2,1,0:T(8,128)S(1)} %get-tuple-element.44), channel_id=1, source_target_pairs={{1,0},{2,1},{3,2},{4,3},{5,4},{6,5},{7,6},{8,7},{9,8},{10,9},{11,1... | collective-permute-start | bytes 122888 | tf_op jit(solution)/shard_map/ppermute | solution.py:165
  9.6 0.7 compare_select_fusion
  10.3 4.4 %shard_map.73.stencil_ref = f32[32,5,16,128]{3,2,1,0:T(8,128)} custom-call(f32[5,32,16,128]{3,2,1,0:T(8,128)} %fields_ref.1), custom_call_target="tpu_custom_call" | custom-call | tf_op jit(solution)/shard_map/pallas_call | solution.py:38
  14.7 0.6 copy-done.7
  15.3 0.6 copy-done.8
  15.9 1.5 %shard_map.74 = f32[32,5,16,128]{3,2,1,0:T(8,128)} custom-call(f32[32,5,16,128]{3,2,1,0:T(8,128)} %shard_map.73.stencil_ref, f32[5,16,128]{2,1,0:T(8,128)} %copy-done.7, f32[5,16,128]{2,1,0:T(8,128)} %copy-done.8), custom_call_target="tpu_custom_call", output_to_operand_aliasing={{}: (0, {})} | custom-call | tf_op jit(solution)/shard_map/pallas_call | solution.py:56
  17.4 4.8 %all-to-all-start = ((f32[5,32,16,128]{3,2,0,1:T(8,128)}), f32[5,32,16,128]{3,2,0,1:T(8,128)S(1)}, u32[]{:S(2)}, u32[]{:S(2)}) async-start(f32[5,32,16,128]{3,2,0,1:T(8,128)} %bitcast.329), calls=%async_computation | async-start | bytes 2621440 | tf_op jit(solution)/shard_map/all_to_all | solution.py:168
  22.3 0.2 copy.27
  22.4 0.7 copy-done.5
  23.2 0.6 gather_fusion
  24.1 0.6 gather_fusion.1
  24.8 13.7 %all-to-all-done = f32[5,32,16,128]{3,2,0,1:T(8,128)S(1)} async-done(((f32[5,32,16,128]{3,2,0,1:T(8,128)}), f32[5,32,16,128]{3,2,0,1:T(8,128)S(1)}, u32[]{:S(2)}, u32[]{:S(2)}) %all-to-all-start) | async-done | bytes 1310752 | tf_op jit(solution)/shard_map/all_to_all | solution.py:168
  38.7 0.2 reshape.393
  39.0 4.9 %fusion = f32[40,8192]{1,0:T(8,128)S(1)} fusion(f32[40,8192,1]{1,0,2:T(8,128)S(1)} %reshape.393, f32[8,8192]{1,0:T(8,128)S(1)} %bitcast.336, f32[8,40,40]{1,0,2:T(8,128)S(1)} %select_bitcast_fusion), kind=kOutput, calls=%fused_computation.3 | convolution fusion | flops 634060800 | bytes 2934784 | tf_op jit(solution)/shard_map/dot_general | solution.py:178
  43.9 0.2 copy.23
  44.1 21.0 %all_to_all.25 = f32[40,4,16,128]{3,2,1,0:T(8,128)} all-to-all(f32[40,4,16,128]{3,2,1,0:T(8,128)S(1)} %bitcast.332), channel_id=1, replica_groups=mesh['mode'=8,'depth'=16] {'mode'}, dimensions={0} | all-to-all | bytes 2621440 | tf_op jit(solution)/shard_map/all_to_all | solution.py:186
  65.1 3.0 %shard_map.75 = (f32[5,32,16,128]{3,2,1,0:T(8,128)}, f32[32,16,128]{2,1,0:T(8,128)}, f32[32,16,128]{2,1,0:T(8,128)}, f32[16,12,16,128]{3,2,1,0:T(8,128)}) custom-call(f32[8,5,4,16,128]{4,3,2,1,0:T(8,128)} %bitcast.331, f32[32,16,128]{2,1,0:T(8,128)} %decay_ref.1), custom_call_target="tpu_custom_call" | custom-call | tf_op jit(solution)/shard_map/pallas_call | solution.py:130
  68.2 8.1 %all-to-all-start.2 = ((f32[16,12,16,128]{3,2,1,0:T(8,128)}), f32[16,12,16,128]{3,2,1,0:T(8,128)S(1)}, u32[]{:S(2)}, u32[]{:S(2)}) async-start(f32[16,12,16,128]{3,2,1,0:T(8,128)} %get-tuple-element.11), calls=%async_computation.2 | async-start | bytes 3145728 | tf_op jit(solution)/shard_map/all_to_all | solution.py:190
  76.3 22.8 %all-to-all-done.2 = f32[16,12,16,128]{3,2,1,0:T(8,128)S(1)} async-done(((f32[16,12,16,128]{3,2,1,0:T(8,128)}), f32[16,12,16,128]{3,2,1,0:T(8,128)S(1)}, u32[]{:S(2)}, u32[]{:S(2)}) %all-to-all-start.2) | async-done | bytes 1572896 | tf_op jit(solution)/shard_map/all_to_all | solution.py:190
  99.3 0.2 fusion.33
  99.5 0.9 copy-done.1
  100.6 1.2 %multiply_add_fusion = f32[5,32,16,128]{3,2,1,0:T(8,128)} fusion(f32[5,32,16,128]{3,2,1,0:T(8,128)S(1)} %copy-done.1, f32[5,16,128]{2,1,0:T(8,128)S(1)} %fusion.33, f32[32,16,128]{2,1,0:T(8,128)S(1)} %copy-done.4, f32[5,16,128]{2,1,0:T(8,128)S(1)} %select_select_fusion, f32[32,16,128]{2,1,0:T(8,128)S(1)} %copy-done.3), kind=kLoop, calls=%fused_computation.6 | loop fusion | flops 1310720 | bytes 3227648 | tf_op jit(solution)/shard_map/add | solution.py:212
  (29 shorter events, 0.9 us)
Async XLA Ops:
  0.8 13.9 %collective-permute-start = (f32[5,16,128]{2,1,0:T(8,128)S(1)}, f32[5,16,128]{2,1,0:T(8,128)S(1)}, u32[]{:S(2)}, u32[]{:S(2)}) collective-permute-start(f32[5,16,128]{2,1,0:T(8,128)S(1)} %get-tuple-element.45), channel_id=1, source_target_pairs={{0,1},{1,2},{2,3},{3,4},{4,5},{5,6},{6,7},{7,8},{8,9},{9,10},{10,1... | collective-permute-start | bytes 122888 | tf_op jit(solution)/shard_map/ppermute | solution.py:164
  7.7 7.0 %collective-permute-start.1 = (f32[5,16,128]{2,1,0:T(8,128)S(1)}, f32[5,16,128]{2,1,0:T(8,128)S(1)}, u32[]{:S(2)}, u32[]{:S(2)}) collective-permute-start(f32[5,16,128]{2,1,0:T(8,128)S(1)} %get-tuple-element.44), channel_id=1, source_target_pairs={{1,0},{2,1},{3,2},{4,3},{5,4},{6,5},{7,6},{8,7},{9,8},{10,9},{11,1... | collective-permute-start | bytes 122888 | tf_op jit(solution)/shard_map/ppermute | solution.py:165
  14.7 0.6 copy-start.7
  15.3 0.6 copy-start.8
  17.4 4.8 %copy-start = (f32[7,32,16,128]{3,2,1,0:T(8,128)S(1)}, f32[7,32,16,128]{3,2,1,0:T(8,128)}, u32[]{:S(2)}) copy-start(f32[7,32,16,128]{3,2,1,0:T(8,128)} %param.9) | copy-start | bytes 5505028
  17.4 4.8 %copy-start.2 = (f32[32,16,128]{2,1,0:T(8,128)S(1)}, f32[32,16,128]{2,1,0:T(8,128)}, u32[]{:S(2)}) copy-start(f32[32,16,128]{2,1,0:T(8,128)} %param.8) | copy-start | bytes 786436
  17.4 21.1 %all-to-all-start = ((f32[5,32,16,128]{3,2,0,1:T(8,128)}), f32[5,32,16,128]{3,2,0,1:T(8,128)S(1)}, u32[]{:S(2)}, u32[]{:S(2)}) async-start(f32[5,32,16,128]{3,2,0,1:T(8,128)} %bitcast.329), calls=%async_computation | async-start | bytes 2621440 | tf_op jit(solution)/shard_map/all_to_all | solution.py:168
  22.2 0.9 copy-start.5
  22.2 1.0 copy-start.6
  22.2 1.6 %copy-start.9 = (s32[40]{0:T(128)S(1)}, s32[40]{0:T(128)}, u32[]{:S(2)}) copy-start(s32[40]{0:T(128)} %param.13) | copy-start | bytes 484
  68.2 30.9 %all-to-all-start.2 = ((f32[16,12,16,128]{3,2,1,0:T(8,128)}), f32[16,12,16,128]{3,2,1,0:T(8,128)S(1)}, u32[]{:S(2)}, u32[]{:S(2)}) async-start(f32[16,12,16,128]{3,2,1,0:T(8,128)} %get-tuple-element.11), calls=%async_computation.2 | async-start | bytes 3145728 | tf_op jit(solution)/shard_map/all_to_all | solution.py:190
  99.1 1.3 %copy-start.1 = (f32[5,32,16,128]{3,2,1,0:T(8,128)S(1)}, f32[5,32,16,128]{3,2,1,0:T(8,128)}, u32[]{:S(2)}) copy-start(f32[5,32,16,128]{3,2,1,0:T(8,128)} %get-tuple-element.9) | copy-start | bytes 3932164
  99.1 1.3 %copy-start.3 = (f32[32,16,128]{2,1,0:T(8,128)S(1)}, f32[32,16,128]{2,1,0:T(8,128)}, u32[]{:S(2)}) copy-start(f32[32,16,128]{2,1,0:T(8,128)} %get-tuple-element.10) | copy-start | bytes 786436
  99.1 1.4 %copy-start.4 = (f32[32,16,128]{2,1,0:T(8,128)S(1)}, f32[32,16,128]{2,1,0:T(8,128)}, u32[]{:S(2)}) copy-start(f32[32,16,128]{2,1,0:T(8,128)} %get-tuple-element.12) | copy-start | bytes 786436

commit v11 on v10

--- a/solution.py
+++ b/solution.py
@@ -16,20 +16,21 @@
 
 
 def stencil_kernel(fields_ref, out_ref):
-    rows = fields_ref.shape[1]
+    modes, rows = fields_ref.shape[0], fields_ref.shape[1]
     plane = fields_ref.shape[2:]
     masks = neighbour_masks(plane, 0) + neighbour_masks(plane, 1)
     axes = [0, 0, 1, 1]
-    for z in range(rows):
-        centre = fields_ref[0, z]
-        beside = jnp.zeros_like(centre)
-        if z + 1 < rows:
-            beside = beside + fields_ref[0, z + 1]
-        if z > 0:
-            beside = beside + fields_ref[0, z - 1]
-        for axis, (shift, inside) in zip(axes, masks):
-            beside = beside + jnp.where(inside, pltpu.roll(centre, shift, axis), 0.0)
-        out_ref[z, 0] = 6.0 * centre - beside
+    for mode in range(modes):
+        for z in range(rows):
+            centre = fields_ref[mode, z]
+            beside = jnp.zeros_like(centre)
+            if z + 1 < rows:
+                beside = beside + fields_ref[mode, z + 1]
+            if z > 0:
+                beside = beside + fields_ref[mode, z - 1]
+            for axis, (shift, inside) in zip(axes, masks):
+                beside = beside + jnp.where(inside, pltpu.roll(centre, shift, axis), 0.0)
+            out_ref[z, mode] = 6.0 * centre - beside
 
 
 def slab_stencil(fields):
@@ -37,9 +38,6 @@
     plane = fields.shape[2:]
     return pl.pallas_call(
         stencil_kernel,
-        grid=(modes,),
-        in_specs=[pl.BlockSpec((1, rows) + plane, lambda i: (i, 0, 0, 0))],
-        out_specs=pl.BlockSpec((rows, 1) + plane, lambda i: (0, i, 0, 0)),
         out_shape=jax.ShapeDtypeStruct((rows, modes) + plane, jnp.float32),
     )(fields)
 

time: 102 us -> 103 us (level)
  starting transfers between devices: 21.7 us -> 23.7 us
  Pallas kernels: 8.92 us -> 7.67 us
    all_to_all x1, starting transfers between devices: 8.09 us -> 10.1 us  [local(): summaries = lax.all_to_all(copies, 'depth', 0, 0, tiled=True)]
    pallas_call x1, Pallas kernels: 4.41 us -> 3.15 us  [slab_stencil(): pl.pallas_call(stencil_kernel, out_shape=jax.ShapeDtypeStruct((rows, mode...]
    ppermute x1, waiting for transfers between devices: 0.01 us -> 1.08 us  [local(): lax.ppermute(fields[:, 0], 'depth', [(i + 1, i) for i in range(slabs - 1)])]
  transfers between devices with their start and end apart: 4 -> 4, of which waited for: 2 -> 3; matrix products, arithmetic and copies ran while one was open for 2% -> 2% of each run, Pallas kernels for 4% -> 3%
where the time goes in v11:
time: 103 us
  waiting for transfers between devices  37.3 us (36%)
  starting transfers between devices  23.7 us (23%)
  blocking collectives  21 us (20%)
  Pallas kernels  7.67 us (7%)
  local copies, waits for them, and re-layouts  5.36 us (5%)
  matrix products  4.91 us (5%)
  other arithmetic  2.52 us (2%)
    all_to_all x1, waiting for transfers between devices, local(): summaries = lax.all_to_all(copies, 'depth', 0, 0, tiled=True)  22.8 us
    all_to_all x1, blocking collectives, local(): mixed_field = lax.all_to_all(mixed_rows, 'mode', 0, 0, tiled=True)  21 us
    all_to_all x1, waiting for transfers between devices, local(): stencil_rows = lax.all_to_all(stencil, 'mode', 1, 0, tiled=True)  13.4 us
    all_to_all x1, starting transfers between devices, local(): summaries = lax.all_to_all(copies, 'depth', 0, 0, tiled=True)  10.1 us
    ppermute x1, starting transfers between devices, local(): lax.ppermute(fields[:, -1], 'depth', [(i, i + 1) for i in range(slabs - 1)])  6.88 us
    dot_general x1, matrix products, local(): jnp.dot(table_rows, stencil_rows, precision=lax.Precision.HIGH, preferred...  4.91 us
    all_to_all x1, starting transfers between devices, local(): stencil_rows = lax.all_to_all(stencil, 'mode', 1, 0, tiled=True)  4.78 us
    pallas_call x1, Pallas kernels, slab_stencil(): pl.pallas_call(stencil_kernel, out_shape=jax.ShapeDtypeStruct((rows, mode...  3.15 us
  transfers between devices with their start and end apart: 4, of which 3 were waited for; matrix products, arithmetic and copies ran while one was open for 2% of the time, Pallas kernels for 3%

profile of v11, /device:TPU:1, one launch (start us, length us, event | category | flops | bytes accessed | tf_op | source)
XLA Modules:
  0.0 102.7 jit_solution(8682910933832685282)
XLA Ops:
  0.0 0.8 slice_bitcast_fusion.30
  0.8 6.9 %collective-permute-start = (f32[5,16,128]{2,1,0:T(8,128)S(1)}, f32[5,16,128]{2,1,0:T(8,128)S(1)}, u32[]{:S(2)}, u32[]{:S(2)}) collective-permute-start(f32[5,16,128]{2,1,0:T(8,128)S(1)} %get-tuple-element.45), channel_id=1, source_target_pairs={{0,1},{1,2},{2,3},{3,4},{4,5},{5,6},{6,7},{7,8},{8,9},{9,10},{10,1... | collective-permute-start | bytes 122888 | tf_op jit(solution)/shard_map/ppermute | solution.py:162
  7.7 1.9 %collective-permute-start.1 = (f32[5,16,128]{2,1,0:T(8,128)S(1)}, f32[5,16,128]{2,1,0:T(8,128)S(1)}, u32[]{:S(2)}, u32[]{:S(2)}) collective-permute-start(f32[5,16,128]{2,1,0:T(8,128)S(1)} %get-tuple-element.44), channel_id=1, source_target_pairs={{1,0},{2,1},{3,2},{4,3},{5,4},{6,5},{7,6},{8,7},{9,8},{10,9},{11,1... | collective-permute-start | bytes 122888 | tf_op jit(solution)/shard_map/ppermute | solution.py:163
  9.6 0.7 compare_select_fusion
  10.3 3.2 %shard_map.73.stencil_ref = f32[32,5,16,128]{3,2,1,0:T(8,128)} custom-call(f32[5,32,16,128]{3,2,1,0:T(8,128)} %fields_ref.1), custom_call_target="tpu_custom_call" | custom-call | tf_op jit(solution)/shard_map/pallas_call | solution.py:39
  13.4 1.1 %collective-permute-done.1.above_ref = f32[5,16,128]{2,1,0:T(8,128)S(1)} collective-permute-done((f32[5,16,128]{2,1,0:T(8,128)S(1)}, f32[5,16,128]{2,1,0:T(8,128)S(1)}, u32[]{:S(2)}, u32[]{:S(2)}) %collective-permute-start.1) | collective-permute-done | bytes 40992 | tf_op jit(solution)/shard_map/ppermute | solution.py:163
  14.5 0.6 copy-done.8
  15.1 1.5 %shard_map.74 = f32[32,5,16,128]{3,2,1,0:T(8,128)} custom-call(f32[32,5,16,128]{3,2,1,0:T(8,128)} %shard_map.73.stencil_ref, f32[5,16,128]{2,1,0:T(8,128)} %copy-done.7, f32[5,16,128]{2,1,0:T(8,128)} %copy-done.8), custom_call_target="tpu_custom_call", output_to_operand_aliasing={{}: (0, {})} | custom-call | tf_op jit(solution)/shard_map/pallas_call | solution.py:54
  16.6 4.8 %all-to-all-start = ((f32[5,32,16,128]{3,2,0,1:T(8,128)}), f32[5,32,16,128]{3,2,0,1:T(8,128)S(1)}, u32[]{:S(2)}, u32[]{:S(2)}) async-start(f32[5,32,16,128]{3,2,0,1:T(8,128)} %bitcast.329), calls=%async_computation | async-start | bytes 2621440 | tf_op jit(solution)/shard_map/all_to_all | solution.py:166
  21.5 0.2 copy.27
  21.6 0.7 copy-done.5
  22.4 0.6 gather_fusion
  23.3 0.6 gather_fusion.1
  24.0 13.4 %all-to-all-done = f32[5,32,16,128]{3,2,0,1:T(8,128)S(1)} async-done(((f32[5,32,16,128]{3,2,0,1:T(8,128)}), f32[5,32,16,128]{3,2,0,1:T(8,128)S(1)}, u32[]{:S(2)}, u32[]{:S(2)}) %all-to-all-start) | async-done | bytes 1310752 | tf_op jit(solution)/shard_map/all_to_all | solution.py:166
  37.6 0.2 reshape.393
  37.8 4.9 %fusion = f32[40,8192]{1,0:T(8,128)S(1)} fusion(f32[40,8192,1]{1,0,2:T(8,128)S(1)} %reshape.393, f32[8,8192]{1,0:T(8,128)S(1)} %bitcast.336, f32[8,40,40]{1,0,2:T(8,128)S(1)} %select_bitcast_fusion), kind=kOutput, calls=%fused_computation.3 | convolution fusion | flops 634060800 | bytes 2934784 | tf_op jit(solution)/shard_map/dot_general | solution.py:176
  42.8 0.2 copy.23
  43.0 21.0 %all_to_all.25 = f32[40,4,16,128]{3,2,1,0:T(8,128)} all-to-all(f32[40,4,16,128]{3,2,1,0:T(8,128)S(1)} %bitcast.332), channel_id=1, replica_groups=mesh['mode'=8,'depth'=16] {'mode'}, dimensions={0} | all-to-all | bytes 2621440 | tf_op jit(solution)/shard_map/all_to_all | solution.py:184
  64.0 3.0 %shard_map.75 = (f32[5,32,16,128]{3,2,1,0:T(8,128)}, f32[32,16,128]{2,1,0:T(8,128)}, f32[32,16,128]{2,1,0:T(8,128)}, f32[16,12,16,128]{3,2,1,0:T(8,128)}) custom-call(f32[8,5,4,16,128]{4,3,2,1,0:T(8,128)} %bitcast.331, f32[32,16,128]{2,1,0:T(8,128)} %decay_ref.1), custom_call_target="tpu_custom_call" | custom-call | tf_op jit(solution)/shard_map/pallas_call | solution.py:128
  67.1 10.1 %all-to-all-start.2 = ((f32[16,12,16,128]{3,2,1,0:T(8,128)}), f32[16,12,16,128]{3,2,1,0:T(8,128)S(1)}, u32[]{:S(2)}, u32[]{:S(2)}) async-start(f32[16,12,16,128]{3,2,1,0:T(8,128)} %get-tuple-element.11), calls=%async_computation.2 | async-start | bytes 3145728 | tf_op jit(solution)/shard_map/all_to_all | solution.py:188
  77.2 22.8 %all-to-all-done.2 = f32[16,12,16,128]{3,2,1,0:T(8,128)S(1)} async-done(((f32[16,12,16,128]{3,2,1,0:T(8,128)}), f32[16,12,16,128]{3,2,1,0:T(8,128)S(1)}, u32[]{:S(2)}, u32[]{:S(2)}) %all-to-all-start.2) | async-done | bytes 1572896 | tf_op jit(solution)/shard_map/all_to_all | solution.py:188
  100.2 0.2 fusion.33
  100.4 0.9 copy-done.1
  101.5 1.2 %multiply_add_fusion = f32[5,32,16,128]{3,2,1,0:T(8,128)} fusion(f32[5,32,16,128]{3,2,1,0:T(8,128)S(1)} %copy-done.1, f32[5,16,128]{2,1,0:T(8,128)S(1)} %fusion.33, f32[32,16,128]{2,1,0:T(8,128)S(1)} %copy-done.4, f32[5,16,128]{2,1,0:T(8,128)S(1)} %select_select_fusion, f32[32,16,128]{2,1,0:T(8,128)S(1)} %copy-done.3), kind=kLoop, calls=%fused_computation.6 | loop fusion | flops 1310720 | bytes 3227648 | tf_op jit(solution)/shard_map/add | solution.py:210
  (29 shorter events, 0.9 us)
Async XLA Ops:
  0.8 12.6 %collective-permute-start = (f32[5,16,128]{2,1,0:T(8,128)S(1)}, f32[5,16,128]{2,1,0:T(8,128)S(1)}, u32[]{:S(2)}, u32[]{:S(2)}) collective-permute-start(f32[5,16,128]{2,1,0:T(8,128)S(1)} %get-tuple-element.45), channel_id=1, source_target_pairs={{0,1},{1,2},{2,3},{3,4},{4,5},{5,6},{6,7},{7,8},{8,9},{9,10},{10,1... | collective-permute-start | bytes 122888 | tf_op jit(solution)/shard_map/ppermute | solution.py:162
  7.7 6.8 %collective-permute-start.1 = (f32[5,16,128]{2,1,0:T(8,128)S(1)}, f32[5,16,128]{2,1,0:T(8,128)S(1)}, u32[]{:S(2)}, u32[]{:S(2)}) collective-permute-start(f32[5,16,128]{2,1,0:T(8,128)S(1)} %get-tuple-element.44), channel_id=1, source_target_pairs={{1,0},{2,1},{3,2},{4,3},{5,4},{6,5},{7,6},{8,7},{9,8},{10,9},{11,1... | collective-permute-start | bytes 122888 | tf_op jit(solution)/shard_map/ppermute | solution.py:163
  13.4 1.1 %copy-start.7 = (f32[5,16,128]{2,1,0:T(8,128)}, f32[5,16,128]{2,1,0:T(8,128)S(1)}, u32[]{:S(2)}) copy-start(f32[5,16,128]{2,1,0:T(8,128)S(1)} %collective-permute-done.below_ref) | copy-start | bytes 122884
  14.5 0.6 copy-start.8
  16.6 4.8 %copy-start = (f32[7,32,16,128]{3,2,1,0:T(8,128)S(1)}, f32[7,32,16,128]{3,2,1,0:T(8,128)}, u32[]{:S(2)}) copy-start(f32[7,32,16,128]{3,2,1,0:T(8,128)} %param.9) | copy-start | bytes 5505028
  16.6 4.8 %copy-start.2 = (f32[32,16,128]{2,1,0:T(8,128)S(1)}, f32[32,16,128]{2,1,0:T(8,128)}, u32[]{:S(2)}) copy-start(f32[32,16,128]{2,1,0:T(8,128)} %param.8) | copy-start | bytes 786436
  16.6 20.8 %all-to-all-start = ((f32[5,32,16,128]{3,2,0,1:T(8,128)}), f32[5,32,16,128]{3,2,0,1:T(8,128)S(1)}, u32[]{:S(2)}, u32[]{:S(2)}) async-start(f32[5,32,16,128]{3,2,0,1:T(8,128)} %bitcast.329), calls=%async_computation | async-start | bytes 2621440 | tf_op jit(solution)/shard_map/all_to_all | solution.py:166
  21.4 0.9 copy-start.5
  21.4 1.0 copy-start.6
  21.5 1.6 %copy-start.9 = (s32[40]{0:T(128)S(1)}, s32[40]{0:T(128)}, u32[]{:S(2)}) copy-start(s32[40]{0:T(128)} %param.13) | copy-start | bytes 484
  67.1 32.9 %all-to-all-start.2 = ((f32[16,12,16,128]{3,2,1,0:T(8,128)}), f32[16,12,16,128]{3,2,1,0:T(8,128)S(1)}, u32[]{:S(2)}, u32[]{:S(2)}) async-start(f32[16,12,16,128]{3,2,1,0:T(8,128)} %get-tuple-element.11), calls=%async_computation.2 | async-start | bytes 3145728 | tf_op jit(solution)/shard_map/all_to_all | solution.py:188
  100.0 1.3 %copy-start.1 = (f32[5,32,16,128]{3,2,1,0:T(8,128)S(1)}, f32[5,32,16,128]{3,2,1,0:T(8,128)}, u32[]{:S(2)}) copy-start(f32[5,32,16,128]{3,2,1,0:T(8,128)} %get-tuple-element.9) | copy-start | bytes 3932164
  100.1 1.3 %copy-start.3 = (f32[32,16,128]{2,1,0:T(8,128)S(1)}, f32[32,16,128]{2,1,0:T(8,128)}, u32[]{:S(2)}) copy-start(f32[32,16,128]{2,1,0:T(8,128)} %get-tuple-element.10) | copy-start | bytes 786436
  100.1 1.4 %copy-start.4 = (f32[32,16,128]{2,1,0:T(8,128)S(1)}, f32[32,16,128]{2,1,0:T(8,128)}, u32[]{:S(2)}) copy-start(f32[32,16,128]{2,1,0:T(8,128)} %get-tuple-element.12) | copy-start | bytes 786436

commit v12 on v9

--- a/solution.py
+++ b/solution.py
@@ -67,84 +67,105 @@
     )(stencil, below, above)
 
 
-def sweep_kernel(mixed_ref, decay_ref, back_ref, coupled_ref, tail_ref, summary_ref):
+def decay_kernel(decay_ref, coupled_ref, tail_ref):
+    rows = decay_ref.shape[0]
+    lateral = decay_ref.shape[1:]
+
+    def forward_row(z, ratio):
+        d = decay_ref[z]
+        ratio = d * ratio
+        coupled_ref[z] = jnp.sqrt(1.0 - d * d) * ratio
+        return ratio
+
+    lax.fori_loop(0, rows, forward_row, jnp.ones(lateral, jnp.float32), unroll=True)
+
+    def backward_row(i, carried):
+        z = rows - 1 - i
+        coupled, tail = carried
+        d = decay_ref[z]
+        coupled = d * coupled + coupled_ref[z]
+        tail = d * tail
+        coupled_ref[z] = coupled
+        tail_ref[z] = tail
+        return coupled, tail
+
+    lax.fori_loop(
+        0,
+        rows,
+        backward_row,
+        (jnp.zeros(lateral, jnp.float32), jnp.ones(lateral, jnp.float32)),
+        unroll=True,
+    )
+
+
+def decay_weights(decay):
+    return pl.pallas_call(
+        decay_kernel,
+        out_shape=(
+            jax.ShapeDtypeStruct(decay.shape, jnp.float32),
+            jax.ShapeDtypeStruct(decay.shape, jnp.float32),
+        ),
+    )(decay)
+
+
+def sweep_kernel(mixed_ref, decay_ref, coupled_ref, tail_ref, back_ref, summary_ref):
     rows = decay_ref.shape[0]
     chunk = mixed_ref.shape[2]
-
-    def forward_row(z, carried):
-        state, ratio = carried
+    lateral = decay_ref.shape[1:]
+    modes = mixed_ref.shape[1]
+
+    def forward_row(z, state):
         d = decay_ref[z]
         g = jnp.sqrt(1.0 - d * d)
         state = d[None] * state + g[None] * mixed_ref[z // chunk, :, z % chunk]
-        ratio = d * ratio
         back_ref[:, z] = g[None] * state
-        coupled_ref[z] = g * ratio
-        return state, ratio
-
-    lateral = decay_ref.shape[1:]
-    modes = mixed_ref.shape[1]
-    state, _ = lax.fori_loop(
-        0,
-        rows,
-        forward_row,
-        (jnp.zeros((modes,) + lateral, jnp.float32), jnp.ones(lateral, jnp.float32)),
-    )
-
-    def backward_row(i, carried):
+        return state
+
+    state = lax.fori_loop(
+        0, rows, forward_row, jnp.zeros((modes,) + lateral, jnp.float32), unroll=True
+    )
+
+    def backward_row(i, back):
         z = rows - 1 - i
-        back, coupled, tail = carried
-        d = decay_ref[z]
-        back = d[None] * back + back_ref[:, z]
-        coupled = d * coupled + coupled_ref[z]
-        tail = d * tail
+        back = decay_ref[z][None] * back + back_ref[:, z]
         back_ref[:, z] = back
-        coupled_ref[z] = coupled
-        tail_ref[z] = tail
-        return back, coupled, tail
-
-    back, coupled, tail = lax.fori_loop(
-        0,
-        rows,
-        backward_row,
-        (
-            jnp.zeros((modes,) + lateral, jnp.float32),
-            jnp.zeros(lateral, jnp.float32),
-            jnp.ones(lateral, jnp.float32),
-        ),
+        return back
+
+    back = lax.fori_loop(
+        0, rows, backward_row, jnp.zeros((modes,) + lateral, jnp.float32), unroll=True
     )
     for copy in range(summary_ref.shape[0]):
-        summary_ref[copy, 0] = tail
-        summary_ref[copy, 1] = coupled
+        summary_ref[copy, 0] = tail_ref[0]
+        summary_ref[copy, 1] = coupled_ref[0]
         summary_ref[copy, 2 : 2 + modes] = state
         summary_ref[copy, 2 + modes :] = back
 
 
-def local_sweeps(mixed, decay, copies):
+def local_sweeps(mixed, decay, coupled, tail, copies):
     groups, modes, chunk = mixed.shape[0], mixed.shape[1], mixed.shape[2]
     rows = decay.shape[0]
     lateral = decay.shape[1:]
     parts = 2
     half = (lateral[0] // parts, lateral[1])
+    by_row = pl.BlockSpec((rows,) + half, lambda i: (0, i, 0))
     return pl.pallas_call(
         sweep_kernel,
         grid=(parts,),
         in_specs=[
             pl.BlockSpec((groups, modes, chunk) + half, lambda i: (0, 0, 0, i, 0)),
-            pl.BlockSpec((rows,) + half, lambda i: (0, i, 0)),
+            by_row,
+            by_row,
+            by_row,
         ],
         out_specs=(
             pl.BlockSpec((modes, rows) + half, lambda i: (0, 0, i, 0)),
-            pl.BlockSpec((rows,) + half, lambda i: (0, i, 0)),
-            pl.BlockSpec((rows,) + half, lambda i: (0, i, 0)),
             pl.BlockSpec((copies, 2 + 2 * modes) + half, lambda i: (0, 0, i, 0)),
         ),
         out_shape=(
             jax.ShapeDtypeStruct((modes, rows) + lateral, jnp.float32),
-            jax.ShapeDtypeStruct(decay.shape, jnp.float32),
-            jax.ShapeDtypeStruct(decay.shape, jnp.float32),
             jax.ShapeDtypeStruct((copies, 2 + 2 * modes) + lateral, jnp.float32),
         ),
-    )(mixed, decay)
+    )(mixed, decay, coupled, tail)
 
 
 def local(fields, mean_field, kl_modes, decay, coupling, pattern, mode_order):
@@ -184,7 +205,8 @@
     mixed_field = lax.all_to_all(mixed_rows, "mode", 0, 0, tiled=True)
     mixed_field = mixed_field.reshape((groups, local_modes, chunk) + lateral)
 
-    back, coupled, tail, copies = local_sweeps(mixed_field, decay, slabs)
+    coupled, tail = decay_weights(decay)
+    back, copies = local_sweeps(mixed_field, decay, coupled, tail, slabs)
     summaries = lax.all_to_all(copies, "depth", 0, 0, tiled=True)
     ratio_all = summaries[:, 0]
     coupled_all = summaries[:, 1]

time: 103 us -> 105 us (1.019)
  blocking collectives: 21 us -> 0 us
  waiting for transfers between devices: 36.6 us -> 54.9 us
  local copies, waits for them, and re-layouts: 5.96 us -> 8.08 us
  starting transfers between devices: 21.7 us -> 23.1 us
    all_to_all x1 -> x0, blocking collectives: 21 us -> none  [local(): mixed_field = lax.all_to_all(mixed_rows, 'mode', 0, 0, tiled=True)]
    all_to_all x0 -> x1, waiting for transfers between devices: none -> 18.4 us  [local(): mixed_field = lax.all_to_all(mixed_rows, 'mode', 0, 0, tiled=True)]
    all_to_all x0 -> x1, starting transfers between devices: none -> 3.57 us  [local(): mixed_field = lax.all_to_all(mixed_rows, 'mode', 0, 0, tiled=True)]
    unnamed x22 -> x24, local copies, waits for them, and re-layouts: 3.42 us -> 5.54 us
    all_to_all x1, starting transfers between devices: 8.09 us -> 6 us  [local(): summaries = lax.all_to_all(copies, 'depth', 0, 0, tiled=True)]
    pallas_call x0 -> x1, Pallas kernels: none -> 1.85 us  [decay_weights(): pl.pallas_call(decay_kernel, out_shape=(jax.ShapeDtypeStruct(decay.shape,...]
  transfers between devices with their start and end apart: 4 -> 5, of which waited for: 2 -> 3; matrix products, arithmetic and copies ran while one was open for 2% -> 2% of each run, Pallas kernels for 4% -> 6%
where the time goes in v12:
time: 105 us
  waiting for transfers between devices  54.9 us (52%)
  starting transfers between devices  23.1 us (22%)
  Pallas kernels  10.8 us (10%)
  local copies, waits for them, and re-layouts  8.08 us (8%)
  matrix products  4.9 us (5%)
  other arithmetic  2.52 us (2%)
    all_to_all x1, waiting for transfers between devices, local(): summaries = lax.all_to_all(copies, 'depth', 0, 0, tiled=True)  22.8 us
    all_to_all x1, waiting for transfers between devices, local(): mixed_field = lax.all_to_all(mixed_rows, 'mode', 0, 0, tiled=True)  18.4 us
    all_to_all x1, waiting for transfers between devices, local(): stencil_rows = lax.all_to_all(stencil, 'mode', 1, 0, tiled=True)  13.7 us
    ppermute x1, starting transfers between devices, local(): lax.ppermute(fields[:, -1], 'depth', [(i, i + 1) for i in range(slabs - 1)])  6.88 us
    all_to_all x1, starting transfers between devices, local(): summaries = lax.all_to_all(copies, 'depth', 0, 0, tiled=True)  6 us
    unnamed x24, local copies, waits for them, and re-layouts  5.54 us
    dot_general x1, matrix products, local(): jnp.dot(table_rows, stencil_rows, precision=lax.Precision.HIGH, preferred...  4.9 us
    all_to_all x1, starting transfers between devices, local(): stencil_rows = lax.all_to_all(stencil, 'mode', 1, 0, tiled=True)  4.78 us
  transfers between devices with their start and end apart: 5, of which 3 were waited for; matrix products, arithmetic and copies ran while one was open for 2% of the time, Pallas kernels for 6%

profile of v12, /device:TPU:1, one launch (start us, length us, event | category | flops | bytes accessed | tf_op | source)
XLA Modules:
  0.0 104.6 jit_solution(8866096394224739903)
XLA Ops:
  0.0 0.8 slice_bitcast_fusion.30
  0.8 6.9 %collective-permute-start = (f32[5,16,128]{2,1,0:T(8,128)S(1)}, f32[5,16,128]{2,1,0:T(8,128)S(1)}, u32[]{:S(2)}, u32[]{:S(2)}) collective-permute-start(f32[5,16,128]{2,1,0:T(8,128)S(1)} %get-tuple-element.45), channel_id=1, source_target_pairs={{0,1},{1,2},{2,3},{3,4},{4,5},{5,6},{6,7},{7,8},{8,9},{9,10},{10,1... | collective-permute-start | bytes 122888 | tf_op jit(solution)/shard_map/ppermute | solution.py:183
  7.7 1.9 %collective-permute-start.1 = (f32[5,16,128]{2,1,0:T(8,128)S(1)}, f32[5,16,128]{2,1,0:T(8,128)S(1)}, u32[]{:S(2)}, u32[]{:S(2)}) collective-permute-start(f32[5,16,128]{2,1,0:T(8,128)S(1)} %get-tuple-element.44), channel_id=1, source_target_pairs={{1,0},{2,1},{3,2},{4,3},{5,4},{6,5},{7,6},{8,7},{9,8},{10,9},{11,1... | collective-permute-start | bytes 122888 | tf_op jit(solution)/shard_map/ppermute | solution.py:184
  9.6 0.7 compare_select_fusion
  10.3 4.4 %shard_map.73.stencil_ref = f32[32,5,16,128]{3,2,1,0:T(8,128)} custom-call(f32[5,32,16,128]{3,2,1,0:T(8,128)} %fields_ref.1), custom_call_target="tpu_custom_call" | custom-call | tf_op jit(solution)/shard_map/pallas_call | solution.py:38
  14.7 0.6 copy-done.8
  15.3 0.6 copy-done.9
  15.9 1.5 %shard_map.74 = f32[32,5,16,128]{3,2,1,0:T(8,128)} custom-call(f32[32,5,16,128]{3,2,1,0:T(8,128)} %shard_map.73.stencil_ref, f32[5,16,128]{2,1,0:T(8,128)} %copy-done.8, f32[5,16,128]{2,1,0:T(8,128)} %copy-done.9), custom_call_target="tpu_custom_call", output_to_operand_aliasing={{}: (0, {})} | custom-call | tf_op jit(solution)/shard_map/pallas_call | solution.py:56
  17.4 4.8 %all-to-all-start = ((f32[5,32,16,128]{3,2,0,1:T(8,128)}), f32[5,32,16,128]{3,2,0,1:T(8,128)S(1)}, u32[]{:S(2)}, u32[]{:S(2)}) async-start(f32[5,32,16,128]{3,2,0,1:T(8,128)} %bitcast.329), calls=%async_computation | async-start | bytes 2621440 | tf_op jit(solution)/shard_map/all_to_all | solution.py:187
  22.4 0.7 copy-done.6
  23.2 0.6 gather_fusion
  24.1 0.6 gather_fusion.1
  24.8 13.7 %all-to-all-done = f32[5,32,16,128]{3,2,0,1:T(8,128)S(1)} async-done(((f32[5,32,16,128]{3,2,0,1:T(8,128)}), f32[5,32,16,128]{3,2,0,1:T(8,128)S(1)}, u32[]{:S(2)}, u32[]{:S(2)}) %all-to-all-start) | async-done | bytes 1310752 | tf_op jit(solution)/shard_map/all_to_all | solution.py:187
  39.0 4.9 %fusion = f32[40,8192]{1,0:T(8,128)S(1)} fusion(f32[40,8192,1]{1,0,2:T(8,128)S(1)} %reshape.393, f32[8,8192]{1,0:T(8,128)S(1)} %bitcast.335, f32[8,40,40]{1,0,2:T(8,128)S(1)} %select_bitcast_fusion), kind=kOutput, calls=%fused_computation.3 | convolution fusion | flops 634060800 | bytes 2934784 | tf_op jit(solution)/shard_map/dot_general | solution.py:197
  43.9 1.3 %copy.23 = f32[5,8,64,128]{3,2,1,0:T(8,128)} copy(f32[5,8,64,128]{3,1,2,0:T(8,128)S(1)} %bitcast.332) | data formatting | bytes 2621440
  45.2 3.6 %all-to-all-start.1 = ((f32[40,4,16,128]{3,2,1,0:T(8,128)}), f32[40,4,16,128]{3,2,1,0:T(8,128)S(1)}, u32[]{:S(2)}, u32[]{:S(2)}) async-start(f32[40,4,16,128]{3,2,1,0:T(8,128)} %bitcast.80), calls=%async_computation.1 | async-start | bytes 2621440 | tf_op jit(solution)/shard_map/all_to_all | solution.py:205
  48.7 1.8 %shard_map.75 = (f32[32,16,128]{2,1,0:T(8,128)}, f32[32,16,128]{2,1,0:T(8,128)}) custom-call(f32[32,16,128]{2,1,0:T(8,128)} %decay_ref.3), custom_call_target="tpu_custom_call" | custom-call | tf_op jit(solution)/shard_map/pallas_call | solution.py:102
  50.6 18.4 %all-to-all-done.1 = f32[40,4,16,128]{3,2,1,0:T(8,128)S(1)} async-done(((f32[40,4,16,128]{3,2,1,0:T(8,128)}), f32[40,4,16,128]{3,2,1,0:T(8,128)S(1)}, u32[]{:S(2)}, u32[]{:S(2)}) %all-to-all-start.1) | async-done | bytes 1310752 | tf_op jit(solution)/shard_map/all_to_all | solution.py:205
  69.0 1.1 %copy-done = f32[40,4,16,128]{3,2,1,0:T(8,128)} copy-done((f32[40,4,16,128]{3,2,1,0:T(8,128)}, f32[40,4,16,128]{3,2,1,0:T(8,128)S(1)}, u32[]{:S(2)}) %copy-start) | copy-done | bytes 1310744
  70.0 3.1 %shard_map.76 = (f32[5,32,16,128]{3,2,1,0:T(8,128)}, f32[16,12,16,128]{3,2,1,0:T(8,128)}) custom-call(f32[8,5,4,16,128]{4,3,2,1,0:T(8,128)} %bitcast.331, f32[32,16,128]{2,1,0:T(8,128)} %decay_ref.3, f32[32,16,128]{2,1,0:T(8,128)} %get-tuple-element.9.coupled_ref, f32[32,16,128]{2,1,0:T(8,128)} %get-tuple-element.10.tail_ref), custom_call_target="tpu_custom_call" | custom-call | tf_op jit(solution)/shard_map/pallas_call | solution.py:151
  73.1 6.0 %all-to-all-start.2 = ((f32[16,12,16,128]{3,2,1,0:T(8,128)}), f32[16,12,16,128]{3,2,1,0:T(8,128)S(1)}, u32[]{:S(2)}, u32[]{:S(2)}) async-start(f32[16,12,16,128]{3,2,1,0:T(8,128)} %get-tuple-element.12), calls=%async_computation.2 | async-start | bytes 3145728 | tf_op jit(solution)/shard_map/all_to_all | solution.py:210
  79.1 22.8 %all-to-all-done.2 = f32[16,12,16,128]{3,2,1,0:T(8,128)S(1)} async-done(((f32[16,12,16,128]{3,2,1,0:T(8,128)}), f32[16,12,16,128]{3,2,1,0:T(8,128)S(1)}, u32[]{:S(2)}, u32[]{:S(2)}) %all-to-all-start.2) | async-done | bytes 1572896 | tf_op jit(solution)/shard_map/all_to_all | solution.py:210
  102.3 0.9 copy-done.2
  103.4 1.2 %multiply_add_fusion = f32[5,32,16,128]{3,2,1,0:T(8,128)} fusion(f32[5,32,16,128]{3,2,1,0:T(8,128)S(1)} %copy-done.2, f32[5,16,128]{2,1,0:T(8,128)S(1)} %fusion.33, f32[32,16,128]{2,1,0:T(8,128)S(1)} %copy-done.4, f32[5,16,128]{2,1,0:T(8,128)S(1)} %select_select_fusion, f32[32,16,128]{2,1,0:T(8,128)S(1)} %copy-done.3), kind=kLoop, calls=%fused_computation.6 | loop fusion | flops 1310720 | bytes 3227648 | tf_op jit(solution)/shard_map/add | solution.py:232
  (33 shorter events, 1.5 us)
Async XLA Ops:
  0.8 13.9 %collective-permute-start = (f32[5,16,128]{2,1,0:T(8,128)S(1)}, f32[5,16,128]{2,1,0:T(8,128)S(1)}, u32[]{:S(2)}, u32[]{:S(2)}) collective-permute-start(f32[5,16,128]{2,1,0:T(8,128)S(1)} %get-tuple-element.45), channel_id=1, source_target_pairs={{0,1},{1,2},{2,3},{3,4},{4,5},{5,6},{6,7},{7,8},{8,9},{9,10},{10,1... | collective-permute-start | bytes 122888 | tf_op jit(solution)/shard_map/ppermute | solution.py:183
  7.7 7.0 %collective-permute-start.1 = (f32[5,16,128]{2,1,0:T(8,128)S(1)}, f32[5,16,128]{2,1,0:T(8,128)S(1)}, u32[]{:S(2)}, u32[]{:S(2)}) collective-permute-start(f32[5,16,128]{2,1,0:T(8,128)S(1)} %get-tuple-element.44), channel_id=1, source_target_pairs={{1,0},{2,1},{3,2},{4,3},{5,4},{6,5},{7,6},{8,7},{9,8},{10,9},{11,1... | collective-permute-start | bytes 122888 | tf_op jit(solution)/shard_map/ppermute | solution.py:184
  14.7 0.6 copy-start.8
  15.3 0.6 copy-start.9
  17.4 4.8 %copy-start.1 = (f32[7,32,16,128]{3,2,1,0:T(8,128)S(1)}, f32[7,32,16,128]{3,2,1,0:T(8,128)}, u32[]{:S(2)}) copy-start(f32[7,32,16,128]{3,2,1,0:T(8,128)} %param.9) | copy-start | bytes 5505028
  17.4 4.8 %copy-start.5 = (f32[32,16,128]{2,1,0:T(8,128)S(1)}, f32[32,16,128]{2,1,0:T(8,128)}, u32[]{:S(2)}) copy-start(f32[32,16,128]{2,1,0:T(8,128)} %param.8) | copy-start | bytes 786436
  17.4 21.1 %all-to-all-start = ((f32[5,32,16,128]{3,2,0,1:T(8,128)}), f32[5,32,16,128]{3,2,0,1:T(8,128)S(1)}, u32[]{:S(2)}, u32[]{:S(2)}) async-start(f32[5,32,16,128]{3,2,0,1:T(8,128)} %bitcast.329), calls=%async_computation | async-start | bytes 2621440 | tf_op jit(solution)/shard_map/all_to_all | solution.py:187
  22.2 0.9 copy-start.6
  22.2 1.0 copy-start.7
  22.3 1.6 %copy-start.10 = (s32[40]{0:T(128)S(1)}, s32[40]{0:T(128)}, u32[]{:S(2)}) copy-start(s32[40]{0:T(128)} %param.13) | copy-start | bytes 484
  45.2 23.8 %all-to-all-start.1 = ((f32[40,4,16,128]{3,2,1,0:T(8,128)}), f32[40,4,16,128]{3,2,1,0:T(8,128)S(1)}, u32[]{:S(2)}, u32[]{:S(2)}) async-start(f32[40,4,16,128]{3,2,1,0:T(8,128)} %bitcast.80), calls=%async_computation.1 | async-start | bytes 2621440 | tf_op jit(solution)/shard_map/all_to_all | solution.py:205
  69.0 1.1 %copy-start = (f32[40,4,16,128]{3,2,1,0:T(8,128)}, f32[40,4,16,128]{3,2,1,0:T(8,128)S(1)}, u32[]{:S(2)}) copy-start(f32[40,4,16,128]{3,2,1,0:T(8,128)S(1)} %all-to-all-done.1) | copy-start | bytes 3932164
  73.1 28.8 %all-to-all-start.2 = ((f32[16,12,16,128]{3,2,1,0:T(8,128)}), f32[16,12,16,128]{3,2,1,0:T(8,128)S(1)}, u32[]{:S(2)}, u32[]{:S(2)}) async-start(f32[16,12,16,128]{3,2,1,0:T(8,128)} %get-tuple-element.12), calls=%async_computation.2 | async-start | bytes 3145728 | tf_op jit(solution)/shard_map/all_to_all | solution.py:210
  101.9 1.3 %copy-start.2 = (f32[5,32,16,128]{3,2,1,0:T(8,128)S(1)}, f32[5,32,16,128]{3,2,1,0:T(8,128)}, u32[]{:S(2)}) copy-start(f32[5,32,16,128]{3,2,1,0:T(8,128)} %get-tuple-element.11) | copy-start | bytes 3932164
  101.9 1.3 %copy-start.3 = (f32[32,16,128]{2,1,0:T(8,128)S(1)}, f32[32,16,128]{2,1,0:T(8,128)}, u32[]{:S(2)}) copy-start(f32[32,16,128]{2,1,0:T(8,128)} %get-tuple-element.9.coupled_ref) | copy-start | bytes 786436
  102.0 1.4 %copy-start.4 = (f32[32,16,128]{2,1,0:T(8,128)S(1)}, f32[32,16,128]{2,1,0:T(8,128)}, u32[]{:S(2)}) copy-start(f32[32,16,128]{2,1,0:T(8,128)} %get-tuple-element.10.tail_ref) | copy-start | bytes 786436

commit v13 on v10

--- a/solution.py
+++ b/solution.py
@@ -125,7 +125,7 @@
     groups, modes, chunk = mixed.shape[0], mixed.shape[1], mixed.shape[2]
     rows = decay.shape[0]
     lateral = decay.shape[1:]
-    parts = 2
+    parts = 1
     half = (lateral[0] // parts, lateral[1])
     return pl.pallas_call(
         sweep_kernel,

time: 102 us -> 103 us (level)
  no operation moved by 1% of the time
where the time goes in v13:
time: 103 us; the launch traced here: 102 us
  waiting for transfers between devices  36.6 us (36%)
  starting transfers between devices  21.7 us (21%)
  blocking collectives  21 us (20%)
  Pallas kernels  9.39 us (9%)
  local copies, waits for them, and re-layouts  5.96 us (6%)
  matrix products  4.91 us (5%)
  other arithmetic  2.52 us (2%)
    all_to_all x1, waiting for transfers between devices, local(): summaries = lax.all_to_all(copies, 'depth', 0, 0, tiled=True)  22.8 us
    all_to_all x1, blocking collectives, local(): mixed_field = lax.all_to_all(mixed_rows, 'mode', 0, 0, tiled=True)  21 us
    all_to_all x1, waiting for transfers between devices, local(): stencil_rows = lax.all_to_all(stencil, 'mode', 1, 0, tiled=True)  13.7 us
    all_to_all x1, starting transfers between devices, local(): summaries = lax.all_to_all(copies, 'depth', 0, 0, tiled=True)  8.09 us
    ppermute x1, starting transfers between devices, local(): lax.ppermute(fields[:, -1], 'depth', [(i, i + 1) for i in range(slabs - 1)])  6.88 us
    dot_general x1, matrix products, local(): jnp.dot(table_rows, stencil_rows, precision=lax.Precision.HIGH, preferred...  4.91 us
    all_to_all x1, starting transfers between devices, local(): stencil_rows = lax.all_to_all(stencil, 'mode', 1, 0, tiled=True)  4.78 us
    pallas_call x1, Pallas kernels, slab_stencil(): pl.pallas_call(stencil_kernel, grid=(modes,), in_specs=[pl.BlockSpec((1,...  4.41 us
  transfers between devices with their start and end apart: 4, of which 2 were waited for; matrix products, arithmetic and copies ran while one was open for 2% of the time, Pallas kernels for 4%

profile of v13, /device:TPU:1, one launch (start us, length us, event | category | flops | bytes accessed | tf_op | source)
XLA Modules:
  0.0 102.3 jit_solution(14864174451962707989)
XLA Ops:
  0.0 0.8 slice_bitcast_fusion.30
  0.8 6.9 %collective-permute-start = (f32[5,16,128]{2,1,0:T(8,128)S(1)}, f32[5,16,128]{2,1,0:T(8,128)S(1)}, u32[]{:S(2)}, u32[]{:S(2)}) collective-permute-start(f32[5,16,128]{2,1,0:T(8,128)S(1)} %get-tuple-element.45), channel_id=1, source_target_pairs={{0,1},{1,2},{2,3},{3,4},{4,5},{5,6},{6,7},{7,8},{8,9},{9,10},{10,1... | collective-permute-start | bytes 122888 | tf_op jit(solution)/shard_map/ppermute | solution.py:164
  7.7 1.9 %collective-permute-start.1 = (f32[5,16,128]{2,1,0:T(8,128)S(1)}, f32[5,16,128]{2,1,0:T(8,128)S(1)}, u32[]{:S(2)}, u32[]{:S(2)}) collective-permute-start(f32[5,16,128]{2,1,0:T(8,128)S(1)} %get-tuple-element.44), channel_id=1, source_target_pairs={{1,0},{2,1},{3,2},{4,3},{5,4},{6,5},{7,6},{8,7},{9,8},{10,9},{11,1... | collective-permute-start | bytes 122888 | tf_op jit(solution)/shard_map/ppermute | solution.py:165
  9.6 0.7 compare_select_fusion
  10.3 4.4 %shard_map.73.stencil_ref = f32[32,5,16,128]{3,2,1,0:T(8,128)} custom-call(f32[5,32,16,128]{3,2,1,0:T(8,128)} %fields_ref.1), custom_call_target="tpu_custom_call" | custom-call | tf_op jit(solution)/shard_map/pallas_call | solution.py:38
  14.7 0.6 copy-done.7
  15.3 0.6 copy-done.8
  15.9 1.5 %shard_map.74 = f32[32,5,16,128]{3,2,1,0:T(8,128)} custom-call(f32[32,5,16,128]{3,2,1,0:T(8,128)} %shard_map.73.stencil_ref, f32[5,16,128]{2,1,0:T(8,128)} %copy-done.7, f32[5,16,128]{2,1,0:T(8,128)} %copy-done.8), custom_call_target="tpu_custom_call", output_to_operand_aliasing={{}: (0, {})} | custom-call | tf_op jit(solution)/shard_map/pallas_call | solution.py:56
  17.4 4.8 %all-to-all-start = ((f32[5,32,16,128]{3,2,0,1:T(8,128)}), f32[5,32,16,128]{3,2,0,1:T(8,128)S(1)}, u32[]{:S(2)}, u32[]{:S(2)}) async-start(f32[5,32,16,128]{3,2,0,1:T(8,128)} %bitcast.329), calls=%async_computation | async-start | bytes 2621440 | tf_op jit(solution)/shard_map/all_to_all | solution.py:168
  22.3 0.2 copy.27
  22.4 0.7 copy-done.5
  23.2 0.6 gather_fusion
  24.1 0.6 gather_fusion.1
  24.8 13.7 %all-to-all-done = f32[5,32,16,128]{3,2,0,1:T(8,128)S(1)} async-done(((f32[5,32,16,128]{3,2,0,1:T(8,128)}), f32[5,32,16,128]{3,2,0,1:T(8,128)S(1)}, u32[]{:S(2)}, u32[]{:S(2)}) %all-to-all-start) | async-done | bytes 1310752 | tf_op jit(solution)/shard_map/all_to_all | solution.py:168
  38.7 0.2 reshape.393
  39.0 4.9 %fusion = f32[40,8192]{1,0:T(8,128)S(1)} fusion(f32[40,8192,1]{1,0,2:T(8,128)S(1)} %reshape.393, f32[8,8192]{1,0:T(8,128)S(1)} %bitcast.336, f32[8,40,40]{1,0,2:T(8,128)S(1)} %select_bitcast_fusion), kind=kOutput, calls=%fused_computation.3 | convolution fusion | flops 634060800 | bytes 2934784 | tf_op jit(solution)/shard_map/dot_general | solution.py:178
  43.9 0.2 copy.23
  44.1 21.0 %all_to_all.25 = f32[40,4,16,128]{3,2,1,0:T(8,128)} all-to-all(f32[40,4,16,128]{3,2,1,0:T(8,128)S(1)} %bitcast.332), channel_id=1, replica_groups=mesh['mode'=8,'depth'=16] {'mode'}, dimensions={0} | all-to-all | bytes 2621440 | tf_op jit(solution)/shard_map/all_to_all | solution.py:186
  65.1 3.5 %shard_map.75 = (f32[5,32,16,128]{3,2,1,0:T(8,128)}, f32[32,16,128]{2,1,0:T(8,128)}, f32[32,16,128]{2,1,0:T(8,128)}, f32[16,12,16,128]{3,2,1,0:T(8,128)}) custom-call(f32[8,5,4,16,128]{4,3,2,1,0:T(8,128)} %bitcast.331, f32[32,16,128]{2,1,0:T(8,128)} %decay_ref.1), custom_call_target="tpu_custom_call" | custom-call | tf_op jit(solution)/shard_map/pallas_call | solution.py:130
  68.7 8.1 %all-to-all-start.2 = ((f32[16,12,16,128]{3,2,1,0:T(8,128)}), f32[16,12,16,128]{3,2,1,0:T(8,128)S(1)}, u32[]{:S(2)}, u32[]{:S(2)}) async-start(f32[16,12,16,128]{3,2,1,0:T(8,128)} %get-tuple-element.11), calls=%async_computation.2 | async-start | bytes 3145728 | tf_op jit(solution)/shard_map/all_to_all | solution.py:190
  76.7 22.8 %all-to-all-done.2 = f32[16,12,16,128]{3,2,1,0:T(8,128)S(1)} async-done(((f32[16,12,16,128]{3,2,1,0:T(8,128)}), f32[16,12,16,128]{3,2,1,0:T(8,128)S(1)}, u32[]{:S(2)}, u32[]{:S(2)}) %all-to-all-start.2) | async-done | bytes 1572896 | tf_op jit(solution)/shard_map/all_to_all | solution.py:190
  99.8 0.2 fusion.33
  100.0 0.9 copy-done.1
  101.0 1.2 %multiply_add_fusion = f32[5,32,16,128]{3,2,1,0:T(8,128)} fusion(f32[5,32,16,128]{3,2,1,0:T(8,128)S(1)} %copy-done.1, f32[5,16,128]{2,1,0:T(8,128)S(1)} %fusion.33, f32[32,16,128]{2,1,0:T(8,128)S(1)} %copy-done.4, f32[5,16,128]{2,1,0:T(8,128)S(1)} %select_select_fusion, f32[32,16,128]{2,1,0:T(8,128)S(1)} %copy-done.3), kind=kLoop, calls=%fused_computation.6 | loop fusion | flops 1310720 | bytes 3227648 | tf_op jit(solution)/shard_map/add | solution.py:212
  (29 shorter events, 0.9 us)
Async XLA Ops:
  0.8 13.9 %collective-permute-start = (f32[5,16,128]{2,1,0:T(8,128)S(1)}, f32[5,16,128]{2,1,0:T(8,128)S(1)}, u32[]{:S(2)}, u32[]{:S(2)}) collective-permute-start(f32[5,16,128]{2,1,0:T(8,128)S(1)} %get-tuple-element.45), channel_id=1, source_target_pairs={{0,1},{1,2},{2,3},{3,4},{4,5},{5,6},{6,7},{7,8},{8,9},{9,10},{10,1... | collective-permute-start | bytes 122888 | tf_op jit(solution)/shard_map/ppermute | solution.py:164
  7.7 7.0 %collective-permute-start.1 = (f32[5,16,128]{2,1,0:T(8,128)S(1)}, f32[5,16,128]{2,1,0:T(8,128)S(1)}, u32[]{:S(2)}, u32[]{:S(2)}) collective-permute-start(f32[5,16,128]{2,1,0:T(8,128)S(1)} %get-tuple-element.44), channel_id=1, source_target_pairs={{1,0},{2,1},{3,2},{4,3},{5,4},{6,5},{7,6},{8,7},{9,8},{10,9},{11,1... | collective-permute-start | bytes 122888 | tf_op jit(solution)/shard_map/ppermute | solution.py:165
  14.7 0.6 copy-start.7
  15.3 0.6 copy-start.8
  17.4 4.8 %copy-start = (f32[7,32,16,128]{3,2,1,0:T(8,128)S(1)}, f32[7,32,16,128]{3,2,1,0:T(8,128)}, u32[]{:S(2)}) copy-start(f32[7,32,16,128]{3,2,1,0:T(8,128)} %param.9) | copy-start | bytes 5505028
  17.4 4.8 %copy-start.2 = (f32[32,16,128]{2,1,0:T(8,128)S(1)}, f32[32,16,128]{2,1,0:T(8,128)}, u32[]{:S(2)}) copy-start(f32[32,16,128]{2,1,0:T(8,128)} %param.8) | copy-start | bytes 786436
  17.4 21.1 %all-to-all-start = ((f32[5,32,16,128]{3,2,0,1:T(8,128)}), f32[5,32,16,128]{3,2,0,1:T(8,128)S(1)}, u32[]{:S(2)}, u32[]{:S(2)}) async-start(f32[5,32,16,128]{3,2,0,1:T(8,128)} %bitcast.329), calls=%async_computation | async-start | bytes 2621440 | tf_op jit(solution)/shard_map/all_to_all | solution.py:168
  22.2 0.9 copy-start.5
  22.2 1.0 copy-start.6
  22.2 1.6 %copy-start.9 = (s32[40]{0:T(128)S(1)}, s32[40]{0:T(128)}, u32[]{:S(2)}) copy-start(s32[40]{0:T(128)} %param.13) | copy-start | bytes 484
  68.7 30.9 %all-to-all-start.2 = ((f32[16,12,16,128]{3,2,1,0:T(8,128)}), f32[16,12,16,128]{3,2,1,0:T(8,128)S(1)}, u32[]{:S(2)}, u32[]{:S(2)}) async-start(f32[16,12,16,128]{3,2,1,0:T(8,128)} %get-tuple-element.11), calls=%async_computation.2 | async-start | bytes 3145728 | tf_op jit(solution)/shard_map/all_to_all | solution.py:190
  99.6 1.3 %copy-start.1 = (f32[5,32,16,128]{3,2,1,0:T(8,128)S(1)}, f32[5,32,16,128]{3,2,1,0:T(8,128)}, u32[]{:S(2)}) copy-start(f32[5,32,16,128]{3,2,1,0:T(8,128)} %get-tuple-element.9) | copy-start | bytes 3932164
  99.6 1.3 %copy-start.3 = (f32[32,16,128]{2,1,0:T(8,128)S(1)}, f32[32,16,128]{2,1,0:T(8,128)}, u32[]{:S(2)}) copy-start(f32[32,16,128]{2,1,0:T(8,128)} %get-tuple-element.10) | copy-start | bytes 786436
  99.6 1.4 %copy-start.4 = (f32[32,16,128]{2,1,0:T(8,128)S(1)}, f32[32,16,128]{2,1,0:T(8,128)}, u32[]{:S(2)}) copy-start(f32[32,16,128]{2,1,0:T(8,128)} %get-tuple-element.12) | copy-start | bytes 786436
